TPU v7x, 32 devices: a whole 2x2x4 slice. The times are simulated.
32 devices in a mesh: grp: 4 (over y, x), box: 8 (over z, core).
Axes of the slice: x: 2, y: 2, z: 4, core: 2. Of those that a mesh axis runs over, the one named last changes fastest.
Arguments:
- leaf_maps: float32 [4, 8, 1024, 1024], P('grp', 'box'), may hold values from -4 to 30
- side_points: int32 [4, 8, 4, 256], P('grp', 'box'), may hold values from 0 to 1023, as said below
Outputs:
- merged_rows: float32 [4, 8, 512, 2048], P('grp', 'box')
Inputs may be any that keep to these rules, and one draw needn't show every extreme that they name: `side_points`: for each leaf box, its four lists of 256 indices together name each of the 1024 rows of its map exactly once.
All inputs are finite; a program needn't handle non-finite values.
Results may differ from a plain program's by a relative error of at most 0.0001.
Values sent between devices are 32-bit elements; how exact they have to be, the bound alone decides.
No kernel may reach another device: no remote copies, remote signals or barrier semaphores. Data moves between devices by JAX's collectives and lax.ppermute only.
A program may use at most 64 MiB of HBM per device.

v0:
```python
import jax
import jax.numpy as jnp
from jax import lax
from jax.sharding import PartitionSpec as P

ITERS_LOW = 3
ITERS_HIGH = 3


def matmul(left, right):
    return jnp.dot(left, right, precision=lax.Precision.HIGHEST, preferred_element_type=jnp.float32)


def matmul_high(left, right):
    return jnp.dot(left, right, precision=lax.Precision.HIGH, preferred_element_type=jnp.float32)


def newton(system, steps, product=matmul):
    size = system.shape[0]
    eye = jnp.eye(size, dtype=jnp.float32)
    recip = 1.0 / jnp.sum(jnp.where(eye > 0, system, 0.0), axis=1)
    inverse = 2.0 * eye * recip[None, :] - recip[:, None] * system * recip[None, :]
    for sweep_index in range(steps - 1):
        inverse = 2.0 * inverse - product(product(inverse, system), inverse)
    return inverse


def swap(value, axis):
    size = lax.axis_size(axis)
    half = size // 2
    pairs = [(source, (source + half) % size) for source in range(size)]
    return lax.ppermute(value, axis, pairs)


def pair_solve(first_i1, second_i1, width):
    system = first_i1[:, :width] + second_i1[:, :width]
    inverse = newton(system, ITERS_LOW)
    coupling = jnp.concatenate([first_i1[:, width:], second_i1[:, width:]], 1)
    return -matmul(inverse, coupling)


def first_rows(rows, solved, width):
    blank = jnp.zeros((rows.shape[0], 3 * width), jnp.float32)
    return jnp.concatenate([rows[:, width:], blank], 1) + matmul(rows[:, :width], solved)


def second_rows(rows, solved, width):
    blank = jnp.zeros((rows.shape[0], 3 * width), jnp.float32)
    return jnp.concatenate([blank, rows[:, width:]], 1) + matmul(rows[:, :width], solved)


def ext_cols(parent, width):
    return jnp.concatenate(
        [parent[:, 0 : 2 * width], parent[:, 3 * width : 5 * width]], 1
    )


def int_cols(parent, width):
    return jnp.concatenate(
        [parent[:, 2 * width : 3 * width], parent[:, 5 * width : 6 * width]], 1
    )


def pick(matrix, rows, cols):
    picked = jnp.take(matrix, rows, axis=0, mode="clip")
    return jnp.take(picked, cols, axis=1, mode="clip")


def body(leaf_maps, side_points):
    upper = lax.axis_index("grp") // (lax.axis_size("grp") // 2)
    right = lax.axis_index("box") // (lax.axis_size("box") // 2)
    leaf = leaf_maps[0, 0]
    side_lists = side_points[0, 0]
    width = side_lists.shape[1]
    order = jnp.stack([1 - right, right, 2 + upper, 3 - upper])
    perm = jnp.take(side_lists, order, axis=0, mode="clip").reshape(4 * width)
    own_i1 = pick(leaf, perm[:width], perm)
    leaf, own_i1 = lax.optimization_barrier((leaf, own_i1))
    own_i2 = pick(leaf, perm[3 * width :], perm)
    own_ov = pick(leaf, perm[width : 3 * width], perm)

    half = width // 2
    vert_i1 = swap(own_i1, "grp")
    vert_i2 = swap(own_i2, "grp")
    side_i1 = swap(own_i1, "box")
    diag_i1 = swap(side_i1, "grp")
    first_half, side_i1 = lax.optimization_barrier((own_i2[:half], side_i1))
    side_first = swap(first_half, "box")
    diag_first = swap(side_first, "grp")
    second_half, side_first = lax.optimization_barrier((own_i2[half:], side_first))
    side_second = swap(second_half, "box")
    diag_second = swap(side_second, "grp")
    side_i2 = jnp.concatenate([side_first, side_second], 0)
    diag_i2 = jnp.concatenate([diag_first, diag_second], 0)

    solved_own = pair_solve(own_i1, side_i1, width)
    own_ext = first_rows(own_ov, solved_own, width)
    own_int = first_rows(own_i2, solved_own, width)
    side_int = second_rows(side_i2, solved_own, width)

    solved_other = pair_solve(vert_i1, diag_i1, width)
    vert_int = first_rows(vert_i2, solved_other, width)
    diag_int = second_rows(diag_i2, solved_other, width)

    near = jnp.concatenate([own_int, side_int], 0)
    far = jnp.concatenate([vert_int, diag_int], 0)
    system_two = int_cols(near, width) + int_cols(far, width)
    inverse_two = newton(system_two, ITERS_HIGH, matmul_high)
    weights = matmul_high(int_cols(own_ext, width), inverse_two)
    own_id = 2 * upper + right
    pieces = [
        own_ext[:, 0 : 2 * width] - matmul_high(weights, near[:, 0 : 2 * width]),
        own_ext[:, 3 * width : 5 * width] - matmul_high(weights, near[:, 3 * width : 5 * width]),
        -matmul_high(weights, far[:, 0 : 2 * width]),
        -matmul_high(weights, far[:, 3 * width : 5 * width]),
    ]
    merged = jnp.zeros((2 * width, 8 * width), jnp.float32)
    for rel, piece in enumerate(pieces):
        start = jnp.bitwise_xor(own_id, rel) * (2 * width)
        merged = lax.dynamic_update_slice(merged, piece, (0, start))
    return merged[None, None]


def solution(mesh):
    in_specs = (P("grp", "box", None, None), P("grp", "box", None, None))
    out_specs = P("grp", "box", None, None)
    return jax.shard_map(body, mesh=mesh, in_specs=in_specs, out_specs=out_specs, check_vma=False)
```

profile of v0, /device:TPU:0, one launch (start us, length us, event | category | flops | bytes accessed | tf_op | source)
XLA Modules:
  0.0 145.0 jit_solution(18339457404805371138)
XLA Ops:
  0.0 0.1 pad_add_fusion.3
  0.1 0.6 copy-done
  0.7 0.6 gather_fusion
  1.3 3.8 %gather_fusion.1 = f32[256,1024]{1,0:T(8,128)S(1)} fusion(f32[1024,1024]{1,0:T(8,128)} %bitcast.63, s32[1024]{0:T(1024)S(1)} %get-tuple-element.31), kind=kCustom, calls=%fused_computation.1 | custom fusion | bytes 2098176 | tf_op jit(solution)/shard_map/jit(_take)/gather | solution.py:65
  5.1 0.3 copy.3
  5.4 3.5 %gather_fusion.2 = f32[1024,256]{1,0:T(8,128)S(1)} fusion(f32[256,1024]{0,1:T(8,128)S(1)} %copy.3, s32[1024]{0:T(1024)S(1)} %get-tuple-element.32), kind=kCustom, calls=%fused_computation.2 | custom fusion | bytes 2101248 | tf_op jit(solution)/shard_map/jit(_take)/gather | solution.py:66
  8.9 1.3 copy.4
  10.2 4.0 %collective-permute-start = (f32[256,1024]{1,0:T(8,128)}, f32[256,1024]{1,0:T(8,128)}, u32[]{:S(2)}, u32[]{:S(2)}) collective-permute-start(f32[256,1024]{1,0:T(8,128)} %bitcast.7), channel_id=1, source_target_pairs={{0,4},{1,5},{2,6},{3,7},{4,0},{5,1},{6,2},{7,3},{8,12},{9,13},{10,... | collective-permute-start | bytes 3145736 | tf_op jit(solution)/shard_map/ppermute | solution.py:32
  14.2 1.5 %collective-permute-start.4 = (f32[256,1024]{1,0:T(8,128)}, f32[256,1024]{1,0:T(8,128)}, u32[]{:S(2)}, u32[]{:S(2)}) collective-permute-start(f32[256,1024]{1,0:T(8,128)} %bitcast.7), channel_id=1, source_target_pairs={{0,16},{8,24},{16,0},{24,8},{1,17},{9,25},{17,1},{25,9},{2,18},{10... | collective-permute-start | bytes 3145736 | tf_op jit(solution)/shard_map/ppermute | solution.py:32
  15.8 3.8 %gather_fusion.5 = f32[256,1024]{1,0:T(8,128)S(1)} fusion(f32[1024,1024]{1,0:T(8,128)} %bitcast.64, s32[1024]{0:T(1024)S(1)} %get-tuple-element.29), kind=kCustom, calls=%fused_computation.5 | custom fusion | bytes 2098176 | tf_op jit(solution)/shard_map/jit(_take)/gather | solution.py:65
  19.5 0.3 copy.7
  19.9 3.5 %gather_fusion.6 = f32[1024,256]{1,0:T(8,128)S(1)} fusion(f32[256,1024]{0,1:T(8,128)S(1)} %copy.7, s32[1024]{0:T(1024)S(1)} %get-tuple-element.32), kind=kCustom, calls=%fused_computation.6 | custom fusion | bytes 2101248 | tf_op jit(solution)/shard_map/jit(_take)/gather | solution.py:66
  23.4 0.3 copy.8
  23.7 0.6 collective-permute-start.3
  24.3 2.1 %slice.116 = f32[256,768]{1,0:T(8,128)} slice(f32[256,1024]{1,0:T(8,128)} %bitcast.7), slice={[0:256], [256:1024]} | slice | bytes 1572864 | tf_op jit(solution)/shard_map/slice | solution.py:38
  26.4 1.0 slice.166
  27.3 5.8 %gather_fusion.3 = f32[512,1024]{1,0:T(8,128)} fusion(f32[1024,1024]{1,0:T(8,128)} %bitcast.65, s32[1024]{0:T(1024)S(1)} %get-tuple-element.30), kind=kCustom, calls=%fused_computation.3 | custom fusion | bytes 4196352 | tf_op jit(solution)/shard_map/jit(_take)/gather | solution.py:65
  33.1 1.9 %copy.5 = f32[512,1024]{0,1:T(8,128)S(1)} copy(f32[512,1024]{1,0:T(8,128)} %gather_fusion.3) | data formatting | bytes 4194304 | tf_op jit(solution)/shard_map/jit(_take)/gather | solution.py:65
  35.0 4.9 %gather_fusion.4 = f32[1024,512]{1,0:T(8,128)} fusion(f32[512,1024]{0,1:T(8,128)S(1)} %copy.5, s32[1024]{0:T(1024)S(1)} %get-tuple-element.32), kind=kCustom, calls=%fused_computation.4 | custom fusion | bytes 4198400 | tf_op jit(solution)/shard_map/jit(_take)/gather | solution.py:66
  39.9 2.1 %copy.6 = f32[1024,512]{0,1:T(8,128)S(1)} copy(f32[1024,512]{1,0:T(8,128)} %gather_fusion.4) | data formatting | bytes 4194304 | tf_op jit(solution)/shard_map/jit(_take)/gather | solution.py:66
  42.0 1.3 slice.159
  43.3 0.1 fusion.97
  43.3 16.8 %collective-permute-done = f32[256,1024]{1,0:T(8,128)} collective-permute-done((f32[256,1024]{1,0:T(8,128)}, f32[256,1024]{1,0:T(8,128)}, u32[]{:S(2)}, u32[]{:S(2)}) %collective-permute-start) | collective-permute-done | bytes 1048608 | tf_op jit(solution)/shard_map/ppermute | solution.py:32
  60.2 1.1 select_reduce_fusion.2
  61.3 1.2 slice.117
  62.5 0.4 fusion.57
  63.0 0.5 convolution_subtract_fusion.7
  63.5 0.4 fusion.99
  63.8 0.1 collective-permute-start.1
  63.9 1.6 %collective-permute-start.5 = (f32[256,1024]{1,0:T(8,128)}, f32[256,1024]{1,0:T(8,128)S(1)}, u32[]{:S(2)}, u32[]{:S(2)}) collective-permute-start(f32[256,1024]{1,0:T(8,128)} %collective-permute-done), channel_id=1, source_target_pairs={{0,16},{8,24},{16,0},{24,8},{1,17},{9,25},{17,1},{25,9},{2,18},{10... | collective-permute-start | bytes 3145736 | tf_op jit(solution)/shard_map/ppermute | solution.py:32
  65.6 0.4 convolution_subtract_fusion.6
  66.0 1.4 convolution_negate_fusion.1
  67.4 2.9 %convolution_add_fusion = f32[512,1536]{1,0:T(8,128)S(1)} fusion(f32[256,1536]{1,0:T(8,128)S(1)} %convolution_negate_fusion.1, f32[512,768]{1,0:T(8,128)S(1)} %copy-done.1, f32[512,1024]{1,0:T(8,128)S(1)} %bitcast.71), kind=kOutput, calls=%fused_computation.7 | convolution fusion | flops 2416705536 | bytes 6815744 | tf_op jit(solution)/shard_map/dot_general | solution.py:11
  70.3 18.9 %collective-permute-done.1 = f32[128,1024]{1,0:T(8,128)S(1)} collective-permute-done((f32[128,1024]{1,0:T(8,128)S(1)}, f32[128,1024]{1,0:T(8,128)S(1)}, u32[]{:S(2)}, u32[]{:S(2)}) %collective-permute-start.1) | collective-permute-done | bytes 524320 | tf_op jit(solution)/shard_map/ppermute | solution.py:32
  89.2 0.1 fusion.96
  89.3 1.3 slice.175
  90.5 1.2 slice.171
  91.7 1.5 %convolution_add_fusion.1 = f32[256,1536]{1,0:T(8,128)S(1)} fusion(f32[256,1536]{1,0:T(8,128)S(1)} %convolution_negate_fusion.1, f32[256,768]{1,0:T(8,128)S(1)} %copy-done.3, f32[256,1024]{1,0:T(8,128)S(1)} %bitcast.69), kind=kOutput, calls=%fused_computation.8 | convolution fusion | flops 1208352768 | bytes 4194304 | tf_op jit(solution)/shard_map/dot_general | solution.py:11
  93.2 1.3 collective-permute-start.6
  94.6 18.9 %collective-permute-done.2 = f32[128,1024]{1,0:T(8,128)S(1)} collective-permute-done((f32[128,1024]{1,0:T(8,128)S(1)}, f32[128,1024]{1,0:T(8,128)S(1)}, u32[]{:S(2)}, u32[]{:S(2)}) %collective-permute-start.2) | collective-permute-done | bytes 524320 | tf_op jit(solution)/shard_map/ppermute | solution.py:32
  113.6 1.3 select_reduce_fusion.1
  114.9 0.4 fusion.54
  115.3 0.5 convolution_subtract_fusion.5
  115.8 0.4 fusion.100
  116.2 1.1 collective-permute-start.7
  117.2 0.4 convolution_subtract_fusion.4
  117.6 1.5 %pad_add_fusion.2 = f32[256,1536]{1,0:T(8,128)S(1)} fusion(f32[256,768]{1,0:T(8,128)S(1)} %slice.169, f32[256,1536]{1,0:T(8,128)S(1)} %convolution_negate_fusion.1, f32[256,1024]{1,0:T(8,128)S(1)} %constant_dynamic-update-slice_fusion), kind=kOutput, calls=%fused_computation.19 | convolution fusion | flops 1208352768 | bytes 4194304 | tf_op jit(solution)/shard_map/dot_general | solution.py:11
  119.2 1.1 slice-done
  120.2 1.7 %convolution_negate_fusion = f32[256,1536]{1,0:T(8,128)S(1)} fusion(f32[256,256]{1,0:T(8,128)S(1)} %convolution_subtract_fusion.4, f32[256,768]{1,0:T(8,128)S(1)} %slice-done, f32[256,768]{1,0:T(8,128)S(1)} %slice.175), kind=kOutput, calls=%fused_computation.9 | convolution fusion | flops 1208745984 | bytes 3407872 | tf_op jit(solution)/shard_map/dot_general | solution.py:11
  121.9 2.4 %pad_add_fusion.1 = f32[256,1536]{1,0:T(8,128)S(1)} fusion(f32[256,768]{1,0:T(8,128)S(1)} %slice.171, f32[256,1536]{1,0:T(8,128)S(1)} %convolution_negate_fusion, f32[256,1024]{1,0:T(8,128)} %collective-permute-done.3), kind=kOutput, calls=%fused_computation.18 | convolution fusion | flops 1208352768 | bytes 4194304 | tf_op jit(solution)/shard_map/dot_general | solution.py:11
  124.3 5.5 %collective-permute-done.7 = f32[128,1024]{1,0:T(8,128)S(1)} collective-permute-done((f32[128,1024]{1,0:T(8,128)S(1)}, f32[128,1024]{1,0:T(8,128)S(1)}, u32[]{:S(2)}, u32[]{:S(2)}) %collective-permute-start.7) | collective-permute-done | bytes 524320 | tf_op jit(solution)/shard_map/ppermute | solution.py:32
  130.0 1.5 %pad_add_fusion = f32[256,1536]{1,0:T(8,128)S(1)} fusion(f32[256,768]{1,0:T(8,128)S(1)} %slice.177, f32[256,1536]{1,0:T(8,128)S(1)} %convolution_negate_fusion, f32[256,1024]{1,0:T(8,128)S(1)} %constant_dynamic-update-slice_fusion.2), kind=kOutput, calls=%fused_computation.17 | convolution fusion | flops 1208352768 | bytes 4194304 | tf_op jit(solution)/shard_map/dot_general | solution.py:11
  131.5 0.2 select_reduce_fusion
  131.7 1.1 fusion.29
  132.8 1.3 convolution_subtract_fusion.3
  134.1 1.0 fusion.101
  135.1 1.0 convolution_subtract_fusion.2
  136.1 1.0 fusion.25
  137.2 0.5 broadcast_in_dim.49
  137.7 1.1 fusion.13
  138.8 1.1 fusion.11
  139.9 1.0 fusion.9
  140.9 2.0 %copy-done.2 = f32[1,1,512,2048]{3,2,1,0:T(8,128)} copy-done((f32[1,1,512,2048]{3,2,1,0:T(8,128)}, f32[1,1,512,2048]{3,2,1,0:T(8,128)S(1)}, u32[]{:S(2)}) %copy-start.2) | copy-done | bytes 4194328
  142.9 2.0 %fusion.7 = f32[1,1,512,2048]{3,2,1,0:T(8,128)} fusion(f32[1,1,512,2048]{3,2,1,0:T(8,128)} %copy-done.2, s32[]{:T(128)S(6)} %select_n.39, f32[512,512]{1,0:T(8,128)S(1)} %fusion.25, f32[256,1536]{1,0:T(8,128)S(1)} %pad_add_fusion, f32[256,1536]{1,0:T(8,128)S(1)} %pad_add_fusion.1), kind=kOutput, calls=%fused_computation.22 | convolution fusion | flops 805830656 | bytes 5242884 | tf_op jit(solution)/shard_map/dot_general | solution.py:15
  (32 shorter events, 0.4 us)
Async XLA Ops:
  0.0 0.7 copy-start
  10.2 50.0 %collective-permute-start = (f32[256,1024]{1,0:T(8,128)}, f32[256,1024]{1,0:T(8,128)}, u32[]{:S(2)}, u32[]{:S(2)}) collective-permute-start(f32[256,1024]{1,0:T(8,128)} %bitcast.7), channel_id=1, source_target_pairs={{0,4},{1,5},{2,6},{3,7},{4,0},{5,1},{6,2},{7,3},{8,12},{9,13},{10,... | collective-permute-start | bytes 3145736 | tf_op jit(solution)/shard_map/ppermute | solution.py:32
  14.2 75.0 %collective-permute-start.4 = (f32[256,1024]{1,0:T(8,128)}, f32[256,1024]{1,0:T(8,128)}, u32[]{:S(2)}, u32[]{:S(2)}) collective-permute-start(f32[256,1024]{1,0:T(8,128)} %bitcast.7), channel_id=1, source_target_pairs={{0,16},{8,24},{16,0},{24,8},{1,17},{9,25},{17,1},{25,9},{2,18},{10... | collective-permute-start | bytes 3145736 | tf_op jit(solution)/shard_map/ppermute | solution.py:32
  23.7 66.8 %collective-permute-start.3 = (f32[256,1024]{1,0:T(8,128)S(1)}, f32[256,1024]{1,0:T(8,128)}, u32[]{:S(2)}, u32[]{:S(2)}) collective-permute-start(f32[256,1024]{1,0:T(8,128)S(1)} %bitcast.66), channel_id=1, source_target_pairs={{0,16},{8,24},{16,0},{24,8},{1,17},{9,25},{17,1},{25,9},{2,18},{10... | collective-permute-start | bytes 3145736 | tf_op jit(solution)/shard_map/ppermute | solution.py:32
  62.5 3.4 %copy-start.4 = (f32[256,768]{1,0:T(8,128)S(1)}, f32[256,768]{1,0:T(8,128)}, u32[]{:S(2)}) copy-start(f32[256,768]{1,0:T(8,128)} %slice.116) | copy-start | bytes 2359300
  63.8 25.3 %collective-permute-start.1 = (f32[128,1024]{1,0:T(8,128)S(1)}, f32[128,1024]{1,0:T(8,128)S(1)}, u32[]{:S(2)}, u32[]{:S(2)}) collective-permute-start(f32[128,1024]{1,0:T(8,128)S(1)} %get-tuple-element.14), channel_id=1, source_target_pairs={{0,4},{1,5},{2,6},{3,7},{4,0},{5,1},{6,2},{7,3},{8,12},{9,13},{10,... | collective-permute-start | bytes 1572872 | tf_op jit(solution)/shard_map/ppermute | solution.py:32
  63.9 49.7 %collective-permute-start.5 = (f32[256,1024]{1,0:T(8,128)}, f32[256,1024]{1,0:T(8,128)S(1)}, u32[]{:S(2)}, u32[]{:S(2)}) collective-permute-start(f32[256,1024]{1,0:T(8,128)} %collective-permute-done), channel_id=1, source_target_pairs={{0,16},{8,24},{16,0},{24,8},{1,17},{9,25},{17,1},{25,9},{2,18},{10... | collective-permute-start | bytes 3145736 | tf_op jit(solution)/shard_map/ppermute | solution.py:32
  65.9 1.5 %copy-start.1 = (f32[512,768]{1,0:T(8,128)S(1)}, f32[512,768]{1,0:T(8,128)}, u32[]{:S(2)}) copy-start(f32[512,768]{1,0:T(8,128)} %slice.159) | copy-start | bytes 4718596
  89.1 24.3 %collective-permute-start.2 = (f32[128,1024]{1,0:T(8,128)S(1)}, f32[128,1024]{1,0:T(8,128)S(1)}, u32[]{:S(2)}, u32[]{:S(2)}) collective-permute-start(f32[128,1024]{1,0:T(8,128)S(1)} %get-tuple-element.16), channel_id=1, source_target_pairs={{0,4},{1,5},{2,6},{3,7},{4,0},{5,1},{6,2},{7,3},{8,12},{9,13},{10,... | collective-permute-start | bytes 1572872 | tf_op jit(solution)/shard_map/ppermute | solution.py:32
  89.2 2.5 %copy-start.3 = (f32[256,768]{1,0:T(8,128)S(1)}, f32[256,768]{1,0:T(8,128)}, u32[]{:S(2)}) copy-start(f32[256,768]{1,0:T(8,128)} %slice.166) | copy-start | bytes 2359300
  93.2 25.9 %collective-permute-start.6 = (f32[128,1024]{1,0:T(8,128)S(1)}, f32[128,1024]{1,0:T(8,128)S(1)}, u32[]{:S(2)}, u32[]{:S(2)}) collective-permute-start(f32[128,1024]{1,0:T(8,128)S(1)} %collective-permute-done.1), channel_id=1, source_target_pairs={{0,16},{8,24},{16,0},{24,8},{1,17},{9,25},{17,1},{25,9},{2,18},{10... | collective-permute-start | bytes 1572872 | tf_op jit(solution)/shard_map/ppermute | solution.py:32
  113.6 2.6 %copy-start.5 = (f32[256,1024]{1,0:T(8,128)}, f32[256,1024]{1,0:T(8,128)S(1)}, u32[]{:S(2)}) copy-start(f32[256,1024]{1,0:T(8,128)S(1)} %collective-permute-done.5) | copy-start | bytes 3145732
  116.2 13.7 %collective-permute-start.7 = (f32[128,1024]{1,0:T(8,128)S(1)}, f32[128,1024]{1,0:T(8,128)S(1)}, u32[]{:S(2)}, u32[]{:S(2)}) collective-permute-start(f32[128,1024]{1,0:T(8,128)S(1)} %collective-permute-done.2), channel_id=1, source_target_pairs={{0,16},{8,24},{16,0},{24,8},{1,17},{9,25},{17,1},{25,9},{2,18},{10... | collective-permute-start | bytes 1572872 | tf_op jit(solution)/shard_map/ppermute | solution.py:32
  119.1 1.1 slice-start
  140.9 2.0 %copy-start.2 = (f32[1,1,512,2048]{3,2,1,0:T(8,128)}, f32[1,1,512,2048]{3,2,1,0:T(8,128)S(1)}, u32[]{:S(2)}) copy-start(f32[1,1,512,2048]{3,2,1,0:T(8,128)S(1)} %fusion.9) | copy-start | bytes 12582916
where the time goes:
time: 146 us; the launch traced here: 145 us
  waiting for transfers between devices  60.1 us (41%)
  local copies, waits for them, and re-layouts  44.6 us (31%)
  matrix products  26.8 us (18%)
  starting transfers between devices  10.2 us (7%)
  other arithmetic  2.72 us (2%)
    ppermute x8, waiting for transfers between devices, swap(): return lax.ppermute(value, axis, pairs)  60.1 us
    dot_general x15, matrix products, matmul(): jnp.dot(left, right, precision=lax.Precision.HIGHEST, preferred_element_t...  16.1 us
    gather x6, local copies, waits for them, and re-layouts, pick(): picked = jnp.take(matrix, rows, axis=0, mode='clip')  15.9 us
    gather x6, local copies, waits for them, and re-layouts, pick(): return jnp.take(picked, cols, axis=1, mode='clip')  15.6 us
    dot_general x9, matrix products, matmul_high(): jnp.dot(left, right, precision=lax.Precision.HIGH, preferred_element_type...  10.7 us
    ppermute x8, starting transfers between devices, swap(): return lax.ppermute(value, axis, pairs)  10.2 us
    slice x5, local copies, waits for them, and re-layouts, pair_solve(): coupling = jnp.concatenate([first_i1[:, width:], second_i1[:, width:]], 1)  5.61 us
    slice x3, local copies, waits for them, and re-layouts, first_rows(): rows[:, width:]  3.4 us
  transfers between devices with their start and end apart: 8, of which 4 were waited for; matrix products, arithmetic and copies ran while one was open for 33% of the time, Pallas kernels for 0%

commit v1 on v0

--- a/solution.py
+++ b/solution.py
@@ -74,24 +74,34 @@
     width = side_lists.shape[1]
     order = jnp.stack([1 - right, right, 2 + upper, 3 - upper])
     perm = jnp.take(side_lists, order, axis=0, mode="clip").reshape(4 * width)
-    own_i1 = pick(leaf, perm[:width], perm)
-    leaf, own_i1 = lax.optimization_barrier((leaf, own_i1))
+    raw_i1 = jnp.take(leaf, perm[:width], axis=0, mode="clip")
+    vert_raw = swap(raw_i1, "grp")
+    side_raw = swap(raw_i1, "box")
+    vert_perm = swap(perm, "grp")
+    side_perm = swap(perm, "box")
+    diag_perm = swap(side_perm, "grp")
+    diag_raw = swap(side_raw, "grp")
+    leaf, raw_i1 = lax.optimization_barrier((leaf, raw_i1))
+    own_i1 = jnp.take(raw_i1, perm, axis=1, mode="clip")
     own_i2 = pick(leaf, perm[3 * width :], perm)
     own_ov = pick(leaf, perm[width : 3 * width], perm)
+    side_i1 = jnp.take(side_raw, side_perm, axis=1, mode="clip")
+    vert_i1 = jnp.take(vert_raw, vert_perm, axis=1, mode="clip")
+    diag_i1 = jnp.take(diag_raw, diag_perm, axis=1, mode="clip")
 
-    half = width // 2
-    vert_i1 = swap(own_i1, "grp")
     vert_i2 = swap(own_i2, "grp")
-    side_i1 = swap(own_i1, "box")
-    diag_i1 = swap(side_i1, "grp")
-    first_half, side_i1 = lax.optimization_barrier((own_i2[:half], side_i1))
-    side_first = swap(first_half, "box")
-    diag_first = swap(side_first, "grp")
-    second_half, side_first = lax.optimization_barrier((own_i2[half:], side_first))
-    side_second = swap(second_half, "box")
-    diag_second = swap(side_second, "grp")
-    side_i2 = jnp.concatenate([side_first, side_second], 0)
-    diag_i2 = jnp.concatenate([diag_first, diag_second], 0)
+    bounds = [0, width // 2, 3 * width // 4, width]
+    side_parts = []
+    diag_parts = []
+    after = side_raw
+    for lo, hi in zip(bounds[:-1], bounds[1:]):
+        part, after = lax.optimization_barrier((own_i2[lo:hi], after))
+        landed = swap(part, "box")
+        side_parts.append(landed)
+        diag_parts.append(swap(landed, "grp"))
+        after = landed
+    side_i2 = jnp.concatenate(side_parts, 0)
+    diag_i2 = jnp.concatenate(diag_parts, 0)
 
     solved_own = pair_solve(own_i1, side_i1, width)
     own_ext = first_rows(own_ov, solved_own, width)

time: 146 us -> 164 us (1.12)
  local copies, waits for them, and re-layouts: 44.6 us -> 80 us
  waiting for transfers between devices: 60.1 us -> 36.1 us
  starting transfers between devices: 10.2 us -> 14.5 us
  matrix products: 26.8 us -> 28.8 us
    gather x0 -> x9, local copies, waits for them, and re-layouts: none -> 27.2 us  [the longest x2 6.24 us: body(): vert_i1 = jnp.take(vert_raw, vert_perm, axis=1, mode='clip')]
    ppermute x8 -> x13, waiting for transfers between devices: 60.1 us -> 36.1 us  [swap(): return lax.ppermute(value, axis, pairs)]
    unnamed x17 -> x41, local copies, waits for them, and re-layouts: 2.72 us -> 8.59 us
    ppermute x0 -> x3, local copies, waits for them, and re-layouts: none -> 4.66 us  [swap(): return lax.ppermute(value, axis, pairs)]
    ppermute x8 -> x13, starting transfers between devices: 10.2 us -> 14.5 us  [swap(): return lax.ppermute(value, axis, pairs)]
    gather x6 -> x4, local copies, waits for them, and re-layouts: 15.9 us -> 11.8 us  [pick(): picked = jnp.take(matrix, rows, axis=0, mode='clip')]
    gather x6 -> x4, local copies, waits for them, and re-layouts: 15.6 us -> 11.6 us  [pick(): return jnp.take(picked, cols, axis=1, mode='clip')]
    slice x1 -> x2, local copies, waits for them, and re-layouts: 0.07 us -> 3.67 us  [body(): part, after = lax.optimization_barrier((own_i2[lo:hi], after))]
  transfers between devices with their start and end apart: 8 -> 13, of which waited for: 4 -> 4; matrix products, arithmetic and copies ran while one was open for 33% -> 54% of each run, Pallas kernels for 0% -> 0%
where the time goes in v1:
time: 164 us; the launch traced here: 162 us
  local copies, waits for them, and re-layouts  80 us (49%)
  waiting for transfers between devices  36.1 us (22%)
  matrix products  28.8 us (18%)
  starting transfers between devices  14.5 us (9%)
  other arithmetic  2.51 us (2%)
    ppermute x13, waiting for transfers between devices, swap(): return lax.ppermute(value, axis, pairs)  36.1 us
    dot_general x15, matrix products, matmul(): jnp.dot(left, right, precision=lax.Precision.HIGHEST, preferred_element_t...  17.9 us
    ppermute x13, starting transfers between devices, swap(): return lax.ppermute(value, axis, pairs)  14.5 us
    gather x4, local copies, waits for them, and re-layouts, pick(): picked = jnp.take(matrix, rows, axis=0, mode='clip')  11.8 us
    gather x4, local copies, waits for them, and re-layouts, pick(): return jnp.take(picked, cols, axis=1, mode='clip')  11.6 us
    dot_general x9, matrix products, matmul_high(): jnp.dot(left, right, precision=lax.Precision.HIGH, preferred_element_type...  10.9 us
    unnamed x41, local copies, waits for them, and re-layouts  8.59 us
    gather x2, local copies, waits for them, and re-layouts, body(): vert_i1 = jnp.take(vert_raw, vert_perm, axis=1, mode='clip')  6.24 us
  transfers between devices with their start and end apart: 13, of which 4 were waited for; matrix products, arithmetic and copies ran while one was open for 54% of the time, Pallas kernels for 0%

profile of v1, /device:TPU:0, one launch (start us, length us, event | category | flops | bytes accessed | tf_op | source)
XLA Modules:
  0.0 162.5 jit_solution(15680184526923306601)
XLA Ops:
  1.3 4.7 %gather_fusion.1 = f32[256,1024]{1,0:T(8,128)} fusion(f32[1024,1024]{1,0:T(8,128)} %bitcast.66, s32[1024]{0:T(1024)S(1)} %pad_clamp_fusion.2), kind=kCustom, calls=%fused_computation.1 | custom fusion | bytes 2098176 | tf_op jit(solution)/shard_map/jit(_take)/gather | solution.py:77
  6.0 4.0 %collective-permute-start = (f32[256,1024]{1,0:T(8,128)}, f32[256,1024]{1,0:T(8,128)}, u32[]{:S(2)}, u32[]{:S(2)}) collective-permute-start(f32[256,1024]{1,0:T(8,128)} %gather_fusion.1), channel_id=1, source_target_pairs={{0,4},{1,5},{2,6},{3,7},{4,0},{5,1},{6,2},{7,3},{8,12},{9,13},{10,... | collective-permute-start | bytes 3145736 | tf_op jit(solution)/shard_map/ppermute | solution.py:32
  10.0 1.5 collective-permute-start.6
  12.1 3.8 %gather_fusion.6 = f32[256,1024]{1,0:T(8,128)S(1)} fusion(f32[1024,1024]{1,0:T(8,128)} %bitcast.67, s32[1024]{0:T(1024)S(1)} %get-tuple-element.27), kind=kCustom, calls=%fused_computation.6 | custom fusion | bytes 2098176 | tf_op jit(solution)/shard_map/jit(_take)/gather | solution.py:65
  16.2 3.5 %gather_fusion.7 = f32[1024,256]{1,0:T(8,128)S(1)} fusion(f32[256,1024]{0,1:T(8,128)S(1)} %copy.9, s32[1024]{0:T(1024)S(1)} %broadcast_clamp_fusion.3), kind=kCustom, calls=%fused_computation.7 | custom fusion | bytes 2101248 | tf_op jit(solution)/shard_map/jit(_take)/gather | solution.py:66
  19.7 1.4 copy.10
  21.0 1.9 %collective-permute-start.5 = (f32[256,1024]{1,0:T(8,128)}, f32[256,1024]{1,0:T(8,128)}, u32[]{:S(2)}, u32[]{:S(2)}) collective-permute-start(f32[256,1024]{1,0:T(8,128)} %bitcast.11), channel_id=1, source_target_pairs={{0,16},{8,24},{16,0},{24,8},{1,17},{9,25},{17,1},{25,9},{2,18},{10... | collective-permute-start | bytes 3145736 | tf_op jit(solution)/shard_map/ppermute | solution.py:32
  22.9 1.8 %fusion.97 = (f32[64,1024]{1,0:T(8,128)}, f32[64,1024]{1,0:T(8,128)S(1)}) fusion(f32[256,1024]{1,0:T(8,128)} %bitcast.11), kind=kLoop, calls=%fused_computation.152 | loop fusion | bytes 1048576 | tf_op jit(solution)/shard_map/slice | solution.py:98
  24.6 2.1 %slice.179 = f32[256,768]{1,0:T(8,128)} slice(f32[256,1024]{1,0:T(8,128)} %bitcast.11), slice={[0:256], [256:1024]} | slice | bytes 1572864 | tf_op jit(solution)/shard_map/slice | solution.py:44
  26.7 1.9 %slice.181 = f32[128,1024]{1,0:T(8,128)} slice(f32[256,1024]{1,0:T(8,128)} %bitcast.11), slice={[0:128], [0:1024]} | slice | bytes 1048576 | tf_op jit(solution)/shard_map/slice | solution.py:98
  28.6 1.6 copy.5
  30.2 3.5 %gather_fusion.4 = f32[1024,256]{1,0:T(8,128)S(1)} fusion(f32[256,1024]{0,1:T(8,128)S(1)} %copy.5, s32[1024]{0:T(1024)S(1)} %broadcast_clamp_fusion.3), kind=kCustom, calls=%fused_computation.4 | custom fusion | bytes 2101248 | tf_op jit(solution)/shard_map/jit(_take)/gather | solution.py:85
  34.0 1.1 slice.173
  35.3 5.8 %gather_fusion.2 = f32[512,1024]{1,0:T(8,128)} fusion(f32[1024,1024]{1,0:T(8,128)} %bitcast.68, s32[1024]{0:T(1024)S(1)} %get-tuple-element.28), kind=kCustom, calls=%fused_computation.2 | custom fusion | bytes 4196352 | tf_op jit(solution)/shard_map/jit(_take)/gather | solution.py:65
  41.1 1.9 %copy.3 = f32[512,1024]{0,1:T(8,128)S(1)} copy(f32[512,1024]{1,0:T(8,128)} %gather_fusion.2) | data formatting | bytes 4194304 | tf_op jit(solution)/shard_map/jit(_take)/gather | solution.py:65
  43.0 4.9 %gather_fusion.3 = f32[1024,512]{1,0:T(8,128)} fusion(f32[512,1024]{0,1:T(8,128)S(1)} %copy.3, s32[1024]{0:T(1024)S(1)} %broadcast_clamp_fusion.3), kind=kCustom, calls=%fused_computation.3 | custom fusion | bytes 4198400 | tf_op jit(solution)/shard_map/jit(_take)/gather | solution.py:66
  47.9 1.9 %copy.4 = f32[1024,512]{0,1:T(8,128)S(1)} copy(f32[1024,512]{1,0:T(8,128)} %gather_fusion.3) | data formatting | bytes 4194304 | tf_op jit(solution)/shard_map/jit(_take)/gather | solution.py:66
  49.8 1.3 slice.169
  51.1 5.0 %collective-permute-done.1 = s32[1024]{0:T(1024)S(1)} collective-permute-done((s32[1024]{0:T(1024)S(1)}, s32[1024]{0:T(1024)S(1)}, u32[]{:S(2)}, u32[]{:S(2)}) %collective-permute-start.1) | collective-permute-done | bytes 4128 | tf_op jit(solution)/shard_map/ppermute | solution.py:32
  56.1 1.6 collective-permute-start.9
  57.7 2.0 %collective-permute-done.9 = s32[1024]{0:T(1024)S(1)} collective-permute-done((s32[1024]{0:T(1024)S(1)}, s32[1024]{0:T(1024)S(1)}, u32[]{:S(2)}, u32[]{:S(2)}) %collective-permute-start.9) | collective-permute-done | bytes 4128 | tf_op jit(solution)/shard_map/ppermute | solution.py:32
  59.7 1.6 copy.7
  61.3 4.7 %gather_fusion.5 = f32[1024,256]{1,0:T(8,128)} fusion(f32[256,1024]{0,1:T(8,128)S(1)} %copy.7, s32[1024]{0:T(1024)S(1)} %broadcast_clamp_fusion.2), kind=kCustom, calls=%fused_computation.5 | custom fusion | bytes 2101248 | tf_op jit(solution)/shard_map/jit(_take)/gather | solution.py:88
  66.0 1.6 copy.8
  67.5 1.1 select_reduce_fusion.2
  70.5 1.4 convolution_negate_fusion.1
  72.0 1.6 %collective-permute-start.8 = (f32[256,1024]{1,0:T(8,128)}, f32[256,1024]{1,0:T(8,128)}, u32[]{:S(2)}, u32[]{:S(2)}) collective-permute-start(f32[256,1024]{1,0:T(8,128)} %collective-permute-done), channel_id=1, source_target_pairs={{0,16},{8,24},{16,0},{24,8},{1,17},{9,25},{17,1},{25,9},{2,18},{10... | collective-permute-start | bytes 3145736 | tf_op jit(solution)/shard_map/ppermute | solution.py:32
  73.6 2.7 %convolution_add_fusion = f32[512,1536]{1,0:T(8,128)S(1)} fusion(f32[256,1536]{1,0:T(8,128)S(1)} %convolution_negate_fusion.1, f32[512,768]{1,0:T(8,128)S(1)} %copy-done.7, f32[512,1024]{1,0:T(8,128)S(1)} %bitcast.70), kind=kOutput, calls=%fused_computation.10 | convolution fusion | flops 2416705536 | bytes 6815744 | tf_op jit(solution)/shard_map/dot_general | solution.py:11
  76.3 18.4 %collective-permute-done.2 = f32[128,1024]{1,0:T(8,128)} collective-permute-done((f32[128,1024]{1,0:T(8,128)S(1)}, f32[128,1024]{1,0:T(8,128)}, u32[]{:S(2)}, u32[]{:S(2)}) %collective-permute-start.2) | collective-permute-done | bytes 524320 | tf_op jit(solution)/shard_map/ppermute | solution.py:32
  94.7 2.4 %convolution_add_fusion.1 = f32[256,1536]{1,0:T(8,128)S(1)} fusion(f32[256,1536]{1,0:T(8,128)S(1)} %convolution_negate_fusion.1, f32[256,768]{1,0:T(8,128)S(1)} %copy-done.11, f32[256,1024]{1,0:T(8,128)} %bitcast.11), kind=kOutput, calls=%fused_computation.11 | convolution fusion | flops 1208352768 | bytes 4194304 | tf_op jit(solution)/shard_map/dot_general | solution.py:11
  97.2 10.7 %collective-permute-done.3 = f32[64,1024]{1,0:T(8,128)} collective-permute-done((f32[64,1024]{1,0:T(8,128)S(1)}, f32[64,1024]{1,0:T(8,128)}, u32[]{:S(2)}, u32[]{:S(2)}) %collective-permute-start.3) | collective-permute-done | bytes 262176 | tf_op jit(solution)/shard_map/ppermute | solution.py:32
  107.9 1.1 fusion.96
  108.9 1.6 copy.11
  110.5 4.7 %gather_fusion.8 = f32[1024,256]{1,0:T(8,128)} fusion(f32[256,1024]{0,1:T(8,128)S(1)} %copy.11, s32[1024]{0:T(1024)S(1)} %broadcast_clamp_fusion.1), kind=kCustom, calls=%fused_computation.8 | custom fusion | bytes 2101248 | tf_op jit(solution)/shard_map/jit(_take)/gather | solution.py:89
  115.2 1.6 copy.12
  116.7 1.0 slice.190
  117.8 1.2 slice.186
  119.0 1.1 collective-permute-start.10
  120.0 1.1 constant_dynamic-update-slice_fusion.2
  121.2 1.1 collective-permute-start.11
  122.2 1.0 constant_dynamic-update-slice_fusion.1
  123.3 1.0 constant_dynamic-update-slice_fusion
  124.3 1.1 collective-permute-start.12
  125.4 2.6 %pad_add_fusion.2 = f32[256,1536]{1,0:T(8,128)} fusion(f32[256,768]{1,0:T(8,128)S(1)} %slice.184, f32[256,1536]{1,0:T(8,128)S(1)} %copy-done.4, f32[256,1024]{1,0:T(8,128)S(1)} %constant_dynamic-update-slice_fusion), kind=kOutput, calls=%fused_computation.22 | convolution fusion | flops 1208352768 | bytes 4194304 | tf_op jit(solution)/shard_map/dot_general | solution.py:11
  128.0 1.6 copy.13
  129.6 4.7 %gather_fusion.9 = f32[1024,256]{1,0:T(8,128)} fusion(f32[256,1024]{0,1:T(8,128)S(1)} %copy.13, s32[1024]{0:T(1024)S(1)} %broadcast_clamp_fusion), kind=kCustom, calls=%fused_computation.9 | custom fusion | bytes 2101248 | tf_op jit(solution)/shard_map/jit(_take)/gather | solution.py:90
  134.2 1.6 copy.14
  135.8 1.1 select_reduce_fusion.1
  138.7 1.1 constant_dynamic-update-slice_fusion.5
  139.8 1.4 convolution_negate_fusion
  141.2 1.0 constant_dynamic-update-slice_fusion.4
  142.2 2.4 %pad_add_fusion.1 = f32[256,1536]{1,0:T(8,128)S(1)} fusion(f32[256,768]{1,0:T(8,128)S(1)} %slice.186, f32[256,1536]{1,0:T(8,128)S(1)} %convolution_negate_fusion, f32[256,1024]{1,0:T(8,128)} %collective-permute-done.5), kind=kOutput, calls=%fused_computation.21 | convolution fusion | flops 1208352768 | bytes 4194304 | tf_op jit(solution)/shard_map/dot_general | solution.py:11
  145.7 1.5 pad_add_fusion
  147.4 1.1 fusion.29
  148.5 1.3 convolution_subtract_fusion.3
  149.8 1.0 fusion.101
  150.9 1.0 convolution_subtract_fusion.2
  152.1 1.0 fusion.25
  153.6 1.4 copy-done.6
  155.0 1.3 fusion.13
  156.3 1.0 fusion.11
  157.4 1.0 fusion.9
  158.5 2.0 %copy-done.8 = f32[1,1,512,2048]{3,2,1,0:T(8,128)} copy-done((f32[1,1,512,2048]{3,2,1,0:T(8,128)}, f32[1,1,512,2048]{3,2,1,0:T(8,128)S(1)}, u32[]{:S(2)}) %copy-start.8) | copy-done | bytes 4194328
  160.5 2.0 %fusion.7 = f32[1,1,512,2048]{3,2,1,0:T(8,128)} fusion(f32[1,1,512,2048]{3,2,1,0:T(8,128)} %copy-done.8, s32[]{:T(128)S(6)} %select_n.39, f32[512,512]{1,0:T(8,128)S(1)} %fusion.25, f32[256,1536]{1,0:T(8,128)S(1)} %pad_add_fusion, f32[256,1536]{1,0:T(8,128)S(1)} %pad_add_fusion.1), kind=kOutput, calls=%fused_computation.25 | convolution fusion | flops 805830656 | bytes 5242884 | tf_op jit(solution)/shard_map/dot_general | solution.py:15
  (79 shorter events, 8.2 us)
Async XLA Ops:
  0.0 0.7 copy-start
  6.0 53.7 %collective-permute-start = (f32[256,1024]{1,0:T(8,128)}, f32[256,1024]{1,0:T(8,128)}, u32[]{:S(2)}, u32[]{:S(2)}) collective-permute-start(f32[256,1024]{1,0:T(8,128)} %gather_fusion.1), channel_id=1, source_target_pairs={{0,4},{1,5},{2,6},{3,7},{4,0},{5,1},{6,2},{7,3},{8,12},{9,13},{10,... | collective-permute-start | bytes 3145736 | tf_op jit(solution)/shard_map/ppermute | solution.py:32
  10.0 98.9 %collective-permute-start.6 = (f32[256,1024]{1,0:T(8,128)}, f32[256,1024]{1,0:T(8,128)}, u32[]{:S(2)}, u32[]{:S(2)}) collective-permute-start(f32[256,1024]{1,0:T(8,128)} %gather_fusion.1), channel_id=1, source_target_pairs={{0,16},{8,24},{16,0},{24,8},{1,17},{9,25},{17,1},{25,9},{2,18},{10... | collective-permute-start | bytes 3145736 | tf_op jit(solution)/shard_map/ppermute | solution.py:32
  11.6 44.6 %collective-permute-start.1 = (s32[1024]{0:T(1024)S(1)}, s32[1024]{0:T(1024)S(1)}, u32[]{:S(2)}, u32[]{:S(2)}) collective-permute-start(s32[1024]{0:T(1024)S(1)} %bitcast.80), channel_id=1, source_target_pairs={{0,4},{1,5},{2,6},{3,7},{4,0},{5,1},{6,2},{7,3},{8,12},{9,13},{10,... | collective-permute-start | bytes 12296 | tf_op jit(solution)/shard_map/ppermute | solution.py:32
  11.9 45.8 %collective-permute-start.7 = (s32[1024]{0:T(1024)S(1)}, s32[1024]{0:T(1024)S(1)}, u32[]{:S(2)}, u32[]{:S(2)}) collective-permute-start(s32[1024]{0:T(1024)S(1)} %bitcast.81), channel_id=1, source_target_pairs={{0,16},{8,24},{16,0},{24,8},{1,17},{9,25},{17,1},{25,9},{2,18},{10... | collective-permute-start | bytes 12296 | tf_op jit(solution)/shard_map/ppermute | solution.py:32
  21.0 96.7 %collective-permute-start.5 = (f32[256,1024]{1,0:T(8,128)}, f32[256,1024]{1,0:T(8,128)}, u32[]{:S(2)}, u32[]{:S(2)}) collective-permute-start(f32[256,1024]{1,0:T(8,128)} %bitcast.11), channel_id=1, source_target_pairs={{0,16},{8,24},{16,0},{24,8},{1,17},{9,25},{17,1},{25,9},{2,18},{10... | collective-permute-start | bytes 3145736 | tf_op jit(solution)/shard_map/ppermute | solution.py:32
  34.0 1.3 copy-start.9
  56.1 3.6 %collective-permute-start.9 = (s32[1024]{0:T(1024)S(1)}, s32[1024]{0:T(1024)S(1)}, u32[]{:S(2)}, u32[]{:S(2)}) collective-permute-start(s32[1024]{0:T(1024)S(1)} %collective-permute-done.1), channel_id=1, source_target_pairs={{0,16},{8,24},{16,0},{24,8},{1,17},{9,25},{17,1},{25,9},{2,18},{10... | collective-permute-start | bytes 12296 | tf_op jit(solution)/shard_map/ppermute | solution.py:32
  68.7 1.7 %copy-start.16 = (f32[128,1024]{1,0:T(8,128)S(1)}, f32[128,1024]{1,0:T(8,128)}, u32[]{:S(2)}) copy-start(f32[128,1024]{1,0:T(8,128)} %slice.181) | copy-start | bytes 1572868
  68.7 1.8 %copy-start.12 = (f32[256,768]{1,0:T(8,128)S(1)}, f32[256,768]{1,0:T(8,128)}, u32[]{:S(2)}) copy-start(f32[256,768]{1,0:T(8,128)} %slice.173) | copy-start | bytes 2359300
  70.4 3.2 %copy-start.7 = (f32[512,768]{1,0:T(8,128)S(1)}, f32[512,768]{1,0:T(8,128)}, u32[]{:S(2)}) copy-start(f32[512,768]{1,0:T(8,128)} %slice.169) | copy-start | bytes 4718596
  70.4 24.3 %collective-permute-start.2 = (f32[128,1024]{1,0:T(8,128)S(1)}, f32[128,1024]{1,0:T(8,128)}, u32[]{:S(2)}, u32[]{:S(2)}) collective-permute-start(f32[128,1024]{1,0:T(8,128)S(1)} %copy-done.16), channel_id=1, source_target_pairs={{0,4},{1,5},{2,6},{3,7},{4,0},{5,1},{6,2},{7,3},{8,12},{9,13},{10,... | collective-permute-start | bytes 1572872 | tf_op jit(solution)/shard_map/ppermute | solution.py:32
  71.9 22.8 %copy-start.3 = (f32[256,1536]{1,0:T(8,128)}, f32[256,1536]{1,0:T(8,128)S(1)}, u32[]{:S(2)}) copy-start(f32[256,1536]{1,0:T(8,128)S(1)} %convolution_negate_fusion.1) | copy-start | bytes 4718596
  72.0 22.8 %copy-start.11 = (f32[256,768]{1,0:T(8,128)S(1)}, f32[256,768]{1,0:T(8,128)}, u32[]{:S(2)}) copy-start(f32[256,768]{1,0:T(8,128)} %slice.179) | copy-start | bytes 2359300
  72.0 56.1 %collective-permute-start.8 = (f32[256,1024]{1,0:T(8,128)}, f32[256,1024]{1,0:T(8,128)}, u32[]{:S(2)}, u32[]{:S(2)}) collective-permute-start(f32[256,1024]{1,0:T(8,128)} %collective-permute-done), channel_id=1, source_target_pairs={{0,16},{8,24},{16,0},{24,8},{1,17},{9,25},{17,1},{25,9},{2,18},{10... | collective-permute-start | bytes 3145736 | tf_op jit(solution)/shard_map/ppermute | solution.py:32
  76.3 31.5 %copy-start.5 = (f32[512,1536]{1,0:T(8,128)}, f32[512,1536]{1,0:T(8,128)S(1)}, u32[]{:S(2)}) copy-start(f32[512,1536]{1,0:T(8,128)S(1)} %convolution_add_fusion) | copy-start | bytes 9437188
  94.7 13.1 %collective-permute-start.3 = (f32[64,1024]{1,0:T(8,128)S(1)}, f32[64,1024]{1,0:T(8,128)}, u32[]{:S(2)}, u32[]{:S(2)}) collective-permute-start(f32[64,1024]{1,0:T(8,128)S(1)} %get-tuple-element.13), channel_id=1, source_target_pairs={{0,4},{1,5},{2,6},{3,7},{4,0},{5,1},{6,2},{7,3},{8,12},{9,13},{10,... | collective-permute-start | bytes 786440 | tf_op jit(solution)/shard_map/ppermute | solution.py:32
  107.9 15.4 %collective-permute-start.4 = (f32[64,1024]{1,0:T(8,128)}, f32[64,1024]{1,0:T(8,128)}, u32[]{:S(2)}, u32[]{:S(2)}) collective-permute-start(f32[64,1024]{1,0:T(8,128)} %get-tuple-element.14), channel_id=1, source_target_pairs={{0,4},{1,5},{2,6},{3,7},{4,0},{5,1},{6,2},{7,3},{8,12},{9,13},{10,... | collective-permute-start | bytes 786440 | tf_op jit(solution)/shard_map/ppermute | solution.py:32
  116.7 2.2 %copy-start.10 = (f32[1024,256]{0,1:T(8,128)}, f32[1024,256]{0,1:T(8,128)S(1)}, u32[]{:S(2)}) copy-start(f32[1024,256]{0,1:T(8,128)S(1)} %copy.12) | copy-start | bytes 3145732
  119.0 19.7 %collective-permute-start.10 = (f32[128,1024]{1,0:T(8,128)}, f32[128,1024]{1,0:T(8,128)}, u32[]{:S(2)}, u32[]{:S(2)}) collective-permute-start(f32[128,1024]{1,0:T(8,128)} %collective-permute-done.2), channel_id=1, source_target_pairs={{0,16},{8,24},{16,0},{24,8},{1,17},{9,25},{17,1},{25,9},{2,18},{10... | collective-permute-start | bytes 1572872 | tf_op jit(solution)/shard_map/ppermute | solution.py:32
  121.2 4.2 %copy-start.4 = (f32[256,1536]{1,0:T(8,128)S(1)}, f32[256,1536]{1,0:T(8,128)}, u32[]{:S(2)}) copy-start(f32[256,1536]{1,0:T(8,128)} %copy-done.3) | copy-start | bytes 4718596
  121.2 20.0 %collective-permute-start.11 = (f32[64,1024]{1,0:T(8,128)}, f32[64,1024]{1,0:T(8,128)}, u32[]{:S(2)}, u32[]{:S(2)}) collective-permute-start(f32[64,1024]{1,0:T(8,128)} %collective-permute-done.3), channel_id=1, source_target_pairs={{0,16},{8,24},{16,0},{24,8},{1,17},{9,25},{17,1},{25,9},{2,18},{10... | collective-permute-start | bytes 786440 | tf_op jit(solution)/shard_map/ppermute | solution.py:32
  124.3 20.4 %collective-permute-start.12 = (f32[64,1024]{1,0:T(8,128)}, f32[64,1024]{1,0:T(8,128)}, u32[]{:S(2)}, u32[]{:S(2)}) collective-permute-start(f32[64,1024]{1,0:T(8,128)} %collective-permute-done.4), channel_id=1, source_target_pairs={{0,16},{8,24},{16,0},{24,8},{1,17},{9,25},{17,1},{25,9},{2,18},{10... | collective-permute-start | bytes 786440 | tf_op jit(solution)/shard_map/ppermute | solution.py:32
  137.9 1.9 %copy-start.13 = (f32[256,768]{1,0:T(8,128)S(1)}, f32[256,768]{1,0:T(8,128)}, u32[]{:S(2)}) copy-start(f32[256,768]{1,0:T(8,128)} %slice.190) | copy-start | bytes 2359300
  145.7 1.5 copy-start.2
  150.9 1.0 copy-start.14
  150.9 1.2 copy-start.15
  153.1 1.9 %copy-start.6 = (f32[512,1536]{1,0:T(8,128)S(1)}, f32[512,1536]{1,0:T(8,128)}, u32[]{:S(2)}) copy-start(f32[512,1536]{1,0:T(8,128)} %copy-done.5) | copy-start | bytes 9437188
  157.4 5.1 %copy-start.1 = (s32[1,1,4,256]{3,2,1,0:T(4,128)S(1)}, s32[1,1,4,256]{3,2,1,0:T(4,128)}, u32[]{:S(2)}) copy-start(s32[1,1,4,256]{3,2,1,0:T(4,128)} %param.3) | copy-start | bytes 12292
  158.5 2.0 %copy-start.8 = (f32[1,1,512,2048]{3,2,1,0:T(8,128)}, f32[1,1,512,2048]{3,2,1,0:T(8,128)S(1)}, u32[]{:S(2)}) copy-start(f32[1,1,512,2048]{3,2,1,0:T(8,128)S(1)} %fusion.9) | copy-start | bytes 12582916

commit v2 on v0

--- a/solution.py
+++ b/solution.py
@@ -32,11 +32,8 @@
     return lax.ppermute(value, axis, pairs)
 
 
-def pair_solve(first_i1, second_i1, width):
-    system = first_i1[:, :width] + second_i1[:, :width]
-    inverse = newton(system, ITERS_LOW)
-    coupling = jnp.concatenate([first_i1[:, width:], second_i1[:, width:]], 1)
-    return -matmul(inverse, coupling)
+def pair_solve(inverse, first_ie, second_ie):
+    return -matmul(inverse, jnp.concatenate([first_ie, second_ie], 1))
 
 
 def first_rows(rows, solved, width):
@@ -80,10 +77,12 @@
     own_ov = pick(leaf, perm[width : 3 * width], perm)
 
     half = width // 2
-    vert_i1 = swap(own_i1, "grp")
+    vert_ie = swap(own_i1[:, width:], "grp")
     vert_i2 = swap(own_i2, "grp")
     side_i1 = swap(own_i1, "box")
-    diag_i1 = swap(side_i1, "grp")
+    diag_ie = swap(side_i1[:, width:], "grp")
+    inverse_own = newton(own_i1[:, :width] + side_i1[:, :width], ITERS_LOW)
+    inverse_other = swap(inverse_own, "grp")
     first_half, side_i1 = lax.optimization_barrier((own_i2[:half], side_i1))
     side_first = swap(first_half, "box")
     diag_first = swap(side_first, "grp")
@@ -93,12 +92,12 @@
     side_i2 = jnp.concatenate([side_first, side_second], 0)
     diag_i2 = jnp.concatenate([diag_first, diag_second], 0)
 
-    solved_own = pair_solve(own_i1, side_i1, width)
+    solved_own = pair_solve(inverse_own, own_i1[:, width:], side_i1[:, width:])
     own_ext = first_rows(own_ov, solved_own, width)
     own_int = first_rows(own_i2, solved_own, width)
     side_int = second_rows(side_i2, solved_own, width)
 
-    solved_other = pair_solve(vert_i1, diag_i1, width)
+    solved_other = pair_solve(inverse_other, vert_ie, diag_ie)
     vert_int = first_rows(vert_i2, solved_other, width)
     diag_int = second_rows(diag_i2, solved_other, width)
 

time: 146 us -> 142 us (0.973)
  waiting for transfers between devices: 60.1 us -> 58.2 us
    ppermute x8 -> x9, waiting for transfers between devices: 60.1 us -> 58.2 us  [swap(): return lax.ppermute(value, axis, pairs)]
    slice x5 -> x3, local copies, waits for them, and re-layouts: 5.61 us -> 4.48 us  [the longest x2 3.3 us: body(): solved_own = pair_solve(inverse_own, own_i1[:, width:], side_i1[:, width:])]
    dot_general x15 -> x11, matrix products: 16.1 us -> 16.8 us  [matmul(): jnp.dot(left, right, precision=lax.Precision.HIGHEST, preferred_element_t...]
    ppermute x8 -> x9, starting transfers between devices: 10.2 us -> 10.6 us  [swap(): return lax.ppermute(value, axis, pairs)]
  transfers between devices with their start and end apart: 8 -> 9, of which waited for: 4 -> 4; matrix products, arithmetic and copies ran while one was open for 33% -> 33% of each run, Pallas kernels for 0% -> 0%
where the time goes in v2:
time: 142 us
  waiting for transfers between devices  58.2 us (41%)
  local copies, waits for them, and re-layouts  43.6 us (31%)
  matrix products  27.5 us (19%)
  starting transfers between devices  10.6 us (7%)
  other arithmetic  1.46 us (1%)
    ppermute x9, waiting for transfers between devices, swap(): return lax.ppermute(value, axis, pairs)  58.2 us
    dot_general x11, matrix products, matmul(): jnp.dot(left, right, precision=lax.Precision.HIGHEST, preferred_element_t...  16.8 us
    gather x6, local copies, waits for them, and re-layouts, pick(): picked = jnp.take(matrix, rows, axis=0, mode='clip')  15.9 us
    gather x6, local copies, waits for them, and re-layouts, pick(): return jnp.take(picked, cols, axis=1, mode='clip')  15.6 us
    dot_general x9, matrix products, matmul_high(): jnp.dot(left, right, precision=lax.Precision.HIGH, preferred_element_type...  10.7 us
    ppermute x9, starting transfers between devices, swap(): return lax.ppermute(value, axis, pairs)  10.6 us
    slice x3, local copies, waits for them, and re-layouts, first_rows(): rows[:, width:]  3.48 us
    slice x2, local copies, waits for them, and re-layouts, body(): solved_own = pair_solve(inverse_own, own_i1[:, width:], side_i1[:, width:])  3.3 us
  transfers between devices with their start and end apart: 9, of which 4 were waited for; matrix products, arithmetic and copies ran while one was open for 33% of the time, Pallas kernels for 0%

profile of v2, /device:TPU:0, one launch (start us, length us, event | category | flops | bytes accessed | tf_op | source)
XLA Modules:
  0.0 141.8 jit_solution(7888558930051549585)
XLA Ops:
  0.0 0.1 pad_add_fusion.3
  0.1 0.6 copy-done
  0.7 0.6 gather_fusion
  1.3 3.8 %gather_fusion.1 = f32[256,1024]{1,0:T(8,128)S(1)} fusion(f32[1024,1024]{1,0:T(8,128)} %bitcast.57, s32[1024]{0:T(1024)S(1)} %get-tuple-element.29), kind=kCustom, calls=%fused_computation.1 | custom fusion | bytes 2098176 | tf_op jit(solution)/shard_map/jit(_take)/gather | solution.py:62
  5.1 0.3 copy.3
  5.4 3.5 %gather_fusion.2 = f32[1024,256]{1,0:T(8,128)S(1)} fusion(f32[256,1024]{0,1:T(8,128)S(1)} %copy.3, s32[1024]{0:T(1024)S(1)} %get-tuple-element.30), kind=kCustom, calls=%fused_computation.2 | custom fusion | bytes 2101248 | tf_op jit(solution)/shard_map/jit(_take)/gather | solution.py:63
  8.9 1.3 copy.4
  10.2 4.0 %collective-permute-start = (f32[256,1024]{1,0:T(8,128)}, f32[256,1024]{1,0:T(8,128)}, u32[]{:S(2)}, u32[]{:S(2)}) collective-permute-start(f32[256,1024]{1,0:T(8,128)} %bitcast.7), channel_id=1, source_target_pairs={{0,4},{1,5},{2,6},{3,7},{4,0},{5,1},{6,2},{7,3},{8,12},{9,13},{10,... | collective-permute-start | bytes 3145736 | tf_op jit(solution)/shard_map/ppermute | solution.py:32
  14.2 2.1 %slice.106 = f32[256,768]{1,0:T(8,128)} slice(f32[256,1024]{1,0:T(8,128)} %bitcast.7), slice={[0:256], [256:1024]} | slice | bytes 1572864 | tf_op jit(solution)/shard_map/slice | solution.py:95
  16.3 1.5 %collective-permute-start.5 = (f32[256,768]{1,0:T(8,128)}, f32[256,768]{1,0:T(8,128)}, u32[]{:S(2)}, u32[]{:S(2)}) collective-permute-start(f32[256,768]{1,0:T(8,128)} %slice.106), channel_id=1, source_target_pairs={{0,16},{8,24},{16,0},{24,8},{1,17},{9,25},{17,1},{25,9},{2,18},{10... | collective-permute-start | bytes 2359304 | tf_op jit(solution)/shard_map/ppermute | solution.py:32
  17.9 3.8 %gather_fusion.5 = f32[256,1024]{1,0:T(8,128)S(1)} fusion(f32[1024,1024]{1,0:T(8,128)} %bitcast.58, s32[1024]{0:T(1024)S(1)} %get-tuple-element.27), kind=kCustom, calls=%fused_computation.5 | custom fusion | bytes 2098176 | tf_op jit(solution)/shard_map/jit(_take)/gather | solution.py:62
  21.6 0.3 copy.7
  22.0 3.5 %gather_fusion.6 = f32[1024,256]{1,0:T(8,128)S(1)} fusion(f32[256,1024]{0,1:T(8,128)S(1)} %copy.7, s32[1024]{0:T(1024)S(1)} %get-tuple-element.30), kind=kCustom, calls=%fused_computation.6 | custom fusion | bytes 2101248 | tf_op jit(solution)/shard_map/jit(_take)/gather | solution.py:63
  25.5 0.3 copy.8
  25.8 0.6 collective-permute-start.3
  26.4 1.0 slice.156
  27.3 5.8 %gather_fusion.3 = f32[512,1024]{1,0:T(8,128)} fusion(f32[1024,1024]{1,0:T(8,128)} %bitcast.59, s32[1024]{0:T(1024)S(1)} %get-tuple-element.28), kind=kCustom, calls=%fused_computation.3 | custom fusion | bytes 4196352 | tf_op jit(solution)/shard_map/jit(_take)/gather | solution.py:62
  33.1 1.9 %copy.5 = f32[512,1024]{0,1:T(8,128)S(1)} copy(f32[512,1024]{1,0:T(8,128)} %gather_fusion.3) | data formatting | bytes 4194304 | tf_op jit(solution)/shard_map/jit(_take)/gather | solution.py:62
  35.0 4.9 %gather_fusion.4 = f32[1024,512]{1,0:T(8,128)} fusion(f32[512,1024]{0,1:T(8,128)S(1)} %copy.5, s32[1024]{0:T(1024)S(1)} %get-tuple-element.30), kind=kCustom, calls=%fused_computation.4 | custom fusion | bytes 4198400 | tf_op jit(solution)/shard_map/jit(_take)/gather | solution.py:63
  39.9 2.1 %copy.6 = f32[1024,512]{0,1:T(8,128)S(1)} copy(f32[1024,512]{1,0:T(8,128)} %gather_fusion.4) | data formatting | bytes 4194304 | tf_op jit(solution)/shard_map/jit(_take)/gather | solution.py:63
  42.0 1.3 slice.148
  43.3 0.1 fusion.78
  43.4 16.8 %collective-permute-done = f32[256,1024]{1,0:T(8,128)} collective-permute-done((f32[256,1024]{1,0:T(8,128)}, f32[256,1024]{1,0:T(8,128)}, u32[]{:S(2)}, u32[]{:S(2)}) %collective-permute-start) | collective-permute-done | bytes 1048608 | tf_op jit(solution)/shard_map/ppermute | solution.py:32
  60.2 1.1 select_reduce_fusion.1
  61.3 0.4 fusion.52
  61.8 0.5 convolution_subtract_fusion.5
  62.2 1.2 slice.109
  63.4 0.1 collective-permute-start.1
  63.5 0.4 fusion.80
  63.9 0.4 convolution_subtract_fusion.4
  64.3 1.6 %collective-permute-start.4 = (f32[256,256]{1,0:T(8,128)S(1)}, f32[256,256]{1,0:T(8,128)S(1)}, u32[]{:S(2)}, u32[]{:S(2)}) collective-permute-start(f32[256,256]{1,0:T(8,128)S(1)} %convolution_subtract_fusion.4), channel_id=1, source_target_pairs={{0,16},{8,24},{16,0},{24,8},{1,17},{9,25},{17,1},{25,9},{2,18},{10... | collective-permute-start | bytes 786440 | tf_op jit(solution)/shard_map/ppermute | solution.py:32
  65.9 1.2 slice.163
  67.1 0.0 copy-start.1
  67.1 0.5 collective-permute-start.6
  67.6 2.6 %convolution_negate_fusion.1 = f32[256,1536]{1,0:T(8,128)S(1)} fusion(f32[256,256]{1,0:T(8,128)S(1)} %convolution_subtract_fusion.4, f32[256,768]{1,0:T(8,128)S(1)} %slice.109, f32[256,768]{1,0:T(8,128)} %slice.106), kind=kOutput, calls=%fused_computation.10 | convolution fusion | flops 1208745984 | bytes 3407872 | tf_op jit(solution)/shard_map/dot_general | solution.py:11
  70.2 2.9 %convolution_add_fusion = f32[512,1536]{1,0:T(8,128)S(1)} fusion(f32[256,1536]{1,0:T(8,128)S(1)} %convolution_negate_fusion.1, f32[512,768]{1,0:T(8,128)S(1)} %copy-done.1, f32[512,1024]{1,0:T(8,128)S(1)} %bitcast.65), kind=kOutput, calls=%fused_computation.7 | convolution fusion | flops 2416705536 | bytes 6815744 | tf_op jit(solution)/shard_map/dot_general | solution.py:11
  73.1 1.3 slice.161
  74.4 0.1 copy-done.3
  74.5 1.5 %convolution_add_fusion.1 = f32[256,1536]{1,0:T(8,128)S(1)} fusion(f32[256,1536]{1,0:T(8,128)S(1)} %convolution_negate_fusion.1, f32[256,768]{1,0:T(8,128)S(1)} %copy-done.3, f32[256,1024]{1,0:T(8,128)S(1)} %bitcast.63), kind=kOutput, calls=%fused_computation.8 | convolution fusion | flops 1208352768 | bytes 4194304 | tf_op jit(solution)/shard_map/dot_general | solution.py:11
  76.0 0.1 fusion.77
  76.1 12.7 %collective-permute-done.1 = f32[128,1024]{1,0:T(8,128)S(1)} collective-permute-done((f32[128,1024]{1,0:T(8,128)S(1)}, f32[128,1024]{1,0:T(8,128)S(1)}, u32[]{:S(2)}, u32[]{:S(2)}) %collective-permute-start.1) | collective-permute-done | bytes 524320 | tf_op jit(solution)/shard_map/ppermute | solution.py:32
  88.8 1.3 collective-permute-start.7
  90.1 2.6 %convolution_negate_fusion = f32[256,1536]{1,0:T(8,128)S(1)} fusion(f32[256,256]{1,0:T(8,128)S(1)} %collective-permute-done.4, f32[256,768]{1,0:T(8,128)S(1)} %collective-permute-done.6, f32[256,768]{1,0:T(8,128)} %collective-permute-done.5), kind=kOutput, calls=%fused_computation.9 | convolution fusion | flops 1208745984 | bytes 3407872 | tf_op jit(solution)/shard_map/dot_general | solution.py:11
  92.7 2.4 %pad_add_fusion.1 = f32[256,1536]{1,0:T(8,128)S(1)} fusion(f32[256,768]{1,0:T(8,128)S(1)} %slice.161, f32[256,1536]{1,0:T(8,128)S(1)} %convolution_negate_fusion, f32[256,1024]{1,0:T(8,128)} %collective-permute-done.3), kind=kOutput, calls=%fused_computation.18 | convolution fusion | flops 1208352768 | bytes 4194304 | tf_op jit(solution)/shard_map/dot_general | solution.py:11
  95.1 17.9 %collective-permute-done.2 = f32[128,1024]{1,0:T(8,128)S(1)} collective-permute-done((f32[128,1024]{1,0:T(8,128)S(1)}, f32[128,1024]{1,0:T(8,128)S(1)}, u32[]{:S(2)}, u32[]{:S(2)}) %collective-permute-start.2) | collective-permute-done | bytes 524320 | tf_op jit(solution)/shard_map/ppermute | solution.py:32
  113.1 1.0 collective-permute-start.8
  114.1 0.1 slice.159
  114.2 1.7 %pad_add_fusion.2 = f32[256,1536]{1,0:T(8,128)S(1)} fusion(f32[256,768]{1,0:T(8,128)S(1)} %slice.159, f32[256,1536]{1,0:T(8,128)S(1)} %convolution_negate_fusion.1, f32[256,1024]{1,0:T(8,128)S(1)} %constant_dynamic-update-slice_fusion), kind=kOutput, calls=%fused_computation.19 | convolution fusion | flops 1208352768 | bytes 4194304 | tf_op jit(solution)/shard_map/dot_general | solution.py:11
  116.0 10.8 %collective-permute-done.8 = f32[128,1024]{1,0:T(8,128)S(1)} collective-permute-done((f32[128,1024]{1,0:T(8,128)S(1)}, f32[128,1024]{1,0:T(8,128)S(1)}, u32[]{:S(2)}, u32[]{:S(2)}) %collective-permute-start.8) | collective-permute-done | bytes 524320 | tf_op jit(solution)/shard_map/ppermute | solution.py:32
  126.8 0.1 slice.164
  126.8 1.5 %pad_add_fusion = f32[256,1536]{1,0:T(8,128)S(1)} fusion(f32[256,768]{1,0:T(8,128)S(1)} %slice.164, f32[256,1536]{1,0:T(8,128)S(1)} %convolution_negate_fusion, f32[256,1024]{1,0:T(8,128)S(1)} %constant_dynamic-update-slice_fusion.2), kind=kOutput, calls=%fused_computation.17 | convolution fusion | flops 1208352768 | bytes 4194304 | tf_op jit(solution)/shard_map/dot_general | solution.py:11
  128.3 0.2 select_reduce_fusion
  128.5 1.1 fusion.29
  129.6 1.3 convolution_subtract_fusion.3
  130.9 1.0 fusion.81
  132.0 1.0 convolution_subtract_fusion.2
  133.0 1.0 fusion.25
  134.0 0.5 broadcast_in_dim.45
  134.6 1.1 fusion.13
  135.6 1.1 fusion.11
  136.7 1.0 fusion.9
  137.8 0.0 copy-start.2
  137.8 2.0 %copy-done.2 = f32[1,1,512,2048]{3,2,1,0:T(8,128)} copy-done((f32[1,1,512,2048]{3,2,1,0:T(8,128)}, f32[1,1,512,2048]{3,2,1,0:T(8,128)S(1)}, u32[]{:S(2)}) %copy-start.2) | copy-done | bytes 4194328
  139.8 2.0 %fusion.7 = f32[1,1,512,2048]{3,2,1,0:T(8,128)} fusion(f32[1,1,512,2048]{3,2,1,0:T(8,128)} %copy-done.2, s32[]{:T(128)S(6)} %select_n.35, f32[512,512]{1,0:T(8,128)S(1)} %fusion.25, f32[256,1536]{1,0:T(8,128)S(1)} %pad_add_fusion, f32[256,1536]{1,0:T(8,128)S(1)} %pad_add_fusion.1), kind=kOutput, calls=%fused_computation.22 | convolution fusion | flops 805830656 | bytes 5242884 | tf_op jit(solution)/shard_map/dot_general | solution.py:15
  (22 shorter events, 0.2 us)
Async XLA Ops:
  0.0 0.7 copy-start
  10.2 50.0 %collective-permute-start = (f32[256,1024]{1,0:T(8,128)}, f32[256,1024]{1,0:T(8,128)}, u32[]{:S(2)}, u32[]{:S(2)}) collective-permute-start(f32[256,1024]{1,0:T(8,128)} %bitcast.7), channel_id=1, source_target_pairs={{0,4},{1,5},{2,6},{3,7},{4,0},{5,1},{6,2},{7,3},{8,12},{9,13},{10,... | collective-permute-start | bytes 3145736 | tf_op jit(solution)/shard_map/ppermute | solution.py:32
  16.3 73.7 %collective-permute-start.5 = (f32[256,768]{1,0:T(8,128)}, f32[256,768]{1,0:T(8,128)}, u32[]{:S(2)}, u32[]{:S(2)}) collective-permute-start(f32[256,768]{1,0:T(8,128)} %slice.106), channel_id=1, source_target_pairs={{0,16},{8,24},{16,0},{24,8},{1,17},{9,25},{17,1},{25,9},{2,18},{10... | collective-permute-start | bytes 2359304 | tf_op jit(solution)/shard_map/ppermute | solution.py:32
  25.8 47.3 %collective-permute-start.3 = (f32[256,1024]{1,0:T(8,128)S(1)}, f32[256,1024]{1,0:T(8,128)}, u32[]{:S(2)}, u32[]{:S(2)}) collective-permute-start(f32[256,1024]{1,0:T(8,128)S(1)} %bitcast.60), channel_id=1, source_target_pairs={{0,16},{8,24},{16,0},{24,8},{1,17},{9,25},{17,1},{25,9},{2,18},{10... | collective-permute-start | bytes 3145736 | tf_op jit(solution)/shard_map/ppermute | solution.py:32
  63.4 25.3 %collective-permute-start.1 = (f32[128,1024]{1,0:T(8,128)S(1)}, f32[128,1024]{1,0:T(8,128)S(1)}, u32[]{:S(2)}, u32[]{:S(2)}) collective-permute-start(f32[128,1024]{1,0:T(8,128)S(1)} %get-tuple-element.14), channel_id=1, source_target_pairs={{0,4},{1,5},{2,6},{3,7},{4,0},{5,1},{6,2},{7,3},{8,12},{9,13},{10,... | collective-permute-start | bytes 1572872 | tf_op jit(solution)/shard_map/ppermute | solution.py:32
  64.3 25.8 %collective-permute-start.4 = (f32[256,256]{1,0:T(8,128)S(1)}, f32[256,256]{1,0:T(8,128)S(1)}, u32[]{:S(2)}, u32[]{:S(2)}) collective-permute-start(f32[256,256]{1,0:T(8,128)S(1)} %convolution_subtract_fusion.4), channel_id=1, source_target_pairs={{0,16},{8,24},{16,0},{24,8},{1,17},{9,25},{17,1},{25,9},{2,18},{10... | collective-permute-start | bytes 786440 | tf_op jit(solution)/shard_map/ppermute | solution.py:32
  67.1 3.1 %copy-start.1 = (f32[512,768]{1,0:T(8,128)S(1)}, f32[512,768]{1,0:T(8,128)}, u32[]{:S(2)}) copy-start(f32[512,768]{1,0:T(8,128)} %slice.148) | copy-start | bytes 4718596
  67.1 23.0 %collective-permute-start.6 = (f32[256,768]{1,0:T(8,128)S(1)}, f32[256,768]{1,0:T(8,128)S(1)}, u32[]{:S(2)}, u32[]{:S(2)}) collective-permute-start(f32[256,768]{1,0:T(8,128)S(1)} %slice.163), channel_id=1, source_target_pairs={{0,16},{8,24},{16,0},{24,8},{1,17},{9,25},{17,1},{25,9},{2,18},{10... | collective-permute-start | bytes 2359304 | tf_op jit(solution)/shard_map/ppermute | solution.py:32
  73.1 1.4 copy-start.3
  88.7 24.3 %collective-permute-start.2 = (f32[128,1024]{1,0:T(8,128)S(1)}, f32[128,1024]{1,0:T(8,128)S(1)}, u32[]{:S(2)}, u32[]{:S(2)}) collective-permute-start(f32[128,1024]{1,0:T(8,128)S(1)} %get-tuple-element.16), channel_id=1, source_target_pairs={{0,4},{1,5},{2,6},{3,7},{4,0},{5,1},{6,2},{7,3},{8,12},{9,13},{10,... | collective-permute-start | bytes 1572872 | tf_op jit(solution)/shard_map/ppermute | solution.py:32
  88.8 25.4 %collective-permute-start.7 = (f32[128,1024]{1,0:T(8,128)S(1)}, f32[128,1024]{1,0:T(8,128)S(1)}, u32[]{:S(2)}, u32[]{:S(2)}) collective-permute-start(f32[128,1024]{1,0:T(8,128)S(1)} %collective-permute-done.1), channel_id=1, source_target_pairs={{0,16},{8,24},{16,0},{24,8},{1,17},{9,25},{17,1},{25,9},{2,18},{10... | collective-permute-start | bytes 1572872 | tf_op jit(solution)/shard_map/ppermute | solution.py:32
  113.1 13.6 %collective-permute-start.8 = (f32[128,1024]{1,0:T(8,128)S(1)}, f32[128,1024]{1,0:T(8,128)S(1)}, u32[]{:S(2)}, u32[]{:S(2)}) collective-permute-start(f32[128,1024]{1,0:T(8,128)S(1)} %collective-permute-done.2), channel_id=1, source_target_pairs={{0,16},{8,24},{16,0},{24,8},{1,17},{9,25},{17,1},{25,9},{2,18},{10... | collective-permute-start | bytes 1572872 | tf_op jit(solution)/shard_map/ppermute | solution.py:32
  137.8 2.0 %copy-start.2 = (f32[1,1,512,2048]{3,2,1,0:T(8,128)}, f32[1,1,512,2048]{3,2,1,0:T(8,128)S(1)}, u32[]{:S(2)}) copy-start(f32[1,1,512,2048]{3,2,1,0:T(8,128)S(1)} %fusion.9) | copy-start | bytes 12582916

commit v3 on v2

--- a/solution.py
+++ b/solution.py
@@ -76,21 +76,24 @@
     own_i2 = pick(leaf, perm[3 * width :], perm)
     own_ov = pick(leaf, perm[width : 3 * width], perm)
 
-    half = width // 2
     vert_ie = swap(own_i1[:, width:], "grp")
     vert_i2 = swap(own_i2, "grp")
     side_i1 = swap(own_i1, "box")
     diag_ie = swap(side_i1[:, width:], "grp")
     inverse_own = newton(own_i1[:, :width] + side_i1[:, :width], ITERS_LOW)
     inverse_other = swap(inverse_own, "grp")
-    first_half, side_i1 = lax.optimization_barrier((own_i2[:half], side_i1))
-    side_first = swap(first_half, "box")
-    diag_first = swap(side_first, "grp")
-    second_half, side_first = lax.optimization_barrier((own_i2[half:], side_first))
-    side_second = swap(second_half, "box")
-    diag_second = swap(side_second, "grp")
-    side_i2 = jnp.concatenate([side_first, side_second], 0)
-    diag_i2 = jnp.concatenate([diag_first, diag_second], 0)
+    bounds = [0, width // 2, 3 * width // 4, width]
+    side_parts = []
+    diag_parts = []
+    after = side_i1
+    for lo, hi in zip(bounds[:-1], bounds[1:]):
+        part, after = lax.optimization_barrier((own_i2[lo:hi], after))
+        landed = swap(part, "box")
+        side_parts.append(landed)
+        diag_parts.append(swap(landed, "grp"))
+        after = landed
+    side_i2 = jnp.concatenate(side_parts, 0)
+    diag_i2 = jnp.concatenate(diag_parts, 0)
 
     solved_own = pair_solve(inverse_own, own_i1[:, width:], side_i1[:, width:])
     own_ext = first_rows(own_ov, solved_own, width)

time: 142 us -> 144 us (1.014)
    ppermute x9 -> x11, starting transfers between devices: 10.6 us -> 11.8 us  [swap(): return lax.ppermute(value, axis, pairs)]
    ppermute x9 -> x11, waiting for transfers between devices: 58.2 us -> 59.2 us  [swap(): return lax.ppermute(value, axis, pairs)]
  transfers between devices with their start and end apart: 9 -> 11, of which waited for: 4 -> 5; matrix products, arithmetic and copies ran while one was open for 33% -> 33% of each run, Pallas kernels for 0% -> 0%
where the time goes in v3:
time: 144 us
  waiting for transfers between devices  59.2 us (41%)
  local copies, waits for them, and re-layouts  43.1 us (30%)
  matrix products  27.6 us (19%)
  starting transfers between devices  11.8 us (8%)
  other arithmetic  1.46 us (1%)
    ppermute x11, waiting for transfers between devices, swap(): return lax.ppermute(value, axis, pairs)  59.2 us
    dot_general x11, matrix products, matmul(): jnp.dot(left, right, precision=lax.Precision.HIGHEST, preferred_element_t...  16.9 us
    gather x6, local copies, waits for them, and re-layouts, pick(): picked = jnp.take(matrix, rows, axis=0, mode='clip')  15.9 us
    gather x6, local copies, waits for them, and re-layouts, pick(): return jnp.take(picked, cols, axis=1, mode='clip')  15.6 us
    ppermute x11, starting transfers between devices, swap(): return lax.ppermute(value, axis, pairs)  11.8 us
    dot_general x9, matrix products, matmul_high(): jnp.dot(left, right, precision=lax.Precision.HIGH, preferred_element_type...  10.7 us
    slice x3, local copies, waits for them, and re-layouts, first_rows(): rows[:, width:]  3.41 us
    slice x2, local copies, waits for them, and re-layouts, body(): solved_own = pair_solve(inverse_own, own_i1[:, width:], side_i1[:, width:])  3.3 us
  transfers between devices with their start and end apart: 11, of which 5 were waited for; matrix products, arithmetic and copies ran while one was open for 33% of the time, Pallas kernels for 0%

profile of v3, /device:TPU:0, one launch (start us, length us, event | category | flops | bytes accessed | tf_op | source)
XLA Modules:
  0.0 143.6 jit_solution(7315233644818227961)
XLA Ops:
  0.0 0.1 pad_add_fusion.3
  0.1 0.6 copy-done
  0.7 0.6 gather_fusion
  1.3 3.8 %gather_fusion.1 = f32[256,1024]{1,0:T(8,128)S(1)} fusion(f32[1024,1024]{1,0:T(8,128)} %bitcast.57, s32[1024]{0:T(1024)S(1)} %get-tuple-element.27), kind=kCustom, calls=%fused_computation.1 | custom fusion | bytes 2098176 | tf_op jit(solution)/shard_map/jit(_take)/gather | solution.py:62
  5.1 0.3 copy.3
  5.4 3.5 %gather_fusion.2 = f32[1024,256]{1,0:T(8,128)S(1)} fusion(f32[256,1024]{0,1:T(8,128)S(1)} %copy.3, s32[1024]{0:T(1024)S(1)} %get-tuple-element.28), kind=kCustom, calls=%fused_computation.2 | custom fusion | bytes 2101248 | tf_op jit(solution)/shard_map/jit(_take)/gather | solution.py:63
  8.9 1.3 copy.4
  10.2 4.0 %collective-permute-start = (f32[256,1024]{1,0:T(8,128)}, f32[256,1024]{1,0:T(8,128)}, u32[]{:S(2)}, u32[]{:S(2)}) collective-permute-start(f32[256,1024]{1,0:T(8,128)} %bitcast.7), channel_id=1, source_target_pairs={{0,4},{1,5},{2,6},{3,7},{4,0},{5,1},{6,2},{7,3},{8,12},{9,13},{10,... | collective-permute-start | bytes 3145736 | tf_op jit(solution)/shard_map/ppermute | solution.py:32
  14.2 2.1 %slice.107 = f32[256,768]{1,0:T(8,128)} slice(f32[256,1024]{1,0:T(8,128)} %bitcast.7), slice={[0:256], [256:1024]} | slice | bytes 1572864 | tf_op jit(solution)/shard_map/slice | solution.py:98
  16.4 1.5 %collective-permute-start.6 = (f32[256,768]{1,0:T(8,128)}, f32[256,768]{1,0:T(8,128)}, u32[]{:S(2)}, u32[]{:S(2)}) collective-permute-start(f32[256,768]{1,0:T(8,128)} %slice.107), channel_id=1, source_target_pairs={{0,16},{8,24},{16,0},{24,8},{1,17},{9,25},{17,1},{25,9},{2,18},{10... | collective-permute-start | bytes 2359304 | tf_op jit(solution)/shard_map/ppermute | solution.py:32
  17.9 3.8 %gather_fusion.5 = f32[256,1024]{1,0:T(8,128)S(1)} fusion(f32[1024,1024]{1,0:T(8,128)} %bitcast.58, s32[1024]{0:T(1024)S(1)} %get-tuple-element.25), kind=kCustom, calls=%fused_computation.5 | custom fusion | bytes 2098176 | tf_op jit(solution)/shard_map/jit(_take)/gather | solution.py:62
  21.7 0.3 copy.7
  22.0 3.5 %gather_fusion.6 = f32[1024,256]{1,0:T(8,128)S(1)} fusion(f32[256,1024]{0,1:T(8,128)S(1)} %copy.7, s32[1024]{0:T(1024)S(1)} %get-tuple-element.28), kind=kCustom, calls=%fused_computation.6 | custom fusion | bytes 2101248 | tf_op jit(solution)/shard_map/jit(_take)/gather | solution.py:63
  25.5 0.3 copy.8
  25.8 0.6 collective-permute-start.4
  26.4 1.0 slice.157
  27.3 0.8 slice.159
  28.2 5.8 %gather_fusion.3 = f32[512,1024]{1,0:T(8,128)} fusion(f32[1024,1024]{1,0:T(8,128)} %bitcast.59, s32[1024]{0:T(1024)S(1)} %get-tuple-element.26), kind=kCustom, calls=%fused_computation.3 | custom fusion | bytes 4196352 | tf_op jit(solution)/shard_map/jit(_take)/gather | solution.py:62
  34.0 1.9 %copy.5 = f32[512,1024]{0,1:T(8,128)S(1)} copy(f32[512,1024]{1,0:T(8,128)} %gather_fusion.3) | data formatting | bytes 4194304 | tf_op jit(solution)/shard_map/jit(_take)/gather | solution.py:62
  35.9 4.9 %gather_fusion.4 = f32[1024,512]{1,0:T(8,128)} fusion(f32[512,1024]{0,1:T(8,128)S(1)} %copy.5, s32[1024]{0:T(1024)S(1)} %get-tuple-element.28), kind=kCustom, calls=%fused_computation.4 | custom fusion | bytes 4198400 | tf_op jit(solution)/shard_map/jit(_take)/gather | solution.py:63
  40.8 2.1 %copy.6 = f32[1024,512]{0,1:T(8,128)S(1)} copy(f32[1024,512]{1,0:T(8,128)} %gather_fusion.4) | data formatting | bytes 4194304 | tf_op jit(solution)/shard_map/jit(_take)/gather | solution.py:63
  42.9 1.3 slice.149
  44.2 16.0 %collective-permute-done = f32[256,1024]{1,0:T(8,128)} collective-permute-done((f32[256,1024]{1,0:T(8,128)}, f32[256,1024]{1,0:T(8,128)}, u32[]{:S(2)}, u32[]{:S(2)}) %collective-permute-start) | collective-permute-done | bytes 1048608 | tf_op jit(solution)/shard_map/ppermute | solution.py:32
  60.2 1.1 select_reduce_fusion.1
  61.3 0.4 fusion.52
  61.8 0.5 convolution_subtract_fusion.5
  62.3 0.4 fusion.80
  62.6 0.4 convolution_subtract_fusion.4
  63.0 1.6 %collective-permute-start.5 = (f32[256,256]{1,0:T(8,128)S(1)}, f32[256,256]{1,0:T(8,128)S(1)}, u32[]{:S(2)}, u32[]{:S(2)}) collective-permute-start(f32[256,256]{1,0:T(8,128)S(1)} %convolution_subtract_fusion.4), channel_id=1, source_target_pairs={{0,16},{8,24},{16,0},{24,8},{1,17},{9,25},{17,1},{25,9},{2,18},{10... | collective-permute-start | bytes 786440 | tf_op jit(solution)/shard_map/ppermute | solution.py:32
  64.7 1.2 slice.152
  65.9 0.0 copy-start.1
  65.9 2.7 %convolution_negate_fusion.1 = f32[256,1536]{1,0:T(8,128)S(1)} fusion(f32[256,256]{1,0:T(8,128)S(1)} %convolution_subtract_fusion.4, f32[256,768]{1,0:T(8,128)S(1)} %slice.152, f32[256,768]{1,0:T(8,128)} %slice.107), kind=kOutput, calls=%fused_computation.10 | convolution fusion | flops 1208745984 | bytes 3407872 | tf_op jit(solution)/shard_map/dot_general | solution.py:11
  68.6 0.5 collective-permute-start.7
  69.1 0.0 collective-permute-start.1
  69.1 2.9 %convolution_add_fusion = f32[512,1536]{1,0:T(8,128)S(1)} fusion(f32[256,1536]{1,0:T(8,128)S(1)} %convolution_negate_fusion.1, f32[512,768]{1,0:T(8,128)S(1)} %copy-done.1, f32[512,1024]{1,0:T(8,128)S(1)} %bitcast.66), kind=kOutput, calls=%fused_computation.7 | convolution fusion | flops 2416705536 | bytes 6815744 | tf_op jit(solution)/shard_map/dot_general | solution.py:11
  72.0 1.5 %convolution_add_fusion.1 = f32[256,1536]{1,0:T(8,128)S(1)} fusion(f32[256,1536]{1,0:T(8,128)S(1)} %convolution_negate_fusion.1, f32[256,768]{1,0:T(8,128)S(1)} %copy-done.3, f32[256,1024]{1,0:T(8,128)S(1)} %bitcast.64), kind=kOutput, calls=%fused_computation.8 | convolution fusion | flops 1208352768 | bytes 4194304 | tf_op jit(solution)/shard_map/dot_general | solution.py:11
  73.5 20.3 %collective-permute-done.1 = f32[128,1024]{1,0:T(8,128)S(1)} collective-permute-done((f32[128,1024]{1,0:T(8,128)S(1)}, f32[128,1024]{1,0:T(8,128)S(1)}, u32[]{:S(2)}, u32[]{:S(2)}) %collective-permute-start.1) | collective-permute-done | bytes 524320 | tf_op jit(solution)/shard_map/ppermute | solution.py:32
  93.8 0.1 fusion.77
  93.9 1.2 slice.164
  95.1 1.3 collective-permute-start.8
  96.5 10.4 %collective-permute-done.2 = f32[64,1024]{1,0:T(8,128)S(1)} collective-permute-done((f32[64,1024]{1,0:T(8,128)S(1)}, f32[64,1024]{1,0:T(8,128)S(1)}, u32[]{:S(2)}, u32[]{:S(2)}) %collective-permute-start.2) | collective-permute-done | bytes 262176 | tf_op jit(solution)/shard_map/ppermute | solution.py:32
  106.9 1.1 collective-permute-start.9
  108.0 2.6 %convolution_negate_fusion = f32[256,1536]{1,0:T(8,128)S(1)} fusion(f32[256,256]{1,0:T(8,128)S(1)} %collective-permute-done.5, f32[256,768]{1,0:T(8,128)S(1)} %collective-permute-done.7, f32[256,768]{1,0:T(8,128)} %collective-permute-done.6), kind=kOutput, calls=%fused_computation.9 | convolution fusion | flops 1208745984 | bytes 3407872 | tf_op jit(solution)/shard_map/dot_general | solution.py:11
  110.6 2.4 %pad_add_fusion.1 = f32[256,1536]{1,0:T(8,128)S(1)} fusion(f32[256,768]{1,0:T(8,128)S(1)} %slice.164, f32[256,1536]{1,0:T(8,128)S(1)} %convolution_negate_fusion, f32[256,1024]{1,0:T(8,128)} %collective-permute-done.4), kind=kOutput, calls=%fused_computation.18 | convolution fusion | flops 1208352768 | bytes 4194304 | tf_op jit(solution)/shard_map/dot_general | solution.py:11
  113.0 7.1 %collective-permute-done.3 = f32[64,1024]{1,0:T(8,128)S(1)} collective-permute-done((f32[64,1024]{1,0:T(8,128)S(1)}, f32[64,1024]{1,0:T(8,128)S(1)}, u32[]{:S(2)}, u32[]{:S(2)}) %collective-permute-start.3) | collective-permute-done | bytes 262176 | tf_op jit(solution)/shard_map/ppermute | solution.py:32
  120.2 0.1 slice.162
  120.2 1.1 collective-permute-start.10
  121.3 1.7 %pad_add_fusion.2 = f32[256,1536]{1,0:T(8,128)S(1)} fusion(f32[256,768]{1,0:T(8,128)S(1)} %slice.162, f32[256,1536]{1,0:T(8,128)S(1)} %convolution_negate_fusion.1, f32[256,1024]{1,0:T(8,128)S(1)} %constant_dynamic-update-slice_fusion), kind=kOutput, calls=%fused_computation.19 | convolution fusion | flops 1208352768 | bytes 4194304 | tf_op jit(solution)/shard_map/dot_general | solution.py:11
  123.1 5.4 %collective-permute-done.10 = f32[64,1024]{1,0:T(8,128)S(1)} collective-permute-done((f32[64,1024]{1,0:T(8,128)S(1)}, f32[64,1024]{1,0:T(8,128)S(1)}, u32[]{:S(2)}, u32[]{:S(2)}) %collective-permute-start.10) | collective-permute-done | bytes 262176 | tf_op jit(solution)/shard_map/ppermute | solution.py:32
  128.5 0.1 slice.166
  128.6 1.5 %pad_add_fusion = f32[256,1536]{1,0:T(8,128)S(1)} fusion(f32[256,768]{1,0:T(8,128)S(1)} %slice.166, f32[256,1536]{1,0:T(8,128)S(1)} %convolution_negate_fusion, f32[256,1024]{1,0:T(8,128)S(1)} %constant_dynamic-update-slice_fusion.3), kind=kOutput, calls=%fused_computation.17 | convolution fusion | flops 1208352768 | bytes 4194304 | tf_op jit(solution)/shard_map/dot_general | solution.py:11
  130.1 0.2 select_reduce_fusion
  130.3 1.1 fusion.29
  131.4 1.3 convolution_subtract_fusion.3
  132.7 1.0 fusion.81
  133.7 1.0 convolution_subtract_fusion.2
  134.8 1.0 fusion.25
  135.8 0.5 broadcast_in_dim.45
  136.3 1.1 fusion.13
  137.4 1.1 fusion.11
  138.5 1.0 fusion.9
  139.5 0.0 copy-start.2
  139.6 2.0 %copy-done.2 = f32[1,1,512,2048]{3,2,1,0:T(8,128)} copy-done((f32[1,1,512,2048]{3,2,1,0:T(8,128)}, f32[1,1,512,2048]{3,2,1,0:T(8,128)S(1)}, u32[]{:S(2)}) %copy-start.2) | copy-done | bytes 4194328
  141.6 2.0 %fusion.7 = f32[1,1,512,2048]{3,2,1,0:T(8,128)} fusion(f32[1,1,512,2048]{3,2,1,0:T(8,128)} %copy-done.2, s32[]{:T(128)S(6)} %select_n.35, f32[512,512]{1,0:T(8,128)S(1)} %fusion.25, f32[256,1536]{1,0:T(8,128)S(1)} %pad_add_fusion, f32[256,1536]{1,0:T(8,128)S(1)} %pad_add_fusion.1), kind=kOutput, calls=%fused_computation.22 | convolution fusion | flops 805830656 | bytes 5242884 | tf_op jit(solution)/shard_map/dot_general | solution.py:15
  (30 shorter events, 0.3 us)
Async XLA Ops:
  0.0 0.7 copy-start
  10.2 50.0 %collective-permute-start = (f32[256,1024]{1,0:T(8,128)}, f32[256,1024]{1,0:T(8,128)}, u32[]{:S(2)}, u32[]{:S(2)}) collective-permute-start(f32[256,1024]{1,0:T(8,128)} %bitcast.7), channel_id=1, source_target_pairs={{0,4},{1,5},{2,6},{3,7},{4,0},{5,1},{6,2},{7,3},{8,12},{9,13},{10,... | collective-permute-start | bytes 3145736 | tf_op jit(solution)/shard_map/ppermute | solution.py:32
  16.4 90.5 %collective-permute-start.6 = (f32[256,768]{1,0:T(8,128)}, f32[256,768]{1,0:T(8,128)}, u32[]{:S(2)}, u32[]{:S(2)}) collective-permute-start(f32[256,768]{1,0:T(8,128)} %slice.107), channel_id=1, source_target_pairs={{0,16},{8,24},{16,0},{24,8},{1,17},{9,25},{17,1},{25,9},{2,18},{10... | collective-permute-start | bytes 2359304 | tf_op jit(solution)/shard_map/ppermute | solution.py:32
  25.8 68.1 %collective-permute-start.4 = (f32[256,1024]{1,0:T(8,128)S(1)}, f32[256,1024]{1,0:T(8,128)}, u32[]{:S(2)}, u32[]{:S(2)}) collective-permute-start(f32[256,1024]{1,0:T(8,128)S(1)} %bitcast.60), channel_id=1, source_target_pairs={{0,16},{8,24},{16,0},{24,8},{1,17},{9,25},{17,1},{25,9},{2,18},{10... | collective-permute-start | bytes 3145736 | tf_op jit(solution)/shard_map/ppermute | solution.py:32
  63.0 45.0 %collective-permute-start.5 = (f32[256,256]{1,0:T(8,128)S(1)}, f32[256,256]{1,0:T(8,128)S(1)}, u32[]{:S(2)}, u32[]{:S(2)}) collective-permute-start(f32[256,256]{1,0:T(8,128)S(1)} %convolution_subtract_fusion.4), channel_id=1, source_target_pairs={{0,16},{8,24},{16,0},{24,8},{1,17},{9,25},{17,1},{25,9},{2,18},{10... | collective-permute-start | bytes 786440 | tf_op jit(solution)/shard_map/ppermute | solution.py:32
  65.9 3.3 %copy-start.4 = (f32[128,1024]{1,0:T(8,128)S(1)}, f32[128,1024]{1,0:T(8,128)}, u32[]{:S(2)}) copy-start(f32[128,1024]{1,0:T(8,128)} %slice.159) | copy-start | bytes 1572868
  65.9 3.3 %copy-start.1 = (f32[512,768]{1,0:T(8,128)S(1)}, f32[512,768]{1,0:T(8,128)}, u32[]{:S(2)}) copy-start(f32[512,768]{1,0:T(8,128)} %slice.149) | copy-start | bytes 4718596
  68.6 3.4 %copy-start.3 = (f32[256,768]{1,0:T(8,128)S(1)}, f32[256,768]{1,0:T(8,128)}, u32[]{:S(2)}) copy-start(f32[256,768]{1,0:T(8,128)} %slice.157) | copy-start | bytes 2359300
  68.6 39.4 %collective-permute-start.7 = (f32[256,768]{1,0:T(8,128)S(1)}, f32[256,768]{1,0:T(8,128)S(1)}, u32[]{:S(2)}, u32[]{:S(2)}) collective-permute-start(f32[256,768]{1,0:T(8,128)S(1)} %slice.152), channel_id=1, source_target_pairs={{0,16},{8,24},{16,0},{24,8},{1,17},{9,25},{17,1},{25,9},{2,18},{10... | collective-permute-start | bytes 2359304 | tf_op jit(solution)/shard_map/ppermute | solution.py:32
  69.1 24.7 %collective-permute-start.1 = (f32[128,1024]{1,0:T(8,128)S(1)}, f32[128,1024]{1,0:T(8,128)S(1)}, u32[]{:S(2)}, u32[]{:S(2)}) collective-permute-start(f32[128,1024]{1,0:T(8,128)S(1)} %copy-done.4), channel_id=1, source_target_pairs={{0,4},{1,5},{2,6},{3,7},{4,0},{5,1},{6,2},{7,3},{8,12},{9,13},{10,... | collective-permute-start | bytes 1572872 | tf_op jit(solution)/shard_map/ppermute | solution.py:32
  93.8 13.0 %collective-permute-start.2 = (f32[64,1024]{1,0:T(8,128)S(1)}, f32[64,1024]{1,0:T(8,128)S(1)}, u32[]{:S(2)}, u32[]{:S(2)}) collective-permute-start(f32[64,1024]{1,0:T(8,128)S(1)} %get-tuple-element.13), channel_id=1, source_target_pairs={{0,4},{1,5},{2,6},{3,7},{4,0},{5,1},{6,2},{7,3},{8,12},{9,13},{10,... | collective-permute-start | bytes 786440 | tf_op jit(solution)/shard_map/ppermute | solution.py:32
  95.1 28.0 %collective-permute-start.8 = (f32[128,1024]{1,0:T(8,128)S(1)}, f32[128,1024]{1,0:T(8,128)S(1)}, u32[]{:S(2)}, u32[]{:S(2)}) collective-permute-start(f32[128,1024]{1,0:T(8,128)S(1)} %collective-permute-done.1), channel_id=1, source_target_pairs={{0,16},{8,24},{16,0},{24,8},{1,17},{9,25},{17,1},{25,9},{2,18},{10... | collective-permute-start | bytes 1572872 | tf_op jit(solution)/shard_map/ppermute | solution.py:32
  106.9 13.3 %collective-permute-start.3 = (f32[64,1024]{1,0:T(8,128)S(1)}, f32[64,1024]{1,0:T(8,128)S(1)}, u32[]{:S(2)}, u32[]{:S(2)}) collective-permute-start(f32[64,1024]{1,0:T(8,128)S(1)} %get-tuple-element.14), channel_id=1, source_target_pairs={{0,4},{1,5},{2,6},{3,7},{4,0},{5,1},{6,2},{7,3},{8,12},{9,13},{10,... | collective-permute-start | bytes 786440 | tf_op jit(solution)/shard_map/ppermute | solution.py:32
  106.9 16.2 %collective-permute-start.9 = (f32[64,1024]{1,0:T(8,128)S(1)}, f32[64,1024]{1,0:T(8,128)S(1)}, u32[]{:S(2)}, u32[]{:S(2)}) collective-permute-start(f32[64,1024]{1,0:T(8,128)S(1)} %collective-permute-done.2), channel_id=1, source_target_pairs={{0,16},{8,24},{16,0},{24,8},{1,17},{9,25},{17,1},{25,9},{2,18},{10... | collective-permute-start | bytes 786440 | tf_op jit(solution)/shard_map/ppermute | solution.py:32
  120.2 8.3 %collective-permute-start.10 = (f32[64,1024]{1,0:T(8,128)S(1)}, f32[64,1024]{1,0:T(8,128)S(1)}, u32[]{:S(2)}, u32[]{:S(2)}) collective-permute-start(f32[64,1024]{1,0:T(8,128)S(1)} %collective-permute-done.3), channel_id=1, source_target_pairs={{0,16},{8,24},{16,0},{24,8},{1,17},{9,25},{17,1},{25,9},{2,18},{10... | collective-permute-start | bytes 786440 | tf_op jit(solution)/shard_map/ppermute | solution.py:32
  139.5 2.0 %copy-start.2 = (f32[1,1,512,2048]{3,2,1,0:T(8,128)}, f32[1,1,512,2048]{3,2,1,0:T(8,128)S(1)}, u32[]{:S(2)}) copy-start(f32[1,1,512,2048]{3,2,1,0:T(8,128)S(1)} %fusion.9) | copy-start | bytes 12582916

commit v4 on v2

--- a/solution.py
+++ b/solution.py
@@ -71,19 +71,22 @@
     width = side_lists.shape[1]
     order = jnp.stack([1 - right, right, 2 + upper, 3 - upper])
     perm = jnp.take(side_lists, order, axis=0, mode="clip").reshape(4 * width)
-    own_i1 = pick(leaf, perm[:width], perm)
-    leaf, own_i1 = lax.optimization_barrier((leaf, own_i1))
+    rows_i1 = jnp.take(leaf, perm[:width], axis=0, mode="clip")
+    own_ii = jnp.take(rows_i1, perm[:width], axis=1, mode="clip")
+    own_ie = jnp.take(rows_i1, perm[width:], axis=1, mode="clip")
+    leaf, own_ii, own_ie = lax.optimization_barrier((leaf, own_ii, own_ie))
     own_i2 = pick(leaf, perm[3 * width :], perm)
     own_ov = pick(leaf, perm[width : 3 * width], perm)
 
     half = width // 2
-    vert_ie = swap(own_i1[:, width:], "grp")
+    vert_ie = swap(own_ie, "grp")
     vert_i2 = swap(own_i2, "grp")
-    side_i1 = swap(own_i1, "box")
-    diag_ie = swap(side_i1[:, width:], "grp")
-    inverse_own = newton(own_i1[:, :width] + side_i1[:, :width], ITERS_LOW)
+    side_ii = swap(own_ii, "box")
+    side_ie = swap(own_ie, "box")
+    diag_ie = swap(side_ie, "grp")
+    inverse_own = newton(own_ii + side_ii, ITERS_LOW)
     inverse_other = swap(inverse_own, "grp")
-    first_half, side_i1 = lax.optimization_barrier((own_i2[:half], side_i1))
+    first_half, side_ie = lax.optimization_barrier((own_i2[:half], side_ie))
     side_first = swap(first_half, "box")
     diag_first = swap(side_first, "grp")
     second_half, side_first = lax.optimization_barrier((own_i2[half:], side_first))
@@ -92,7 +95,7 @@
     side_i2 = jnp.concatenate([side_first, side_second], 0)
     diag_i2 = jnp.concatenate([diag_first, diag_second], 0)
 
-    solved_own = pair_solve(inverse_own, own_i1[:, width:], side_i1[:, width:])
+    solved_own = pair_solve(inverse_own, own_ie, side_ie)
     own_ext = first_rows(own_ov, solved_own, width)
     own_int = first_rows(own_i2, solved_own, width)
     side_int = second_rows(side_i2, solved_own, width)

time: 142 us -> 144 us (1.014)
  waiting for transfers between devices: 58.2 us -> 65.9 us
  local copies, waits for them, and re-layouts: 43.6 us -> 38.2 us
    gather x0 -> x5, local copies, waits for them, and re-layouts: none -> 8.13 us  [the longest x2 4.09 us: body(): rows_i1 = jnp.take(leaf, perm[:width], axis=0, mode='clip')]
    ppermute x9 -> x10, waiting for transfers between devices: 58.2 us -> 65.9 us  [swap(): return lax.ppermute(value, axis, pairs)]
    gather x6 -> x4, local copies, waits for them, and re-layouts: 15.6 us -> 10.8 us  [pick(): return jnp.take(picked, cols, axis=1, mode='clip')]
    slice x3 -> x1, local copies, waits for them, and re-layouts: 4.48 us -> 0.01 us  [body(): own_ie = jnp.take(rows_i1, perm[width:], axis=1, mode='clip')]
    gather x6 -> x4, local copies, waits for them, and re-layouts: 15.9 us -> 11.8 us  [pick(): picked = jnp.take(matrix, rows, axis=0, mode='clip')]
    ppermute x9 -> x10, starting transfers between devices: 10.6 us -> 10.3 us  [swap(): return lax.ppermute(value, axis, pairs)]
  transfers between devices with their start and end apart: 9 -> 10, of which waited for: 4 -> 4; matrix products, arithmetic and copies ran while one was open for 33% -> 30% of each run, Pallas kernels for 0% -> 0%
where the time goes in v4:
time: 144 us
  waiting for transfers between devices  65.9 us (46%)
  local copies, waits for them, and re-layouts  38.2 us (27%)
  matrix products  27.9 us (19%)
  starting transfers between devices  10.3 us (7%)
    ppermute x10, waiting for transfers between devices, swap(): return lax.ppermute(value, axis, pairs)  65.9 us
    dot_general x11, matrix products, matmul(): jnp.dot(left, right, precision=lax.Precision.HIGHEST, preferred_element_t...  17.2 us
    gather x4, local copies, waits for them, and re-layouts, pick(): picked = jnp.take(matrix, rows, axis=0, mode='clip')  11.8 us
    gather x4, local copies, waits for them, and re-layouts, pick(): return jnp.take(picked, cols, axis=1, mode='clip')  10.8 us
    dot_general x9, matrix products, matmul_high(): jnp.dot(left, right, precision=lax.Precision.HIGH, preferred_element_type...  10.7 us
    ppermute x10, starting transfers between devices, swap(): return lax.ppermute(value, axis, pairs)  10.3 us
    gather x2, local copies, waits for them, and re-layouts, body(): rows_i1 = jnp.take(leaf, perm[:width], axis=0, mode='clip')  4.09 us
    slice x3, local copies, waits for them, and re-layouts, first_rows(): rows[:, width:]  3.4 us
  transfers between devices with their start and end apart: 10, of which 4 were waited for; matrix products, arithmetic and copies ran while one was open for 30% of the time, Pallas kernels for 0%

profile of v4, /device:TPU:0, one launch (start us, length us, event | category | flops | bytes accessed | tf_op | source)
XLA Modules:
  0.0 144.0 jit_solution(8610083725039238875)
XLA Ops:
  0.0 0.1 pad_add_fusion.3
  0.1 0.6 copy-done
  0.7 0.6 gather_fusion
  1.3 3.8 %gather_fusion.1 = f32[256,1024]{1,0:T(8,128)S(1)} fusion(f32[1024,1024]{1,0:T(8,128)} %bitcast.58, s32[1024]{0:T(1024)S(1)} %get-tuple-element.32), kind=kCustom, calls=%fused_computation.1 | custom fusion | bytes 2098176 | tf_op jit(solution)/shard_map/jit(_take)/gather | solution.py:74
  5.1 0.3 copy.3
  5.4 1.0 gather_fusion.2
  6.4 2.9 %gather_fusion.3 = f32[768,256]{1,0:T(8,128)} fusion(f32[256,1024]{0,1:T(8,128)S(1)} %copy.3, s32[1024]{0:T(1024)S(1)} %get-tuple-element.31), kind=kCustom, calls=%fused_computation.3 | custom fusion | bytes 1575936 | tf_op jit(solution)/shard_map/jit(_take)/gather | solution.py:76
  9.3 0.1 copy.4
  9.5 4.1 %collective-permute-start.1 = (f32[256,768]{0,1:T(8,128)}, f32[256,768]{0,1:T(8,128)}, u32[]{:S(2)}, u32[]{:S(2)}) collective-permute-start(f32[256,768]{0,1:T(8,128)} %bitcast.8), channel_id=1, source_target_pairs={{0,4},{1,5},{2,6},{3,7},{4,0},{5,1},{6,2},{7,3},{8,12},{9,13},{10,... | collective-permute-start | bytes 2359304 | tf_op jit(solution)/shard_map/ppermute | solution.py:32
  13.6 1.5 %collective-permute-start.6 = (f32[256,768]{0,1:T(8,128)}, f32[256,768]{0,1:T(8,128)}, u32[]{:S(2)}, u32[]{:S(2)}) collective-permute-start(f32[256,768]{0,1:T(8,128)} %bitcast.8), channel_id=1, source_target_pairs={{0,16},{8,24},{16,0},{24,8},{1,17},{9,25},{17,1},{25,9},{2,18},{10... | collective-permute-start | bytes 2359304 | tf_op jit(solution)/shard_map/ppermute | solution.py:32
  15.1 0.3 collective-permute-start
  15.4 3.8 %gather_fusion.6 = f32[256,1024]{1,0:T(8,128)S(1)} fusion(f32[1024,1024]{1,0:T(8,128)} %bitcast.59, s32[1024]{0:T(1024)S(1)} %get-tuple-element.29), kind=kCustom, calls=%fused_computation.6 | custom fusion | bytes 2098176 | tf_op jit(solution)/shard_map/jit(_take)/gather | solution.py:62
  19.2 0.3 copy.8
  19.6 3.5 %gather_fusion.7 = f32[1024,256]{1,0:T(8,128)S(1)} fusion(f32[256,1024]{0,1:T(8,128)S(1)} %copy.8, s32[1024]{0:T(1024)S(1)} %broadcast_clamp_fusion), kind=kCustom, calls=%fused_computation.7 | custom fusion | bytes 2101248 | tf_op jit(solution)/shard_map/jit(_take)/gather | solution.py:63
  23.0 0.3 copy.9
  23.4 0.3 collective-permute-start.4
  23.7 0.9 slice.143
  24.6 5.8 %gather_fusion.4 = f32[512,1024]{1,0:T(8,128)} fusion(f32[1024,1024]{1,0:T(8,128)} %bitcast.60, s32[1024]{0:T(1024)S(1)} %get-tuple-element.30), kind=kCustom, calls=%fused_computation.4 | custom fusion | bytes 4196352 | tf_op jit(solution)/shard_map/jit(_take)/gather | solution.py:62
  30.4 1.9 %copy.6 = f32[512,1024]{0,1:T(8,128)S(1)} copy(f32[512,1024]{1,0:T(8,128)} %gather_fusion.4) | data formatting | bytes 4194304 | tf_op jit(solution)/shard_map/jit(_take)/gather | solution.py:62
  32.3 4.9 %gather_fusion.5 = f32[1024,512]{1,0:T(8,128)} fusion(f32[512,1024]{0,1:T(8,128)S(1)} %copy.6, s32[1024]{0:T(1024)S(1)} %broadcast_clamp_fusion), kind=kCustom, calls=%fused_computation.5 | custom fusion | bytes 4198400 | tf_op jit(solution)/shard_map/jit(_take)/gather | solution.py:63
  37.2 2.1 %copy.7 = f32[1024,512]{0,1:T(8,128)S(1)} copy(f32[1024,512]{1,0:T(8,128)} %gather_fusion.5) | data formatting | bytes 4194304 | tf_op jit(solution)/shard_map/jit(_take)/gather | solution.py:63
  39.3 1.3 slice.136
  40.6 0.1 fusion.79
  40.7 18.8 %collective-permute-done = f32[256,256]{1,0:T(8,128)} collective-permute-done((f32[256,256]{1,0:T(8,128)S(1)}, f32[256,256]{1,0:T(8,128)}, u32[]{:S(2)}, u32[]{:S(2)}) %collective-permute-start) | collective-permute-done | bytes 262176 | tf_op jit(solution)/shard_map/ppermute | solution.py:32
  59.5 1.1 select_reduce_fusion.1
  60.6 0.4 fusion.53
  61.0 0.5 multiply_subtract_fusion.3
  61.5 0.4 fusion.81
  61.9 0.4 convolution_subtract_fusion.4
  62.3 1.6 %collective-permute-start.5 = (f32[256,256]{1,0:T(8,128)S(1)}, f32[256,256]{1,0:T(8,128)S(1)}, u32[]{:S(2)}, u32[]{:S(2)}) collective-permute-start(f32[256,256]{1,0:T(8,128)S(1)} %convolution_subtract_fusion.4), channel_id=1, source_target_pairs={{0,16},{8,24},{16,0},{24,8},{1,17},{9,25},{17,1},{25,9},{2,18},{10... | collective-permute-start | bytes 786440 | tf_op jit(solution)/shard_map/ppermute | solution.py:32
  63.9 0.0 collective-permute-done.1
  63.9 3.0 %convolution_negate_fusion.1 = f32[256,1536]{1,0:T(8,128)S(1)} fusion(f32[256,256]{1,0:T(8,128)S(1)} %convolution_subtract_fusion.4, f32[256,768]{0,1:T(8,128)} %collective-permute-done.1, f32[256,768]{0,1:T(8,128)} %bitcast.8), kind=kOutput, calls=%fused_computation.11 | convolution fusion | flops 1208745984 | bytes 3407872 | tf_op jit(solution)/shard_map/dot_general | solution.py:11
  66.9 0.1 collective-permute-start.2
  67.0 0.5 collective-permute-start.7
  67.5 2.9 %convolution_add_fusion = f32[512,1536]{1,0:T(8,128)S(1)} fusion(f32[256,1536]{1,0:T(8,128)S(1)} %convolution_negate_fusion.1, f32[512,768]{1,0:T(8,128)S(1)} %copy-done.1, f32[512,1024]{1,0:T(8,128)S(1)} %bitcast.66), kind=kOutput, calls=%fused_computation.8 | convolution fusion | flops 2416705536 | bytes 6815744 | tf_op jit(solution)/shard_map/dot_general | solution.py:11
  70.4 1.5 %convolution_add_fusion.1 = f32[256,1536]{1,0:T(8,128)S(1)} fusion(f32[256,1536]{1,0:T(8,128)S(1)} %convolution_negate_fusion.1, f32[256,768]{1,0:T(8,128)S(1)} %copy-done.3, f32[256,1024]{1,0:T(8,128)S(1)} %bitcast.64), kind=kOutput, calls=%fused_computation.9 | convolution fusion | flops 1208352768 | bytes 4194304 | tf_op jit(solution)/shard_map/dot_general | solution.py:11
  71.9 0.1 fusion.78
  71.9 1.2 slice.148
  73.1 18.5 %collective-permute-done.2 = f32[128,1024]{1,0:T(8,128)S(1)} collective-permute-done((f32[128,1024]{1,0:T(8,128)S(1)}, f32[128,1024]{1,0:T(8,128)S(1)}, u32[]{:S(2)}, u32[]{:S(2)}) %collective-permute-start.2) | collective-permute-done | bytes 524320 | tf_op jit(solution)/shard_map/ppermute | solution.py:32
  91.6 0.0 collective-permute-start.3
  91.6 0.8 collective-permute-start.8
  92.4 0.0 collective-permute-done.5
  92.5 2.6 %convolution_negate_fusion = f32[256,1536]{1,0:T(8,128)S(1)} fusion(f32[256,256]{1,0:T(8,128)S(1)} %collective-permute-done.5, f32[256,768]{0,1:T(8,128)S(1)} %collective-permute-done.7, f32[256,768]{0,1:T(8,128)} %collective-permute-done.6), kind=kOutput, calls=%fused_computation.10 | convolution fusion | flops 1208745984 | bytes 3407872 | tf_op jit(solution)/shard_map/dot_general | solution.py:11
  95.1 2.4 %pad_add_fusion.1 = f32[256,1536]{1,0:T(8,128)S(1)} fusion(f32[256,768]{1,0:T(8,128)S(1)} %slice.148, f32[256,1536]{1,0:T(8,128)S(1)} %convolution_negate_fusion, f32[256,1024]{1,0:T(8,128)} %collective-permute-done.4), kind=kOutput, calls=%fused_computation.19 | convolution fusion | flops 1208352768 | bytes 4194304 | tf_op jit(solution)/shard_map/dot_general | solution.py:11
  97.5 18.1 %collective-permute-done.3 = f32[128,1024]{1,0:T(8,128)S(1)} collective-permute-done((f32[128,1024]{1,0:T(8,128)S(1)}, f32[128,1024]{1,0:T(8,128)S(1)}, u32[]{:S(2)}, u32[]{:S(2)}) %collective-permute-start.3) | collective-permute-done | bytes 524320 | tf_op jit(solution)/shard_map/ppermute | solution.py:32
  115.7 1.0 collective-permute-start.9
  116.7 0.1 slice.146
  116.8 1.7 %pad_add_fusion.2 = f32[256,1536]{1,0:T(8,128)S(1)} fusion(f32[256,768]{1,0:T(8,128)S(1)} %slice.146, f32[256,1536]{1,0:T(8,128)S(1)} %convolution_negate_fusion.1, f32[256,1024]{1,0:T(8,128)S(1)} %constant_dynamic-update-slice_fusion), kind=kOutput, calls=%fused_computation.20 | convolution fusion | flops 1208352768 | bytes 4194304 | tf_op jit(solution)/shard_map/dot_general | solution.py:11
  118.5 10.4 %collective-permute-done.9 = f32[128,1024]{1,0:T(8,128)S(1)} collective-permute-done((f32[128,1024]{1,0:T(8,128)S(1)}, f32[128,1024]{1,0:T(8,128)S(1)}, u32[]{:S(2)}, u32[]{:S(2)}) %collective-permute-start.9) | collective-permute-done | bytes 524320 | tf_op jit(solution)/shard_map/ppermute | solution.py:32
  129.0 0.1 slice.150
  129.1 1.5 %pad_add_fusion = f32[256,1536]{1,0:T(8,128)S(1)} fusion(f32[256,768]{1,0:T(8,128)S(1)} %slice.150, f32[256,1536]{1,0:T(8,128)S(1)} %convolution_negate_fusion, f32[256,1024]{1,0:T(8,128)S(1)} %constant_dynamic-update-slice_fusion.2), kind=kOutput, calls=%fused_computation.18 | convolution fusion | flops 1208352768 | bytes 4194304 | tf_op jit(solution)/shard_map/dot_general | solution.py:11
  130.5 0.2 select_reduce_fusion
  130.7 1.1 fusion.29
  131.8 1.3 convolution_subtract_fusion.3
  133.1 1.0 fusion.82
  134.2 1.0 convolution_subtract_fusion.2
  135.2 1.0 fusion.25
  136.3 0.5 broadcast_in_dim.50
  136.8 1.1 fusion.13
  137.8 1.1 fusion.11
  138.9 1.0 fusion.9
  140.0 0.0 copy-start.2
  140.0 2.0 %copy-done.2 = f32[1,1,512,2048]{3,2,1,0:T(8,128)} copy-done((f32[1,1,512,2048]{3,2,1,0:T(8,128)}, f32[1,1,512,2048]{3,2,1,0:T(8,128)S(1)}, u32[]{:S(2)}) %copy-start.2) | copy-done | bytes 4194328
  142.0 2.0 %fusion.7 = f32[1,1,512,2048]{3,2,1,0:T(8,128)} fusion(f32[1,1,512,2048]{3,2,1,0:T(8,128)} %copy-done.2, s32[]{:T(128)S(6)} %select_n.35, f32[512,512]{1,0:T(8,128)S(1)} %fusion.25, f32[256,1536]{1,0:T(8,128)S(1)} %pad_add_fusion, f32[256,1536]{1,0:T(8,128)S(1)} %pad_add_fusion.1), kind=kOutput, calls=%fused_computation.23 | convolution fusion | flops 805830656 | bytes 5242884 | tf_op jit(solution)/shard_map/dot_general | solution.py:15
  (25 shorter events, 0.2 us)
Async XLA Ops:
  0.0 0.7 copy-start
  9.5 54.4 %collective-permute-start.1 = (f32[256,768]{0,1:T(8,128)}, f32[256,768]{0,1:T(8,128)}, u32[]{:S(2)}, u32[]{:S(2)}) collective-permute-start(f32[256,768]{0,1:T(8,128)} %bitcast.8), channel_id=1, source_target_pairs={{0,4},{1,5},{2,6},{3,7},{4,0},{5,1},{6,2},{7,3},{8,12},{9,13},{10,... | collective-permute-start | bytes 2359304 | tf_op jit(solution)/shard_map/ppermute | solution.py:32
  13.6 78.9 %collective-permute-start.6 = (f32[256,768]{0,1:T(8,128)}, f32[256,768]{0,1:T(8,128)}, u32[]{:S(2)}, u32[]{:S(2)}) collective-permute-start(f32[256,768]{0,1:T(8,128)} %bitcast.8), channel_id=1, source_target_pairs={{0,16},{8,24},{16,0},{24,8},{1,17},{9,25},{17,1},{25,9},{2,18},{10... | collective-permute-start | bytes 2359304 | tf_op jit(solution)/shard_map/ppermute | solution.py:32
  15.1 44.4 %collective-permute-start = (f32[256,256]{1,0:T(8,128)S(1)}, f32[256,256]{1,0:T(8,128)}, u32[]{:S(2)}, u32[]{:S(2)}) collective-permute-start(f32[256,256]{1,0:T(8,128)S(1)} %bitcast.67), channel_id=1, source_target_pairs={{0,4},{1,5},{2,6},{3,7},{4,0},{5,1},{6,2},{7,3},{8,12},{9,13},{10,... | collective-permute-start | bytes 786440 | tf_op jit(solution)/shard_map/ppermute | solution.py:32
  23.4 48.6 %collective-permute-start.4 = (f32[256,1024]{1,0:T(8,128)S(1)}, f32[256,1024]{1,0:T(8,128)}, u32[]{:S(2)}, u32[]{:S(2)}) collective-permute-start(f32[256,1024]{1,0:T(8,128)S(1)} %bitcast.61), channel_id=1, source_target_pairs={{0,16},{8,24},{16,0},{24,8},{1,17},{9,25},{17,1},{25,9},{2,18},{10... | collective-permute-start | bytes 3145736 | tf_op jit(solution)/shard_map/ppermute | solution.py:32
  62.3 30.2 %collective-permute-start.5 = (f32[256,256]{1,0:T(8,128)S(1)}, f32[256,256]{1,0:T(8,128)S(1)}, u32[]{:S(2)}, u32[]{:S(2)}) collective-permute-start(f32[256,256]{1,0:T(8,128)S(1)} %convolution_subtract_fusion.4), channel_id=1, source_target_pairs={{0,16},{8,24},{16,0},{24,8},{1,17},{9,25},{17,1},{25,9},{2,18},{10... | collective-permute-start | bytes 786440 | tf_op jit(solution)/shard_map/ppermute | solution.py:32
  63.9 3.6 %copy-start.1 = (f32[512,768]{1,0:T(8,128)S(1)}, f32[512,768]{1,0:T(8,128)}, u32[]{:S(2)}) copy-start(f32[512,768]{1,0:T(8,128)} %slice.136) | copy-start | bytes 4718596
  66.9 3.5 %copy-start.3 = (f32[256,768]{1,0:T(8,128)S(1)}, f32[256,768]{1,0:T(8,128)}, u32[]{:S(2)}) copy-start(f32[256,768]{1,0:T(8,128)} %slice.143) | copy-start | bytes 2359300
  66.9 24.7 %collective-permute-start.2 = (f32[128,1024]{1,0:T(8,128)S(1)}, f32[128,1024]{1,0:T(8,128)S(1)}, u32[]{:S(2)}, u32[]{:S(2)}) collective-permute-start(f32[128,1024]{1,0:T(8,128)S(1)} %get-tuple-element.16), channel_id=1, source_target_pairs={{0,4},{1,5},{2,6},{3,7},{4,0},{5,1},{6,2},{7,3},{8,12},{9,13},{10,... | collective-permute-start | bytes 1572872 | tf_op jit(solution)/shard_map/ppermute | solution.py:32
  67.0 25.5 %collective-permute-start.7 = (f32[256,768]{0,1:T(8,128)}, f32[256,768]{0,1:T(8,128)S(1)}, u32[]{:S(2)}, u32[]{:S(2)}) collective-permute-start(f32[256,768]{0,1:T(8,128)} %collective-permute-done.1), channel_id=1, source_target_pairs={{0,16},{8,24},{16,0},{24,8},{1,17},{9,25},{17,1},{25,9},{2,18},{10... | collective-permute-start | bytes 2359304 | tf_op jit(solution)/shard_map/ppermute | solution.py:32
  91.6 24.0 %collective-permute-start.3 = (f32[128,1024]{1,0:T(8,128)S(1)}, f32[128,1024]{1,0:T(8,128)S(1)}, u32[]{:S(2)}, u32[]{:S(2)}) collective-permute-start(f32[128,1024]{1,0:T(8,128)S(1)} %get-tuple-element.18), channel_id=1, source_target_pairs={{0,4},{1,5},{2,6},{3,7},{4,0},{5,1},{6,2},{7,3},{8,12},{9,13},{10,... | collective-permute-start | bytes 1572872 | tf_op jit(solution)/shard_map/ppermute | solution.py:32
  91.6 25.1 %collective-permute-start.8 = (f32[128,1024]{1,0:T(8,128)S(1)}, f32[128,1024]{1,0:T(8,128)S(1)}, u32[]{:S(2)}, u32[]{:S(2)}) collective-permute-start(f32[128,1024]{1,0:T(8,128)S(1)} %collective-permute-done.2), channel_id=1, source_target_pairs={{0,16},{8,24},{16,0},{24,8},{1,17},{9,25},{17,1},{25,9},{2,18},{10... | collective-permute-start | bytes 1572872 | tf_op jit(solution)/shard_map/ppermute | solution.py:32
  115.7 13.3 %collective-permute-start.9 = (f32[128,1024]{1,0:T(8,128)S(1)}, f32[128,1024]{1,0:T(8,128)S(1)}, u32[]{:S(2)}, u32[]{:S(2)}) collective-permute-start(f32[128,1024]{1,0:T(8,128)S(1)} %collective-permute-done.3), channel_id=1, source_target_pairs={{0,16},{8,24},{16,0},{24,8},{1,17},{9,25},{17,1},{25,9},{2,18},{10... | collective-permute-start | bytes 1572872 | tf_op jit(solution)/shard_map/ppermute | solution.py:32
  140.0 2.0 %copy-start.2 = (f32[1,1,512,2048]{3,2,1,0:T(8,128)}, f32[1,1,512,2048]{3,2,1,0:T(8,128)S(1)}, u32[]{:S(2)}) copy-start(f32[1,1,512,2048]{3,2,1,0:T(8,128)S(1)} %fusion.9) | copy-start | bytes 12582916

commit v5 on v2

--- a/solution.py
+++ b/solution.py
@@ -32,18 +32,18 @@
     return lax.ppermute(value, axis, pairs)
 
 
-def pair_solve(inverse, first_ie, second_ie):
-    return -matmul(inverse, jnp.concatenate([first_ie, second_ie], 1))
+def pair_solve(inverse, first_ie, second_ie, product=matmul):
+    return -product(inverse, jnp.concatenate([first_ie, second_ie], 1))
 
 
-def first_rows(rows, solved, width):
+def first_rows(rows, solved, width, product=matmul):
     blank = jnp.zeros((rows.shape[0], 3 * width), jnp.float32)
-    return jnp.concatenate([rows[:, width:], blank], 1) + matmul(rows[:, :width], solved)
+    return jnp.concatenate([rows[:, width:], blank], 1) + product(rows[:, :width], solved)
 
 
-def second_rows(rows, solved, width):
+def second_rows(rows, solved, width, product=matmul):
     blank = jnp.zeros((rows.shape[0], 3 * width), jnp.float32)
-    return jnp.concatenate([blank, rows[:, width:]], 1) + matmul(rows[:, :width], solved)
+    return jnp.concatenate([blank, rows[:, width:]], 1) + product(rows[:, :width], solved)
 
 
 def ext_cols(parent, width):
@@ -97,9 +97,9 @@
     own_int = first_rows(own_i2, solved_own, width)
     side_int = second_rows(side_i2, solved_own, width)
 
-    solved_other = pair_solve(inverse_other, vert_ie, diag_ie)
-    vert_int = first_rows(vert_i2, solved_other, width)
-    diag_int = second_rows(diag_i2, solved_other, width)
+    solved_other = pair_solve(inverse_other, vert_ie, diag_ie, matmul_high)
+    vert_int = first_rows(vert_i2, solved_other, width, matmul_high)
+    diag_int = second_rows(diag_i2, solved_other, width, matmul_high)
 
     near = jnp.concatenate([own_int, side_int], 0)
     far = jnp.concatenate([vert_int, diag_int], 0)
@@ -107,16 +107,21 @@
     inverse_two = newton(system_two, ITERS_HIGH, matmul_high)
     weights = matmul_high(int_cols(own_ext, width), inverse_two)
     own_id = 2 * upper + right
-    pieces = [
-        own_ext[:, 0 : 2 * width] - matmul_high(weights, near[:, 0 : 2 * width]),
-        own_ext[:, 3 * width : 5 * width] - matmul_high(weights, near[:, 3 * width : 5 * width]),
-        -matmul_high(weights, far[:, 0 : 2 * width]),
-        -matmul_high(weights, far[:, 3 * width : 5 * width]),
+    blocks = [
+        near[:, 0 : 2 * width],
+        near[:, 3 * width : 5 * width],
+        far[:, 0 : 2 * width],
+        far[:, 3 * width : 5 * width],
     ]
-    merged = jnp.zeros((2 * width, 8 * width), jnp.float32)
-    for rel, piece in enumerate(pieces):
+    coupling_two = jnp.zeros((2 * width, 8 * width), jnp.float32)
+    for rel, block in enumerate(blocks):
         start = jnp.bitwise_xor(own_id, rel) * (2 * width)
-        merged = lax.dynamic_update_slice(merged, piece, (0, start))
+        coupling_two = lax.dynamic_update_slice(coupling_two, block, (0, start))
+    own_block = jnp.zeros((2 * width, 8 * width), jnp.float32)
+    own_block = lax.dynamic_update_slice(own_block, own_ext[:, 0 : 2 * width], (0, own_id * (2 * width)))
+    mate_start = jnp.bitwise_xor(own_id, 1) * (2 * width)
+    own_block = lax.dynamic_update_slice(own_block, own_ext[:, 3 * width : 5 * width], (0, mate_start))
+    merged = own_block - matmul_high(weights, coupling_two)
     return merged[None, None]
 
 

time: 142 us -> 136 us (0.958)
  waiting for transfers between devices: 58.2 us -> 55.3 us
  matrix products: 27.5 us -> 24.8 us
    dot_general x11 -> x8, matrix products: 16.8 us -> 9.83 us  [matmul(): jnp.dot(left, right, precision=lax.Precision.HIGHEST, preferred_element_t...]
    dot_general x9, matrix products: 10.7 us -> 15 us  [matmul_high(): jnp.dot(left, right, precision=lax.Precision.HIGH, preferred_element_type...]
    ppermute x9, waiting for transfers between devices: 58.2 us -> 55.3 us  [swap(): return lax.ppermute(value, axis, pairs)]
    unnamed x13, local copies, waits for them, and re-layouts: 2.8 us -> 0.71 us
  transfers between devices with their start and end apart: 9 -> 9, of which waited for: 4 -> 5; matrix products, arithmetic and copies ran while one was open for 33% -> 35% of each run, Pallas kernels for 0% -> 0%
where the time goes in v5:
time: 136 us; the launch traced here: 135 us
  waiting for transfers between devices  55.3 us (41%)
  local copies, waits for them, and re-layouts  42.4 us (31%)
  matrix products  24.8 us (18%)
  starting transfers between devices  10.6 us (8%)
  other arithmetic  1.88 us (1%)
    ppermute x9, waiting for transfers between devices, swap(): return lax.ppermute(value, axis, pairs)  55.3 us
    gather x6, local copies, waits for them, and re-layouts, pick(): picked = jnp.take(matrix, rows, axis=0, mode='clip')  15.9 us
    gather x6, local copies, waits for them, and re-layouts, pick(): return jnp.take(picked, cols, axis=1, mode='clip')  15.6 us
    dot_general x9, matrix products, matmul_high(): jnp.dot(left, right, precision=lax.Precision.HIGH, preferred_element_type...  15 us
    ppermute x9, starting transfers between devices, swap(): return lax.ppermute(value, axis, pairs)  10.6 us
    dot_general x8, matrix products, matmul(): jnp.dot(left, right, precision=lax.Precision.HIGHEST, preferred_element_t...  9.83 us
    slice x3, local copies, waits for them, and re-layouts, first_rows(): rows[:, width:]  3.41 us
    slice x2, local copies, waits for them, and re-layouts, body(): solved_own = pair_solve(inverse_own, own_i1[:, width:], side_i1[:, width:])  3.3 us
  transfers between devices with their start and end apart: 9, of which 5 were waited for; matrix products, arithmetic and copies ran while one was open for 35% of the time, Pallas kernels for 0%

profile of v5, /device:TPU:0, one launch (start us, length us, event | category | flops | bytes accessed | tf_op | source)
XLA Modules:
  0.0 135.4 jit_solution(585411378642111932)
XLA Ops:
  0.0 0.1 pad_add_fusion.3
  0.1 0.6 copy-done
  0.7 0.6 gather_fusion
  1.3 3.8 %gather_fusion.1 = f32[256,1024]{1,0:T(8,128)S(1)} fusion(f32[1024,1024]{1,0:T(8,128)} %bitcast.41, s32[1024]{0:T(1024)S(1)} %get-tuple-element.30), kind=kCustom, calls=%fused_computation.1 | custom fusion | bytes 2098176 | tf_op jit(solution)/shard_map/jit(_take)/gather | solution.py:62
  5.1 0.3 copy.3
  5.4 3.5 %gather_fusion.2 = f32[1024,256]{1,0:T(8,128)S(1)} fusion(f32[256,1024]{0,1:T(8,128)S(1)} %copy.3, s32[1024]{0:T(1024)S(1)} %get-tuple-element.31), kind=kCustom, calls=%fused_computation.2 | custom fusion | bytes 2101248 | tf_op jit(solution)/shard_map/jit(_take)/gather | solution.py:63
  8.9 1.3 copy.4
  10.2 4.0 %collective-permute-start = (f32[256,1024]{1,0:T(8,128)}, f32[256,1024]{1,0:T(8,128)}, u32[]{:S(2)}, u32[]{:S(2)}) collective-permute-start(f32[256,1024]{1,0:T(8,128)} %bitcast.7), channel_id=1, source_target_pairs={{0,4},{1,5},{2,6},{3,7},{4,0},{5,1},{6,2},{7,3},{8,12},{9,13},{10,... | collective-permute-start | bytes 3145736 | tf_op jit(solution)/shard_map/ppermute | solution.py:32
  14.2 2.1 %slice.106 = f32[256,768]{1,0:T(8,128)} slice(f32[256,1024]{1,0:T(8,128)} %bitcast.7), slice={[0:256], [256:1024]} | slice | bytes 1572864 | tf_op jit(solution)/shard_map/slice | solution.py:95
  16.3 1.5 %collective-permute-start.5 = (f32[256,768]{1,0:T(8,128)}, f32[256,768]{1,0:T(8,128)}, u32[]{:S(2)}, u32[]{:S(2)}) collective-permute-start(f32[256,768]{1,0:T(8,128)} %slice.106), channel_id=1, source_target_pairs={{0,16},{8,24},{16,0},{24,8},{1,17},{9,25},{17,1},{25,9},{2,18},{10... | collective-permute-start | bytes 2359304 | tf_op jit(solution)/shard_map/ppermute | solution.py:32
  17.9 3.8 %gather_fusion.5 = f32[256,1024]{1,0:T(8,128)S(1)} fusion(f32[1024,1024]{1,0:T(8,128)} %bitcast.42, s32[1024]{0:T(1024)S(1)} %get-tuple-element.28), kind=kCustom, calls=%fused_computation.5 | custom fusion | bytes 2098176 | tf_op jit(solution)/shard_map/jit(_take)/gather | solution.py:62
  21.6 0.3 copy.7
  22.0 3.5 %gather_fusion.6 = f32[1024,256]{1,0:T(8,128)S(1)} fusion(f32[256,1024]{0,1:T(8,128)S(1)} %copy.7, s32[1024]{0:T(1024)S(1)} %get-tuple-element.31), kind=kCustom, calls=%fused_computation.6 | custom fusion | bytes 2101248 | tf_op jit(solution)/shard_map/jit(_take)/gather | solution.py:63
  25.5 0.3 copy.8
  25.8 0.6 collective-permute-start.3
  26.4 1.0 slice.157
  27.3 5.8 %gather_fusion.3 = f32[512,1024]{1,0:T(8,128)} fusion(f32[1024,1024]{1,0:T(8,128)} %bitcast.43, s32[1024]{0:T(1024)S(1)} %get-tuple-element.29), kind=kCustom, calls=%fused_computation.3 | custom fusion | bytes 4196352 | tf_op jit(solution)/shard_map/jit(_take)/gather | solution.py:62
  33.1 1.9 %copy.5 = f32[512,1024]{0,1:T(8,128)S(1)} copy(f32[512,1024]{1,0:T(8,128)} %gather_fusion.3) | data formatting | bytes 4194304 | tf_op jit(solution)/shard_map/jit(_take)/gather | solution.py:62
  35.0 4.9 %gather_fusion.4 = f32[1024,512]{1,0:T(8,128)} fusion(f32[512,1024]{0,1:T(8,128)S(1)} %copy.5, s32[1024]{0:T(1024)S(1)} %get-tuple-element.31), kind=kCustom, calls=%fused_computation.4 | custom fusion | bytes 4198400 | tf_op jit(solution)/shard_map/jit(_take)/gather | solution.py:63
  39.9 2.1 %copy.6 = f32[1024,512]{0,1:T(8,128)S(1)} copy(f32[1024,512]{1,0:T(8,128)} %gather_fusion.4) | data formatting | bytes 4194304 | tf_op jit(solution)/shard_map/jit(_take)/gather | solution.py:63
  42.0 1.3 slice.148
  43.3 0.1 fusion.60
  43.4 16.8 %collective-permute-done = f32[256,1024]{1,0:T(8,128)} collective-permute-done((f32[256,1024]{1,0:T(8,128)}, f32[256,1024]{1,0:T(8,128)}, u32[]{:S(2)}, u32[]{:S(2)}) %collective-permute-start) | collective-permute-done | bytes 1048608 | tf_op jit(solution)/shard_map/ppermute | solution.py:32
  60.2 1.2 slice.109
  61.4 1.1 select_reduce_fusion.1
  62.5 0.4 fusion.38
  63.0 0.5 convolution_subtract_fusion.3
  63.4 0.4 fusion.62
  63.8 0.4 convolution_subtract_fusion.2
  64.2 1.6 %collective-permute-start.4 = (f32[256,256]{1,0:T(8,128)S(1)}, f32[256,256]{1,0:T(8,128)S(1)}, u32[]{:S(2)}, u32[]{:S(2)}) collective-permute-start(f32[256,256]{1,0:T(8,128)S(1)} %convolution_subtract_fusion.2), channel_id=1, source_target_pairs={{0,16},{8,24},{16,0},{24,8},{1,17},{9,25},{17,1},{25,9},{2,18},{10... | collective-permute-start | bytes 786440 | tf_op jit(solution)/shard_map/ppermute | solution.py:32
  65.9 2.6 %convolution_negate_fusion.1 = f32[256,1536]{1,0:T(8,128)S(1)} fusion(f32[256,256]{1,0:T(8,128)S(1)} %convolution_subtract_fusion.2, f32[256,768]{1,0:T(8,128)S(1)} %slice.109, f32[256,768]{1,0:T(8,128)} %slice.106), kind=kOutput, calls=%fused_computation.11 | convolution fusion | flops 1208745984 | bytes 3407872 | tf_op jit(solution)/shard_map/dot_general | solution.py:11
  68.5 1.3 slice.164
  69.7 0.0 copy-start.2
  69.7 0.5 collective-permute-start.6
  70.2 1.5 %convolution_add_fusion.1 = f32[256,1536]{1,0:T(8,128)S(1)} fusion(f32[256,1536]{1,0:T(8,128)S(1)} %convolution_negate_fusion.1, f32[256,768]{1,0:T(8,128)S(1)} %copy-done.3, f32[256,1024]{1,0:T(8,128)S(1)} %bitcast.47), kind=kOutput, calls=%fused_computation.9 | convolution fusion | flops 1208352768 | bytes 4194304 | tf_op jit(solution)/shard_map/dot_general | solution.py:11
  71.7 2.7 %convolution_add_fusion = f32[512,1536]{1,0:T(8,128)S(1)} fusion(f32[256,1536]{1,0:T(8,128)S(1)} %convolution_negate_fusion.1, f32[512,768]{1,0:T(8,128)S(1)} %copy-done.2, f32[512,1024]{1,0:T(8,128)S(1)} %bitcast.49), kind=kOutput, calls=%fused_computation.8 | convolution fusion | flops 2416705536 | bytes 6815744 | tf_op jit(solution)/shard_map/dot_general | solution.py:11
  74.4 0.5 broadcast.44.clone
  74.9 0.1 slice_dynamic-update-slice_fusion.1
  75.1 1.2 slice.162
  76.2 0.1 slice_dynamic-update-slice_fusion
  76.3 0.1 fusion.59
  76.4 9.0 %collective-permute-done.1 = f32[128,1024]{1,0:T(8,128)S(1)} collective-permute-done((f32[128,1024]{1,0:T(8,128)S(1)}, f32[128,1024]{1,0:T(8,128)S(1)}, u32[]{:S(2)}, u32[]{:S(2)}) %collective-permute-start.1) | collective-permute-done | bytes 524320 | tf_op jit(solution)/shard_map/ppermute | solution.py:32
  85.4 1.3 collective-permute-start.7
  86.8 3.5 %collective-permute-done.6 = f32[256,768]{1,0:T(8,128)S(1)} collective-permute-done((f32[256,768]{1,0:T(8,128)S(1)}, f32[256,768]{1,0:T(8,128)S(1)}, u32[]{:S(2)}, u32[]{:S(2)}) %collective-permute-start.6) | collective-permute-done | bytes 786464 | tf_op jit(solution)/shard_map/ppermute | solution.py:32
  90.3 2.0 %convolution_negate_fusion = f32[256,1536]{1,0:T(8,128)S(1)} fusion(f32[256,256]{1,0:T(8,128)S(1)} %collective-permute-done.4, f32[256,768]{1,0:T(8,128)S(1)} %collective-permute-done.6, f32[256,768]{1,0:T(8,128)} %collective-permute-done.5), kind=kOutput, calls=%fused_computation.10 | convolution fusion | flops 604766208 | bytes 3407872 | tf_op jit(solution)/shard_map/dot_general | solution.py:15
  92.2 1.8 %pad_add_fusion.1 = f32[256,1536]{1,0:T(8,128)S(1)} fusion(f32[256,768]{1,0:T(8,128)S(1)} %slice.162, f32[256,1536]{1,0:T(8,128)S(1)} %convolution_negate_fusion, f32[256,1024]{1,0:T(8,128)} %collective-permute-done.3), kind=kOutput, calls=%fused_computation.19 | convolution fusion | flops 604372992 | bytes 4194304 | tf_op jit(solution)/shard_map/dot_general | solution.py:15
  94.0 15.7 %collective-permute-done.2 = f32[128,1024]{1,0:T(8,128)S(1)} collective-permute-done((f32[128,1024]{1,0:T(8,128)S(1)}, f32[128,1024]{1,0:T(8,128)S(1)}, u32[]{:S(2)}, u32[]{:S(2)}) %collective-permute-start.2) | collective-permute-done | bytes 524320 | tf_op jit(solution)/shard_map/ppermute | solution.py:32
  109.8 0.1 slice.160
  109.9 1.0 collective-permute-start.8
  111.0 1.4 %pad_add_fusion.2 = f32[256,1536]{1,0:T(8,128)S(1)} fusion(f32[256,768]{1,0:T(8,128)S(1)} %slice.160, f32[256,1536]{1,0:T(8,128)S(1)} %convolution_negate_fusion.1, f32[256,1024]{1,0:T(8,128)S(1)} %constant_dynamic-update-slice_fusion), kind=kOutput, calls=%fused_computation.20 | convolution fusion | flops 1208352768 | bytes 4194304 | tf_op jit(solution)/shard_map/dot_general | solution.py:11
  112.4 0.7 broadcast.44.clone.1
  113.1 0.1 maximum_dynamic-update-slice_fusion.1
  113.2 0.1 fusion.7
  113.3 10.3 %collective-permute-done.8 = f32[128,1024]{1,0:T(8,128)S(1)} collective-permute-done((f32[128,1024]{1,0:T(8,128)S(1)}, f32[128,1024]{1,0:T(8,128)S(1)}, u32[]{:S(2)}, u32[]{:S(2)}) %collective-permute-start.8) | collective-permute-done | bytes 524320 | tf_op jit(solution)/shard_map/ppermute | solution.py:32
  123.6 0.1 slice.165
  123.7 0.8 pad_add_fusion
  124.5 0.1 maximum_dynamic-update-slice_fusion
  124.6 0.3 select_reduce_fusion
  125.0 1.1 fusion.15
  126.1 1.3 convolution_subtract_fusion.1
  127.3 1.0 fusion.63
  128.3 1.0 convolution_subtract_fusion
  129.4 1.0 fusion.11
  130.4 5.1 %subtract_bitcast_fusion = f32[1,1,512,2048]{3,2,1,0:T(8,128)} fusion(f32[512,2048]{1,0:T(8,128)S(1)} %slice_dynamic-update-slice_fusion, f32[512,512]{1,0:T(8,128)S(1)} %fusion.11, f32[512,2048]{1,0:T(8,128)S(1)} %get-tuple-element.21), kind=kOutput, calls=%fused_computation.7 | convolution fusion | flops 3222274048 | bytes 13631488 | tf_op jit(solution)/shard_map/dot_general | solution.py:15
  (25 shorter events, 0.2 us)
Async XLA Ops:
  0.0 0.7 copy-start
  10.2 50.0 %collective-permute-start = (f32[256,1024]{1,0:T(8,128)}, f32[256,1024]{1,0:T(8,128)}, u32[]{:S(2)}, u32[]{:S(2)}) collective-permute-start(f32[256,1024]{1,0:T(8,128)} %bitcast.7), channel_id=1, source_target_pairs={{0,4},{1,5},{2,6},{3,7},{4,0},{5,1},{6,2},{7,3},{8,12},{9,13},{10,... | collective-permute-start | bytes 3145736 | tf_op jit(solution)/shard_map/ppermute | solution.py:32
  16.3 70.4 %collective-permute-start.5 = (f32[256,768]{1,0:T(8,128)}, f32[256,768]{1,0:T(8,128)}, u32[]{:S(2)}, u32[]{:S(2)}) collective-permute-start(f32[256,768]{1,0:T(8,128)} %slice.106), channel_id=1, source_target_pairs={{0,16},{8,24},{16,0},{24,8},{1,17},{9,25},{17,1},{25,9},{2,18},{10... | collective-permute-start | bytes 2359304 | tf_op jit(solution)/shard_map/ppermute | solution.py:32
  25.8 49.2 %collective-permute-start.3 = (f32[256,1024]{1,0:T(8,128)S(1)}, f32[256,1024]{1,0:T(8,128)}, u32[]{:S(2)}, u32[]{:S(2)}) collective-permute-start(f32[256,1024]{1,0:T(8,128)S(1)} %bitcast.44), channel_id=1, source_target_pairs={{0,16},{8,24},{16,0},{24,8},{1,17},{9,25},{17,1},{25,9},{2,18},{10... | collective-permute-start | bytes 3145736 | tf_op jit(solution)/shard_map/ppermute | solution.py:32
  60.2 25.2 %collective-permute-start.1 = (f32[128,1024]{1,0:T(8,128)S(1)}, f32[128,1024]{1,0:T(8,128)S(1)}, u32[]{:S(2)}, u32[]{:S(2)}) collective-permute-start(f32[128,1024]{1,0:T(8,128)S(1)} %get-tuple-element.14), channel_id=1, source_target_pairs={{0,4},{1,5},{2,6},{3,7},{4,0},{5,1},{6,2},{7,3},{8,12},{9,13},{10,... | collective-permute-start | bytes 1572872 | tf_op jit(solution)/shard_map/ppermute | solution.py:32
  64.2 22.6 %collective-permute-start.4 = (f32[256,256]{1,0:T(8,128)S(1)}, f32[256,256]{1,0:T(8,128)S(1)}, u32[]{:S(2)}, u32[]{:S(2)}) collective-permute-start(f32[256,256]{1,0:T(8,128)S(1)} %convolution_subtract_fusion.2), channel_id=1, source_target_pairs={{0,16},{8,24},{16,0},{24,8},{1,17},{9,25},{17,1},{25,9},{2,18},{10... | collective-permute-start | bytes 786440 | tf_op jit(solution)/shard_map/ppermute | solution.py:32
  68.4 1.8 %copy-start.3 = (f32[256,768]{1,0:T(8,128)S(1)}, f32[256,768]{1,0:T(8,128)}, u32[]{:S(2)}) copy-start(f32[256,768]{1,0:T(8,128)} %slice.157) | copy-start | bytes 2359300
  69.7 2.0 %copy-start.2 = (f32[512,768]{1,0:T(8,128)S(1)}, f32[512,768]{1,0:T(8,128)}, u32[]{:S(2)}) copy-start(f32[512,768]{1,0:T(8,128)} %slice.148) | copy-start | bytes 4718596
  69.7 20.5 %collective-permute-start.6 = (f32[256,768]{1,0:T(8,128)S(1)}, f32[256,768]{1,0:T(8,128)S(1)}, u32[]{:S(2)}, u32[]{:S(2)}) collective-permute-start(f32[256,768]{1,0:T(8,128)S(1)} %slice.164), channel_id=1, source_target_pairs={{0,16},{8,24},{16,0},{24,8},{1,17},{9,25},{17,1},{25,9},{2,18},{10... | collective-permute-start | bytes 2359304 | tf_op jit(solution)/shard_map/ppermute | solution.py:32
  85.4 24.3 %collective-permute-start.2 = (f32[128,1024]{1,0:T(8,128)S(1)}, f32[128,1024]{1,0:T(8,128)S(1)}, u32[]{:S(2)}, u32[]{:S(2)}) collective-permute-start(f32[128,1024]{1,0:T(8,128)S(1)} %get-tuple-element.16), channel_id=1, source_target_pairs={{0,4},{1,5},{2,6},{3,7},{4,0},{5,1},{6,2},{7,3},{8,12},{9,13},{10,... | collective-permute-start | bytes 1572872 | tf_op jit(solution)/shard_map/ppermute | solution.py:32
  85.4 25.5 %collective-permute-start.7 = (f32[128,1024]{1,0:T(8,128)S(1)}, f32[128,1024]{1,0:T(8,128)S(1)}, u32[]{:S(2)}, u32[]{:S(2)}) collective-permute-start(f32[128,1024]{1,0:T(8,128)S(1)} %collective-permute-done.1), channel_id=1, source_target_pairs={{0,16},{8,24},{16,0},{24,8},{1,17},{9,25},{17,1},{25,9},{2,18},{10... | collective-permute-start | bytes 1572872 | tf_op jit(solution)/shard_map/ppermute | solution.py:32
  109.9 13.7 %collective-permute-start.8 = (f32[128,1024]{1,0:T(8,128)S(1)}, f32[128,1024]{1,0:T(8,128)S(1)}, u32[]{:S(2)}, u32[]{:S(2)}) collective-permute-start(f32[128,1024]{1,0:T(8,128)S(1)} %collective-permute-done.2), channel_id=1, source_target_pairs={{0,16},{8,24},{16,0},{24,8},{1,17},{9,25},{17,1},{25,9},{2,18},{10... | collective-permute-start | bytes 1572872 | tf_op jit(solution)/shard_map/ppermute | solution.py:32
  130.4 5.1 %copy-start.1 = (s32[1,1,4,256]{3,2,1,0:T(4,128)S(1)}, s32[1,1,4,256]{3,2,1,0:T(4,128)}, u32[]{:S(2)}) copy-start(s32[1,1,4,256]{3,2,1,0:T(4,128)} %param.3) | copy-start | bytes 12292

commit v6 on v5

--- a/solution.py
+++ b/solution.py
@@ -58,6 +58,20 @@
     )
 
 
+def select_cols(rows, cols):
+    size = rows.shape[1]
+    chooser = (jnp.arange(size, dtype=jnp.int32)[:, None] == cols[None, :]).astype(jnp.bfloat16)
+    high = lax.reduce_precision(rows, exponent_bits=8, mantissa_bits=7)
+    rest = rows - high
+    middle = lax.reduce_precision(rest, exponent_bits=8, mantissa_bits=7)
+    low = rest - middle
+    parts = [
+        jnp.dot(part.astype(jnp.bfloat16), chooser, preferred_element_type=jnp.float32)
+        for part in (high, middle, low)
+    ]
+    return (parts[0] + parts[1]) + parts[2]
+
+
 def pick(matrix, rows, cols):
     picked = jnp.take(matrix, rows, axis=0, mode="clip")
     return jnp.take(picked, cols, axis=1, mode="clip")
@@ -71,13 +85,15 @@
     width = side_lists.shape[1]
     order = jnp.stack([1 - right, right, 2 + upper, 3 - upper])
     perm = jnp.take(side_lists, order, axis=0, mode="clip").reshape(4 * width)
-    own_i1 = pick(leaf, perm[:width], perm)
-    leaf, own_i1 = lax.optimization_barrier((leaf, own_i1))
+    rows_i1 = jnp.take(leaf, perm[:width], axis=0, mode="clip")
+    own_i1 = select_cols(rows_i1, perm)
+    own_ie = select_cols(rows_i1, perm[width:])
+    leaf, own_i1, own_ie = lax.optimization_barrier((leaf, own_i1, own_ie))
     own_i2 = pick(leaf, perm[3 * width :], perm)
     own_ov = pick(leaf, perm[width : 3 * width], perm)
 
     half = width // 2
-    vert_ie = swap(own_i1[:, width:], "grp")
+    vert_ie = swap(own_ie, "grp")
     vert_i2 = swap(own_i2, "grp")
     side_i1 = swap(own_i1, "box")
     diag_ie = swap(side_i1[:, width:], "grp")
@@ -92,7 +108,7 @@
     side_i2 = jnp.concatenate([side_first, side_second], 0)
     diag_i2 = jnp.concatenate([diag_first, diag_second], 0)
 
-    solved_own = pair_solve(inverse_own, own_i1[:, width:], side_i1[:, width:])
+    solved_own = pair_solve(inverse_own, own_ie, side_i1[:, width:])
     own_ext = first_rows(own_ov, solved_own, width)
     own_int = first_rows(own_i2, solved_own, width)
     side_int = second_rows(side_i2, solved_own, width)

time: 136 us -> 139 us (1.022)
  matrix products: 24.8 us -> 32.5 us
  local copies, waits for them, and re-layouts: 42.4 us -> 35.1 us
  waiting for transfers between devices: 55.3 us -> 57.5 us
    dot_general x0 -> x6, matrix products: none -> 7.69 us  [select_cols(): jnp.dot(part.astype(jnp.bfloat16), chooser, preferred_element_type=jnp.fl...]
    gather x6 -> x4, local copies, waits for them, and re-layouts: 15.6 us -> 10.8 us  [pick(): return jnp.take(picked, cols, axis=1, mode='clip')]
    gather x6 -> x4, local copies, waits for them, and re-layouts: 15.9 us -> 11.8 us  [pick(): picked = jnp.take(matrix, rows, axis=0, mode='clip')]
    gather x0 -> x1, local copies, waits for them, and re-layouts: none -> 3.76 us  [body(): rows_i1 = jnp.take(leaf, perm[:width], axis=0, mode='clip')]
    ppermute x9, waiting for transfers between devices: 55.3 us -> 57.5 us  [swap(): return lax.ppermute(value, axis, pairs)]
    slice x2, local copies, waits for them, and re-layouts: 3.3 us -> 1.19 us  [the longest x1 1.18 us: body(): solved_own = pair_solve(inverse_own, own_ie, side_i1[:, width:])]
  transfers between devices with their start and end apart: 9 -> 9, of which waited for: 5 -> 5; matrix products, arithmetic and copies ran while one was open for 35% -> 33% of each run, Pallas kernels for 0% -> 0%
where the time goes in v6:
time: 139 us; the launch traced here: 138 us
  waiting for transfers between devices  57.5 us (41%)
  local copies, waits for them, and re-layouts  35.1 us (25%)
  matrix products  32.5 us (23%)
  starting transfers between devices  10.6 us (8%)
  other arithmetic  1.88 us (1%)
    ppermute x9, waiting for transfers between devices, swap(): return lax.ppermute(value, axis, pairs)  57.5 us
    dot_general x9, matrix products, matmul_high(): jnp.dot(left, right, precision=lax.Precision.HIGH, preferred_element_type...  15 us
    gather x4, local copies, waits for them, and re-layouts, pick(): picked = jnp.take(matrix, rows, axis=0, mode='clip')  11.8 us
    gather x4, local copies, waits for them, and re-layouts, pick(): return jnp.take(picked, cols, axis=1, mode='clip')  10.8 us
    ppermute x9, starting transfers between devices, swap(): return lax.ppermute(value, axis, pairs)  10.6 us
    dot_general x8, matrix products, matmul(): jnp.dot(left, right, precision=lax.Precision.HIGHEST, preferred_element_t...  9.84 us
    dot_general x6, matrix products, select_cols(): jnp.dot(part.astype(jnp.bfloat16), chooser, preferred_element_type=jnp.fl...  7.69 us
    gather x1, local copies, waits for them, and re-layouts, body(): rows_i1 = jnp.take(leaf, perm[:width], axis=0, mode='clip')  3.76 us
  transfers between devices with their start and end apart: 9, of which 5 were waited for; matrix products, arithmetic and copies ran while one was open for 33% of the time, Pallas kernels for 0%

profile of v6, /device:TPU:0, one launch (start us, length us, event | category | flops | bytes accessed | tf_op | source)
XLA Modules:
  0.0 138.0 jit_solution(9120119603224118590)
XLA Ops:
  0.0 0.1 pad_add_fusion.3
  0.1 0.6 copy-done
  0.7 0.6 gather_fusion
  1.3 3.8 %gather_fusion.1 = f32[256,1024]{1,0:T(8,128)S(1)} fusion(f32[1024,1024]{1,0:T(8,128)} %bitcast.40, s32[1024]{0:T(1024)S(1)} %get-tuple-element.32), kind=kCustom, calls=%fused_computation.1 | custom fusion | bytes 2098176 | tf_op jit(solution)/shard_map/jit(_take)/gather | solution.py:88
  5.1 1.1 fusion
  6.1 1.0 fusion.1
  7.2 0.9 fusion.3
  8.1 0.9 fusion.4
  9.0 2.0 %fusion.19 = f32[256,1024]{1,0:T(8,128)} fusion(f32[256,1024]{1,0:T(8,128)S(1)} %fusion, f32[256,1024]{1,0:T(8,128)S(1)} %fusion.1, s32[1024]{0:T(1024)S(1)} %bitcast.53, f32[256,1024]{1,0:T(8,128)S(1)} %gather_fusion.1), kind=kOutput, calls=%fused_computation.41 | convolution fusion | flops 538968064 | bytes 4198400 | tf_op jit(solution)/shard_map/dot_general | solution.py:69
  11.0 1.7 %fusion.21 = f32[256,768]{1,0:T(8,128)} fusion(f32[256,768]{1,0:T(8,128)S(1)} %fusion.3, f32[256,768]{1,0:T(8,128)S(1)} %fusion.4, s32[768]{0:T(1024)S(1)} %eq.45, f32[256,1024]{1,0:T(8,128)S(1)} %gather_fusion.1), kind=kOutput, calls=%fused_computation.43 | convolution fusion | flops 404357120 | bytes 3410944 | tf_op jit(solution)/shard_map/dot_general | solution.py:69
  12.8 4.0 %collective-permute-start = (f32[256,1024]{1,0:T(8,128)}, f32[256,1024]{1,0:T(8,128)}, u32[]{:S(2)}, u32[]{:S(2)}) collective-permute-start(f32[256,1024]{1,0:T(8,128)} %fusion.19), channel_id=1, source_target_pairs={{0,4},{1,5},{2,6},{3,7},{4,0},{5,1},{6,2},{7,3},{8,12},{9,13},{10,... | collective-permute-start | bytes 3145736 | tf_op jit(solution)/shard_map/ppermute | solution.py:32
  16.8 1.5 %collective-permute-start.5 = (f32[256,768]{1,0:T(8,128)}, f32[256,768]{1,0:T(8,128)}, u32[]{:S(2)}, u32[]{:S(2)}) collective-permute-start(f32[256,768]{1,0:T(8,128)} %fusion.21), channel_id=1, source_target_pairs={{0,16},{8,24},{16,0},{24,8},{1,17},{9,25},{17,1},{25,9},{2,18},{10... | collective-permute-start | bytes 2359304 | tf_op jit(solution)/shard_map/ppermute | solution.py:32
  18.4 3.8 %gather_fusion.4 = f32[256,1024]{1,0:T(8,128)S(1)} fusion(f32[1024,1024]{1,0:T(8,128)} %bitcast.41, s32[1024]{0:T(1024)S(1)} %get-tuple-element.30), kind=kCustom, calls=%fused_computation.4 | custom fusion | bytes 2098176 | tf_op jit(solution)/shard_map/jit(_take)/gather | solution.py:76
  22.1 0.3 copy.5
  22.5 3.5 %gather_fusion.5 = f32[1024,256]{1,0:T(8,128)S(1)} fusion(f32[256,1024]{0,1:T(8,128)S(1)} %copy.5, s32[1024]{0:T(1024)S(1)} %get-tuple-element.33), kind=kCustom, calls=%fused_computation.5 | custom fusion | bytes 2101248 | tf_op jit(solution)/shard_map/jit(_take)/gather | solution.py:77
  25.9 0.3 copy.6
  26.3 0.6 collective-permute-start.3
  26.8 1.0 slice.156
  27.8 5.8 %gather_fusion.2 = f32[512,1024]{1,0:T(8,128)} fusion(f32[1024,1024]{1,0:T(8,128)} %bitcast.42, s32[1024]{0:T(1024)S(1)} %get-tuple-element.31), kind=kCustom, calls=%fused_computation.2 | custom fusion | bytes 4196352 | tf_op jit(solution)/shard_map/jit(_take)/gather | solution.py:76
  33.6 1.9 %copy.3 = f32[512,1024]{0,1:T(8,128)S(1)} copy(f32[512,1024]{1,0:T(8,128)} %gather_fusion.2) | data formatting | bytes 4194304 | tf_op jit(solution)/shard_map/jit(_take)/gather | solution.py:76
  35.5 4.9 %gather_fusion.3 = f32[1024,512]{1,0:T(8,128)} fusion(f32[512,1024]{0,1:T(8,128)S(1)} %copy.3, s32[1024]{0:T(1024)S(1)} %get-tuple-element.33), kind=kCustom, calls=%fused_computation.3 | custom fusion | bytes 4198400 | tf_op jit(solution)/shard_map/jit(_take)/gather | solution.py:77
  40.4 2.1 %copy.4 = f32[1024,512]{0,1:T(8,128)S(1)} copy(f32[1024,512]{1,0:T(8,128)} %gather_fusion.3) | data formatting | bytes 4194304 | tf_op jit(solution)/shard_map/jit(_take)/gather | solution.py:77
  42.5 1.3 slice.147
  43.8 0.1 fusion.79
  43.9 18.9 %collective-permute-done = f32[256,1024]{1,0:T(8,128)} collective-permute-done((f32[256,1024]{1,0:T(8,128)}, f32[256,1024]{1,0:T(8,128)}, u32[]{:S(2)}, u32[]{:S(2)}) %collective-permute-start) | collective-permute-done | bytes 1048608 | tf_op jit(solution)/shard_map/ppermute | solution.py:32
  62.8 1.2 slice.109
  64.0 1.1 select_reduce_fusion.1
  65.1 0.4 fusion.55
  65.6 0.5 convolution_subtract_fusion.3
  66.0 0.4 fusion.81
  66.4 0.4 convolution_subtract_fusion.2
  66.8 1.6 %collective-permute-start.4 = (f32[256,256]{1,0:T(8,128)S(1)}, f32[256,256]{1,0:T(8,128)S(1)}, u32[]{:S(2)}, u32[]{:S(2)}) collective-permute-start(f32[256,256]{1,0:T(8,128)S(1)} %convolution_subtract_fusion.2), channel_id=1, source_target_pairs={{0,16},{8,24},{16,0},{24,8},{1,17},{9,25},{17,1},{25,9},{2,18},{10... | collective-permute-start | bytes 786440 | tf_op jit(solution)/shard_map/ppermute | solution.py:32
  68.5 2.6 %convolution_negate_fusion.1 = f32[256,1536]{1,0:T(8,128)S(1)} fusion(f32[256,256]{1,0:T(8,128)S(1)} %convolution_subtract_fusion.2, f32[256,768]{1,0:T(8,128)S(1)} %slice.109, f32[256,768]{1,0:T(8,128)} %fusion.21), kind=kOutput, calls=%fused_computation.18 | convolution fusion | flops 1208745984 | bytes 3407872 | tf_op jit(solution)/shard_map/dot_general | solution.py:11
  71.0 1.2 slice.163
  72.2 0.5 collective-permute-start.6
  72.8 1.5 %convolution_add_fusion.1 = f32[256,1536]{1,0:T(8,128)S(1)} fusion(f32[256,1536]{1,0:T(8,128)S(1)} %convolution_negate_fusion.1, f32[256,768]{1,0:T(8,128)S(1)} %copy-done.3, f32[256,1024]{1,0:T(8,128)S(1)} %bitcast.46), kind=kOutput, calls=%fused_computation.16 | convolution fusion | flops 1208352768 | bytes 4194304 | tf_op jit(solution)/shard_map/dot_general | solution.py:11
  74.2 2.7 %convolution_add_fusion = f32[512,1536]{1,0:T(8,128)S(1)} fusion(f32[256,1536]{1,0:T(8,128)S(1)} %convolution_negate_fusion.1, f32[512,768]{1,0:T(8,128)S(1)} %copy-done.2, f32[512,1024]{1,0:T(8,128)S(1)} %bitcast.48), kind=kOutput, calls=%fused_computation.11 | convolution fusion | flops 2416705536 | bytes 6815744 | tf_op jit(solution)/shard_map/dot_general | solution.py:11
  77.0 0.5 broadcast.44.clone
  77.5 0.1 slice_dynamic-update-slice_fusion.1
  77.6 1.2 slice.161
  78.8 0.1 slice_dynamic-update-slice_fusion
  78.9 0.1 fusion.78
  78.9 9.1 %collective-permute-done.1 = f32[128,1024]{1,0:T(8,128)S(1)} collective-permute-done((f32[128,1024]{1,0:T(8,128)S(1)}, f32[128,1024]{1,0:T(8,128)S(1)}, u32[]{:S(2)}, u32[]{:S(2)}) %collective-permute-start.1) | collective-permute-done | bytes 524320 | tf_op jit(solution)/shard_map/ppermute | solution.py:32
  88.0 1.3 collective-permute-start.7
  89.4 3.4 %collective-permute-done.6 = f32[256,768]{1,0:T(8,128)S(1)} collective-permute-done((f32[256,768]{1,0:T(8,128)S(1)}, f32[256,768]{1,0:T(8,128)S(1)}, u32[]{:S(2)}, u32[]{:S(2)}) %collective-permute-start.6) | collective-permute-done | bytes 786464 | tf_op jit(solution)/shard_map/ppermute | solution.py:32
  92.8 2.0 %convolution_negate_fusion = f32[256,1536]{1,0:T(8,128)S(1)} fusion(f32[256,256]{1,0:T(8,128)S(1)} %collective-permute-done.4, f32[256,768]{1,0:T(8,128)S(1)} %collective-permute-done.6, f32[256,768]{1,0:T(8,128)} %collective-permute-done.5), kind=kOutput, calls=%fused_computation.17 | convolution fusion | flops 604766208 | bytes 3407872 | tf_op jit(solution)/shard_map/dot_general | solution.py:15
  94.7 1.8 %pad_add_fusion.1 = f32[256,1536]{1,0:T(8,128)S(1)} fusion(f32[256,768]{1,0:T(8,128)S(1)} %slice.161, f32[256,1536]{1,0:T(8,128)S(1)} %convolution_negate_fusion, f32[256,1024]{1,0:T(8,128)} %collective-permute-done.3), kind=kOutput, calls=%fused_computation.29 | convolution fusion | flops 604372992 | bytes 4194304 | tf_op jit(solution)/shard_map/dot_general | solution.py:15
  96.6 15.8 %collective-permute-done.2 = f32[128,1024]{1,0:T(8,128)S(1)} collective-permute-done((f32[128,1024]{1,0:T(8,128)S(1)}, f32[128,1024]{1,0:T(8,128)S(1)}, u32[]{:S(2)}, u32[]{:S(2)}) %collective-permute-start.2) | collective-permute-done | bytes 524320 | tf_op jit(solution)/shard_map/ppermute | solution.py:32
  112.5 1.0 collective-permute-start.8
  113.5 1.4 %pad_add_fusion.2 = f32[256,1536]{1,0:T(8,128)S(1)} fusion(f32[256,768]{1,0:T(8,128)S(1)} %slice.159, f32[256,1536]{1,0:T(8,128)S(1)} %convolution_negate_fusion.1, f32[256,1024]{1,0:T(8,128)S(1)} %constant_dynamic-update-slice_fusion), kind=kOutput, calls=%fused_computation.30 | convolution fusion | flops 1208352768 | bytes 4194304 | tf_op jit(solution)/shard_map/dot_general | solution.py:11
  115.0 0.7 broadcast.44.clone.1
  115.7 0.1 maximum_dynamic-update-slice_fusion.1
  115.8 0.1 fusion.24
  115.9 10.3 %collective-permute-done.8 = f32[128,1024]{1,0:T(8,128)S(1)} collective-permute-done((f32[128,1024]{1,0:T(8,128)S(1)}, f32[128,1024]{1,0:T(8,128)S(1)}, u32[]{:S(2)}, u32[]{:S(2)}) %collective-permute-start.8) | collective-permute-done | bytes 524320 | tf_op jit(solution)/shard_map/ppermute | solution.py:32
  126.2 0.1 slice.164
  126.3 0.8 pad_add_fusion
  127.1 0.1 maximum_dynamic-update-slice_fusion
  127.2 0.3 select_reduce_fusion
  127.6 1.1 fusion.32
  128.6 1.3 convolution_subtract_fusion.1
  129.9 1.0 fusion.82
  130.9 1.0 convolution_subtract_fusion
  131.9 1.0 fusion.28
  133.0 5.1 %subtract_bitcast_fusion = f32[1,1,512,2048]{3,2,1,0:T(8,128)} fusion(f32[512,2048]{1,0:T(8,128)S(1)} %slice_dynamic-update-slice_fusion, f32[512,512]{1,0:T(8,128)S(1)} %fusion.28, f32[512,2048]{1,0:T(8,128)S(1)} %get-tuple-element.23), kind=kOutput, calls=%fused_computation.6 | convolution fusion | flops 3222274048 | bytes 13631488 | tf_op jit(solution)/shard_map/dot_general | solution.py:15
  (29 shorter events, 0.3 us)
Async XLA Ops:
  0.0 0.7 copy-start
  12.8 50.0 %collective-permute-start = (f32[256,1024]{1,0:T(8,128)}, f32[256,1024]{1,0:T(8,128)}, u32[]{:S(2)}, u32[]{:S(2)}) collective-permute-start(f32[256,1024]{1,0:T(8,128)} %fusion.19), channel_id=1, source_target_pairs={{0,4},{1,5},{2,6},{3,7},{4,0},{5,1},{6,2},{7,3},{8,12},{9,13},{10,... | collective-permute-start | bytes 3145736 | tf_op jit(solution)/shard_map/ppermute | solution.py:32
  16.8 72.5 %collective-permute-start.5 = (f32[256,768]{1,0:T(8,128)}, f32[256,768]{1,0:T(8,128)}, u32[]{:S(2)}, u32[]{:S(2)}) collective-permute-start(f32[256,768]{1,0:T(8,128)} %fusion.21), channel_id=1, source_target_pairs={{0,16},{8,24},{16,0},{24,8},{1,17},{9,25},{17,1},{25,9},{2,18},{10... | collective-permute-start | bytes 2359304 | tf_op jit(solution)/shard_map/ppermute | solution.py:32
  26.3 51.3 %collective-permute-start.3 = (f32[256,1024]{1,0:T(8,128)S(1)}, f32[256,1024]{1,0:T(8,128)}, u32[]{:S(2)}, u32[]{:S(2)}) collective-permute-start(f32[256,1024]{1,0:T(8,128)S(1)} %bitcast.43), channel_id=1, source_target_pairs={{0,16},{8,24},{16,0},{24,8},{1,17},{9,25},{17,1},{25,9},{2,18},{10... | collective-permute-start | bytes 3145736 | tf_op jit(solution)/shard_map/ppermute | solution.py:32
  62.8 25.2 %collective-permute-start.1 = (f32[128,1024]{1,0:T(8,128)S(1)}, f32[128,1024]{1,0:T(8,128)S(1)}, u32[]{:S(2)}, u32[]{:S(2)}) collective-permute-start(f32[128,1024]{1,0:T(8,128)S(1)} %get-tuple-element.16), channel_id=1, source_target_pairs={{0,4},{1,5},{2,6},{3,7},{4,0},{5,1},{6,2},{7,3},{8,12},{9,13},{10,... | collective-permute-start | bytes 1572872 | tf_op jit(solution)/shard_map/ppermute | solution.py:32
  66.8 6.0 %copy-start.3 = (f32[256,768]{1,0:T(8,128)S(1)}, f32[256,768]{1,0:T(8,128)}, u32[]{:S(2)}) copy-start(f32[256,768]{1,0:T(8,128)} %slice.156) | copy-start | bytes 2359300
  66.8 22.5 %collective-permute-start.4 = (f32[256,256]{1,0:T(8,128)S(1)}, f32[256,256]{1,0:T(8,128)S(1)}, u32[]{:S(2)}, u32[]{:S(2)}) collective-permute-start(f32[256,256]{1,0:T(8,128)S(1)} %convolution_subtract_fusion.2), channel_id=1, source_target_pairs={{0,16},{8,24},{16,0},{24,8},{1,17},{9,25},{17,1},{25,9},{2,18},{10... | collective-permute-start | bytes 786440 | tf_op jit(solution)/shard_map/ppermute | solution.py:32
  72.2 2.0 %copy-start.2 = (f32[512,768]{1,0:T(8,128)S(1)}, f32[512,768]{1,0:T(8,128)}, u32[]{:S(2)}) copy-start(f32[512,768]{1,0:T(8,128)} %slice.147) | copy-start | bytes 4718596
  72.2 20.5 %collective-permute-start.6 = (f32[256,768]{1,0:T(8,128)S(1)}, f32[256,768]{1,0:T(8,128)S(1)}, u32[]{:S(2)}, u32[]{:S(2)}) collective-permute-start(f32[256,768]{1,0:T(8,128)S(1)} %slice.163), channel_id=1, source_target_pairs={{0,16},{8,24},{16,0},{24,8},{1,17},{9,25},{17,1},{25,9},{2,18},{10... | collective-permute-start | bytes 2359304 | tf_op jit(solution)/shard_map/ppermute | solution.py:32
  88.0 24.3 %collective-permute-start.2 = (f32[128,1024]{1,0:T(8,128)S(1)}, f32[128,1024]{1,0:T(8,128)S(1)}, u32[]{:S(2)}, u32[]{:S(2)}) collective-permute-start(f32[128,1024]{1,0:T(8,128)S(1)} %get-tuple-element.18), channel_id=1, source_target_pairs={{0,4},{1,5},{2,6},{3,7},{4,0},{5,1},{6,2},{7,3},{8,12},{9,13},{10,... | collective-permute-start | bytes 1572872 | tf_op jit(solution)/shard_map/ppermute | solution.py:32
  88.0 25.5 %collective-permute-start.7 = (f32[128,1024]{1,0:T(8,128)S(1)}, f32[128,1024]{1,0:T(8,128)S(1)}, u32[]{:S(2)}, u32[]{:S(2)}) collective-permute-start(f32[128,1024]{1,0:T(8,128)S(1)} %collective-permute-done.1), channel_id=1, source_target_pairs={{0,16},{8,24},{16,0},{24,8},{1,17},{9,25},{17,1},{25,9},{2,18},{10... | collective-permute-start | bytes 1572872 | tf_op jit(solution)/shard_map/ppermute | solution.py:32
  112.5 13.7 %collective-permute-start.8 = (f32[128,1024]{1,0:T(8,128)S(1)}, f32[128,1024]{1,0:T(8,128)S(1)}, u32[]{:S(2)}, u32[]{:S(2)}) collective-permute-start(f32[128,1024]{1,0:T(8,128)S(1)} %collective-permute-done.2), channel_id=1, source_target_pairs={{0,16},{8,24},{16,0},{24,8},{1,17},{9,25},{17,1},{25,9},{2,18},{10... | collective-permute-start | bytes 1572872 | tf_op jit(solution)/shard_map/ppermute | solution.py:32
  133.0 5.1 %copy-start.1 = (s32[1,1,4,256]{3,2,1,0:T(4,128)S(1)}, s32[1,1,4,256]{3,2,1,0:T(4,128)}, u32[]{:S(2)}) copy-start(s32[1,1,4,256]{3,2,1,0:T(4,128)} %param.3) | copy-start | bytes 12292

commit v7 on v5

--- a/solution.py
+++ b/solution.py
@@ -83,14 +83,14 @@
     diag_ie = swap(side_i1[:, width:], "grp")
     inverse_own = newton(own_i1[:, :width] + side_i1[:, :width], ITERS_LOW)
     inverse_other = swap(inverse_own, "grp")
-    first_half, side_i1 = lax.optimization_barrier((own_i2[:half], side_i1))
-    side_first = swap(first_half, "box")
-    diag_first = swap(side_first, "grp")
-    second_half, side_first = lax.optimization_barrier((own_i2[half:], side_first))
-    side_second = swap(second_half, "box")
-    diag_second = swap(side_second, "grp")
-    side_i2 = jnp.concatenate([side_first, side_second], 0)
-    diag_i2 = jnp.concatenate([diag_first, diag_second], 0)
+    own_a = jnp.concatenate([own_i2[:, :width], own_i2[:, 3 * width :]], 1)
+    part_a, side_i1 = lax.optimization_barrier((own_a, side_i1))
+    side_a = swap(part_a, "box")
+    diag_a = swap(side_a, "grp")
+    part_b, side_a = lax.optimization_barrier((own_i2[:, width : 3 * width], side_a))
+    side_b = swap(part_b, "box")
+    diag_b = swap(side_b, "grp")
+    side_i2 = jnp.concatenate([side_a[:, :width], side_b, side_a[:, width:]], 1)
 
     solved_own = pair_solve(inverse_own, own_i1[:, width:], side_i1[:, width:])
     own_ext = first_rows(own_ov, solved_own, width)
@@ -99,19 +99,24 @@
 
     solved_other = pair_solve(inverse_other, vert_ie, diag_ie, matmul_high)
     vert_int = first_rows(vert_i2, solved_other, width, matmul_high)
-    diag_int = second_rows(diag_i2, solved_other, width, matmul_high)
+    diag_prod = matmul_high(diag_a[:, :width], solved_other)
+    diag_inner = jnp.concatenate(
+        [diag_prod[:, 2 * width : 3 * width], diag_prod[:, 5 * width :] + diag_a[:, width:]], 1
+    )
 
     near = jnp.concatenate([own_int, side_int], 0)
-    far = jnp.concatenate([vert_int, diag_int], 0)
-    system_two = int_cols(near, width) + int_cols(far, width)
+    far_int = jnp.concatenate([int_cols(vert_int, width), diag_inner], 0)
+    system_two = int_cols(near, width) + far_int
     inverse_two = newton(system_two, ITERS_HIGH, matmul_high)
     weights = matmul_high(int_cols(own_ext, width), inverse_two)
     own_id = 2 * upper + right
     blocks = [
         near[:, 0 : 2 * width],
         near[:, 3 * width : 5 * width],
-        far[:, 0 : 2 * width],
-        far[:, 3 * width : 5 * width],
+        jnp.concatenate([vert_int[:, 0 : 2 * width], diag_prod[:, 0 : 2 * width]], 0),
+        jnp.concatenate(
+            [vert_int[:, 3 * width : 5 * width], diag_prod[:, 3 * width : 5 * width] + diag_b], 0
+        ),
     ]
     coupling_two = jnp.zeros((2 * width, 8 * width), jnp.float32)
     for rel, block in enumerate(blocks):

time: 136 us -> 140 us (1.029)
  waiting for transfers between devices: 55.3 us -> 58.1 us
    ppermute x9, waiting for transfers between devices: 55.3 us -> 58.1 us  [swap(): return lax.ppermute(value, axis, pairs)]
  transfers between devices with their start and end apart: 9 -> 9, of which waited for: 5 -> 4; matrix products, arithmetic and copies ran while one was open for 35% -> 36% of each run, Pallas kernels for 0% -> 0%
where the time goes in v7:
time: 140 us
  waiting for transfers between devices  58.1 us (42%)
  local copies, waits for them, and re-layouts  43.2 us (31%)
  matrix products  25.6 us (18%)
  starting transfers between devices  10.2 us (7%)
  other arithmetic  2.28 us (2%)
    ppermute x9, waiting for transfers between devices, swap(): return lax.ppermute(value, axis, pairs)  58.1 us
    gather x6, local copies, waits for them, and re-layouts, pick(): picked = jnp.take(matrix, rows, axis=0, mode='clip')  15.9 us
    dot_general x9, matrix products, matmul_high(): jnp.dot(left, right, precision=lax.Precision.HIGH, preferred_element_type...  15.6 us
    gather x6, local copies, waits for them, and re-layouts, pick(): return jnp.take(picked, cols, axis=1, mode='clip')  15.6 us
    ppermute x9, starting transfers between devices, swap(): return lax.ppermute(value, axis, pairs)  10.2 us
    dot_general x8, matrix products, matmul(): jnp.dot(left, right, precision=lax.Precision.HIGHEST, preferred_element_t...  10 us
    slice x3, local copies, waits for them, and re-layouts, first_rows(): rows[:, width:]  3.48 us
    slice x2, local copies, waits for them, and re-layouts, body(): solved_own = pair_solve(inverse_own, own_i1[:, width:], side_i1[:, width:])  3.3 us
  transfers between devices with their start and end apart: 9, of which 4 were waited for; matrix products, arithmetic and copies ran while one was open for 36% of the time, Pallas kernels for 0%

profile of v7, /device:TPU:0, one launch (start us, length us, event | category | flops | bytes accessed | tf_op | source)
XLA Modules:
  0.0 139.9 jit_solution(16340074246081208092)
XLA Ops:
  0.0 0.1 pad_add_fusion.1
  0.1 0.6 copy-done
  0.7 0.6 gather_fusion
  1.3 3.8 %gather_fusion.1 = f32[256,1024]{1,0:T(8,128)S(1)} fusion(f32[1024,1024]{1,0:T(8,128)} %bitcast.41, s32[1024]{0:T(1024)S(1)} %pad_clamp_fusion.2), kind=kCustom, calls=%fused_computation.1 | custom fusion | bytes 2098176 | tf_op jit(solution)/shard_map/jit(_take)/gather | solution.py:62
  5.1 0.3 copy.3
  5.4 3.5 %gather_fusion.2 = f32[1024,256]{1,0:T(8,128)S(1)} fusion(f32[256,1024]{0,1:T(8,128)S(1)} %copy.3, s32[1024]{0:T(1024)S(1)} %broadcast_clamp_fusion), kind=kCustom, calls=%fused_computation.2 | custom fusion | bytes 2101248 | tf_op jit(solution)/shard_map/jit(_take)/gather | solution.py:63
  8.9 1.3 copy.4
  10.2 4.0 %collective-permute-start = (f32[256,1024]{1,0:T(8,128)}, f32[256,1024]{1,0:T(8,128)}, u32[]{:S(2)}, u32[]{:S(2)}) collective-permute-start(f32[256,1024]{1,0:T(8,128)} %bitcast.7), channel_id=1, source_target_pairs={{0,4},{1,5},{2,6},{3,7},{4,0},{5,1},{6,2},{7,3},{8,12},{9,13},{10,... | collective-permute-start | bytes 3145736 | tf_op jit(solution)/shard_map/ppermute | solution.py:32
  14.3 2.1 %slice.119 = f32[256,768]{1,0:T(8,128)} slice(f32[256,1024]{1,0:T(8,128)} %bitcast.7), slice={[0:256], [256:1024]} | slice | bytes 1572864 | tf_op jit(solution)/shard_map/slice | solution.py:95
  16.4 1.5 %collective-permute-start.5 = (f32[256,768]{1,0:T(8,128)}, f32[256,768]{1,0:T(8,128)}, u32[]{:S(2)}, u32[]{:S(2)}) collective-permute-start(f32[256,768]{1,0:T(8,128)} %slice.119), channel_id=1, source_target_pairs={{0,16},{8,24},{16,0},{24,8},{1,17},{9,25},{17,1},{25,9},{2,18},{10... | collective-permute-start | bytes 2359304 | tf_op jit(solution)/shard_map/ppermute | solution.py:32
  17.9 3.8 %gather_fusion.5 = f32[256,1024]{1,0:T(8,128)S(1)} fusion(f32[1024,1024]{1,0:T(8,128)} %bitcast.42, s32[1024]{0:T(1024)S(1)} %pad_clamp_fusion), kind=kCustom, calls=%fused_computation.5 | custom fusion | bytes 2098176 | tf_op jit(solution)/shard_map/jit(_take)/gather | solution.py:62
  21.7 0.3 copy.7
  22.0 3.5 %gather_fusion.6 = f32[1024,256]{1,0:T(8,128)S(1)} fusion(f32[256,1024]{0,1:T(8,128)S(1)} %copy.7, s32[1024]{0:T(1024)S(1)} %broadcast_clamp_fusion), kind=kCustom, calls=%fused_computation.6 | custom fusion | bytes 2101248 | tf_op jit(solution)/shard_map/jit(_take)/gather | solution.py:63
  25.5 0.3 copy.8
  25.8 0.6 collective-permute-start.3
  26.4 0.8 slice.176
  27.2 1.0 slice.175
  28.2 5.8 %gather_fusion.3 = f32[512,1024]{1,0:T(8,128)} fusion(f32[1024,1024]{1,0:T(8,128)} %bitcast.43, s32[1024]{0:T(1024)S(1)} %pad_clamp_fusion.1), kind=kCustom, calls=%fused_computation.3 | custom fusion | bytes 4196352 | tf_op jit(solution)/shard_map/jit(_take)/gather | solution.py:62
  34.0 1.9 %copy.5 = f32[512,1024]{0,1:T(8,128)S(1)} copy(f32[512,1024]{1,0:T(8,128)} %gather_fusion.3) | data formatting | bytes 4194304 | tf_op jit(solution)/shard_map/jit(_take)/gather | solution.py:62
  35.9 4.9 %gather_fusion.4 = f32[1024,512]{1,0:T(8,128)} fusion(f32[512,1024]{0,1:T(8,128)S(1)} %copy.5, s32[1024]{0:T(1024)S(1)} %broadcast_clamp_fusion), kind=kCustom, calls=%fused_computation.4 | custom fusion | bytes 4198400 | tf_op jit(solution)/shard_map/jit(_take)/gather | solution.py:63
  40.8 2.1 %copy.6 = f32[1024,512]{0,1:T(8,128)S(1)} copy(f32[1024,512]{1,0:T(8,128)} %gather_fusion.4) | data formatting | bytes 4194304 | tf_op jit(solution)/shard_map/jit(_take)/gather | solution.py:63
  42.9 1.3 slice.165
  44.3 15.9 %collective-permute-done = f32[256,1024]{1,0:T(8,128)} collective-permute-done((f32[256,1024]{1,0:T(8,128)}, f32[256,1024]{1,0:T(8,128)}, u32[]{:S(2)}, u32[]{:S(2)}) %collective-permute-start) | collective-permute-done | bytes 1048608 | tf_op jit(solution)/shard_map/ppermute | solution.py:32
  60.2 1.1 select_reduce_fusion.1
  61.4 0.4 fusion.33
  61.8 0.5 convolution_subtract_fusion.3
  62.3 0.4 fusion.61
  62.7 0.4 convolution_subtract_fusion.2
  63.0 1.6 %collective-permute-start.4 = (f32[256,256]{1,0:T(8,128)S(1)}, f32[256,256]{1,0:T(8,128)S(1)}, u32[]{:S(2)}, u32[]{:S(2)}) collective-permute-start(f32[256,256]{1,0:T(8,128)S(1)} %convolution_subtract_fusion.2), channel_id=1, source_target_pairs={{0,16},{8,24},{16,0},{24,8},{1,17},{9,25},{17,1},{25,9},{2,18},{10... | collective-permute-start | bytes 786440 | tf_op jit(solution)/shard_map/ppermute | solution.py:32
  64.7 1.2 slice.123
  65.9 1.2 slice.179
  67.1 0.5 collective-permute-start.6
  67.6 2.6 %convolution_negate_fusion.1 = f32[256,1536]{1,0:T(8,128)S(1)} fusion(f32[256,256]{1,0:T(8,128)S(1)} %convolution_subtract_fusion.2, f32[256,768]{1,0:T(8,128)S(1)} %slice.123, f32[256,768]{1,0:T(8,128)} %slice.119), kind=kOutput, calls=%fused_computation.11 | convolution fusion | flops 1208745984 | bytes 3407872 | tf_op jit(solution)/shard_map/dot_general | solution.py:11
  70.2 2.8 %convolution_add_fusion = f32[512,1536]{1,0:T(8,128)S(1)} fusion(f32[256,1536]{1,0:T(8,128)S(1)} %convolution_negate_fusion.1, f32[512,768]{1,0:T(8,128)S(1)} %copy-done.2, f32[512,1024]{1,0:T(8,128)S(1)} %bitcast.50), kind=kOutput, calls=%fused_computation.8 | convolution fusion | flops 2416705536 | bytes 6815744 | tf_op jit(solution)/shard_map/dot_general | solution.py:11
  73.1 1.3 slice.177
  74.3 0.1 copy-done.3
  74.4 1.5 %convolution_add_fusion.1 = f32[256,1536]{1,0:T(8,128)S(1)} fusion(f32[256,1536]{1,0:T(8,128)S(1)} %convolution_negate_fusion.1, f32[256,768]{1,0:T(8,128)S(1)} %copy-done.3, f32[256,1024]{1,0:T(8,128)S(1)} %bitcast.48), kind=kOutput, calls=%fused_computation.9 | convolution fusion | flops 1208352768 | bytes 4194304 | tf_op jit(solution)/shard_map/dot_general | solution.py:11
  75.9 0.5 broadcast.42.clone.1
  76.4 0.1 slice_dynamic-update-slice_fusion.1
  76.5 0.1 fusion.55
  76.6 12.8 %collective-permute-done.1 = f32[256,512]{1,0:T(8,128)S(1)} collective-permute-done((f32[256,512]{1,0:T(8,128)S(1)}, f32[256,512]{1,0:T(8,128)S(1)}, u32[]{:S(2)}, u32[]{:S(2)}) %collective-permute-start.1) | collective-permute-done | bytes 524320 | tf_op jit(solution)/shard_map/ppermute | solution.py:32
  89.4 0.1 collective-permute-start.2
  89.5 0.8 collective-permute-start.7
  90.3 2.0 %convolution_negate_fusion = f32[256,1536]{1,0:T(8,128)S(1)} fusion(f32[256,256]{1,0:T(8,128)S(1)} %collective-permute-done.4, f32[256,768]{1,0:T(8,128)S(1)} %collective-permute-done.6, f32[256,768]{1,0:T(8,128)} %collective-permute-done.5), kind=kOutput, calls=%fused_computation.10 | convolution fusion | flops 604766208 | bytes 3407872 | tf_op jit(solution)/shard_map/dot_general | solution.py:15
  92.3 1.8 %pad_add_fusion = f32[256,1536]{1,0:T(8,128)S(1)} fusion(f32[256,768]{1,0:T(8,128)S(1)} %slice.177, f32[256,1536]{1,0:T(8,128)S(1)} %convolution_negate_fusion, f32[256,1024]{1,0:T(8,128)} %collective-permute-done.3), kind=kOutput, calls=%fused_computation.19 | convolution fusion | flops 604372992 | bytes 4194304 | tf_op jit(solution)/shard_map/dot_general | solution.py:15
  94.1 0.2 fusion.56
  94.3 19.2 %collective-permute-done.2 = f32[256,512]{1,0:T(8,128)S(1)} collective-permute-done((f32[256,512]{1,0:T(8,128)S(1)}, f32[256,512]{1,0:T(8,128)S(1)}, u32[]{:S(2)}, u32[]{:S(2)}) %collective-permute-start.2) | collective-permute-done | bytes 524320 | tf_op jit(solution)/shard_map/ppermute | solution.py:32
  113.5 1.5 %maximum_add_fusion = f32[256,1536]{1,0:T(8,128)S(1)} fusion(f32[256,256]{1,0:T(8,128)S(1)} %slice.130, f32[256,512]{1,0:T(8,128)S(1)} %collective-permute-done.2, f32[1536]{0:T(1024)S(1)} %pad.17.clone, f32[256,1536]{1,0:T(8,128)S(1)} %convolution_negate_fusion.1, f32[256,512]{1,0:T(8,128)S(1)} %collective-permute-done.1), kind=kOutput, calls=%fused_computation.15 | convolution fusion | flops 1209139200 | bytes 4202496 | tf_op jit(solution)/shard_map/dot_general | solution.py:11
  115.0 0.7 broadcast.42.clone
  115.7 0.1 maximum_dynamic-update-slice_fusion
  115.8 0.8 fusion.23
  116.6 0.1 fusion.58
  116.7 0.5 select_reduce_fusion
  117.2 1.1 fusion.13
  118.3 1.3 convolution_subtract_fusion.1
  119.6 1.0 fusion.62
  120.7 1.1 collective-permute-start.8
  121.7 1.0 convolution_subtract_fusion
  122.8 1.0 fusion.9
  123.8 10.2 %collective-permute-done.8 = f32[256,512]{1,0:T(8,128)S(1)} collective-permute-done((f32[256,512]{1,0:T(8,128)S(1)}, f32[256,512]{1,0:T(8,128)S(1)}, u32[]{:S(2)}, u32[]{:S(2)}) %collective-permute-start.8) | collective-permute-done | bytes 524320 | tf_op jit(solution)/shard_map/ppermute | solution.py:32
  134.0 0.1 slice_add_fusion
  134.1 0.1 maximum_dynamic-update-slice_fusion.1
  134.3 0.1 maximum_dynamic-update-slice_fusion.2
  134.4 5.5 %subtract_bitcast_fusion = f32[1,1,512,2048]{3,2,1,0:T(8,128)} fusion(f32[512,2048]{1,0:T(8,128)S(1)} %get-tuple-element.36, f32[512,512]{1,0:T(8,128)S(1)} %fusion.9, f32[512,2048]{1,0:T(8,128)S(1)} %maximum_dynamic-update-slice_fusion.2), kind=kOutput, calls=%fused_computation.7 | convolution fusion | flops 3222274048 | bytes 13631488 | tf_op jit(solution)/shard_map/dot_general | solution.py:15
  (31 shorter events, 0.3 us)
Async XLA Ops:
  0.0 0.7 copy-start
  10.2 50.0 %collective-permute-start = (f32[256,1024]{1,0:T(8,128)}, f32[256,1024]{1,0:T(8,128)}, u32[]{:S(2)}, u32[]{:S(2)}) collective-permute-start(f32[256,1024]{1,0:T(8,128)} %bitcast.7), channel_id=1, source_target_pairs={{0,4},{1,5},{2,6},{3,7},{4,0},{5,1},{6,2},{7,3},{8,12},{9,13},{10,... | collective-permute-start | bytes 3145736 | tf_op jit(solution)/shard_map/ppermute | solution.py:32
  16.4 73.9 %collective-permute-start.5 = (f32[256,768]{1,0:T(8,128)}, f32[256,768]{1,0:T(8,128)}, u32[]{:S(2)}, u32[]{:S(2)}) collective-permute-start(f32[256,768]{1,0:T(8,128)} %slice.119), channel_id=1, source_target_pairs={{0,16},{8,24},{16,0},{24,8},{1,17},{9,25},{17,1},{25,9},{2,18},{10... | collective-permute-start | bytes 2359304 | tf_op jit(solution)/shard_map/ppermute | solution.py:32
  25.8 47.2 %collective-permute-start.3 = (f32[256,1024]{1,0:T(8,128)S(1)}, f32[256,1024]{1,0:T(8,128)}, u32[]{:S(2)}, u32[]{:S(2)}) collective-permute-start(f32[256,1024]{1,0:T(8,128)S(1)} %bitcast.44), channel_id=1, source_target_pairs={{0,16},{8,24},{16,0},{24,8},{1,17},{9,25},{17,1},{25,9},{2,18},{10... | collective-permute-start | bytes 3145736 | tf_op jit(solution)/shard_map/ppermute | solution.py:32
  63.0 27.2 %collective-permute-start.4 = (f32[256,256]{1,0:T(8,128)S(1)}, f32[256,256]{1,0:T(8,128)S(1)}, u32[]{:S(2)}, u32[]{:S(2)}) collective-permute-start(f32[256,256]{1,0:T(8,128)S(1)} %convolution_subtract_fusion.2), channel_id=1, source_target_pairs={{0,16},{8,24},{16,0},{24,8},{1,17},{9,25},{17,1},{25,9},{2,18},{10... | collective-permute-start | bytes 786440 | tf_op jit(solution)/shard_map/ppermute | solution.py:32
  64.7 24.7 %collective-permute-start.1 = (f32[256,512]{1,0:T(8,128)S(1)}, f32[256,512]{1,0:T(8,128)S(1)}, u32[]{:S(2)}, u32[]{:S(2)}) collective-permute-start(f32[256,512]{1,0:T(8,128)S(1)} %pad_maximum_fusion.1), channel_id=1, source_target_pairs={{0,4},{1,5},{2,6},{3,7},{4,0},{5,1},{6,2},{7,3},{8,12},{9,13},{10,... | collective-permute-start | bytes 1572872 | tf_op jit(solution)/shard_map/ppermute | solution.py:32
  67.1 3.1 %copy-start.2 = (f32[512,768]{1,0:T(8,128)S(1)}, f32[512,768]{1,0:T(8,128)}, u32[]{:S(2)}) copy-start(f32[512,768]{1,0:T(8,128)} %slice.165) | copy-start | bytes 4718596
  67.1 23.2 %collective-permute-start.6 = (f32[256,768]{1,0:T(8,128)S(1)}, f32[256,768]{1,0:T(8,128)S(1)}, u32[]{:S(2)}, u32[]{:S(2)}) collective-permute-start(f32[256,768]{1,0:T(8,128)S(1)} %slice.179), channel_id=1, source_target_pairs={{0,16},{8,24},{16,0},{24,8},{1,17},{9,25},{17,1},{25,9},{2,18},{10... | collective-permute-start | bytes 2359304 | tf_op jit(solution)/shard_map/ppermute | solution.py:32
  73.0 1.4 copy-start.3
  76.5 12.9 %copy-start.4 = (f32[256,512]{1,0:T(8,128)S(1)}, f32[256,512]{1,0:T(8,128)}, u32[]{:S(2)}) copy-start(f32[256,512]{1,0:T(8,128)} %slice.176) | copy-start | bytes 1572868
  89.4 24.1 %collective-permute-start.2 = (f32[256,512]{1,0:T(8,128)S(1)}, f32[256,512]{1,0:T(8,128)S(1)}, u32[]{:S(2)}, u32[]{:S(2)}) collective-permute-start(f32[256,512]{1,0:T(8,128)S(1)} %copy-done.4), channel_id=1, source_target_pairs={{0,4},{1,5},{2,6},{3,7},{4,0},{5,1},{6,2},{7,3},{8,12},{9,13},{10,... | collective-permute-start | bytes 1572872 | tf_op jit(solution)/shard_map/ppermute | solution.py:32
  89.5 26.3 %collective-permute-start.7 = (f32[256,512]{1,0:T(8,128)S(1)}, f32[256,512]{1,0:T(8,128)S(1)}, u32[]{:S(2)}, u32[]{:S(2)}) collective-permute-start(f32[256,512]{1,0:T(8,128)S(1)} %collective-permute-done.1), channel_id=1, source_target_pairs={{0,16},{8,24},{16,0},{24,8},{1,17},{9,25},{17,1},{25,9},{2,18},{10... | collective-permute-start | bytes 1572872 | tf_op jit(solution)/shard_map/ppermute | solution.py:32
  120.7 13.3 %collective-permute-start.8 = (f32[256,512]{1,0:T(8,128)S(1)}, f32[256,512]{1,0:T(8,128)S(1)}, u32[]{:S(2)}, u32[]{:S(2)}) collective-permute-start(f32[256,512]{1,0:T(8,128)S(1)} %collective-permute-done.2), channel_id=1, source_target_pairs={{0,16},{8,24},{16,0},{24,8},{1,17},{9,25},{17,1},{25,9},{2,18},{10... | collective-permute-start | bytes 1572872 | tf_op jit(solution)/shard_map/ppermute | solution.py:32
  134.4 5.5 %copy-start.1 = (s32[1,1,4,256]{3,2,1,0:T(4,128)S(1)}, s32[1,1,4,256]{3,2,1,0:T(4,128)}, u32[]{:S(2)}) copy-start(s32[1,1,4,256]{3,2,1,0:T(4,128)} %param.3) | copy-start | bytes 12292

commit v8 on v7

--- a/solution.py
+++ b/solution.py
@@ -89,7 +89,6 @@
     diag_a = swap(side_a, "grp")
     part_b, side_a = lax.optimization_barrier((own_i2[:, width : 3 * width], side_a))
     side_b = swap(part_b, "box")
-    diag_b = swap(side_b, "grp")
     side_i2 = jnp.concatenate([side_a[:, :width], side_b, side_a[:, width:]], 1)
 
     solved_own = pair_solve(inverse_own, own_i1[:, width:], side_i1[:, width:])
@@ -107,6 +106,8 @@
     near = jnp.concatenate([own_int, side_int], 0)
     far_int = jnp.concatenate([int_cols(vert_int, width), diag_inner], 0)
     system_two = int_cols(near, width) + far_int
+    system_two, side_b = lax.optimization_barrier((system_two, side_b))
+    diag_b = swap(side_b, "grp")
     inverse_two = newton(system_two, ITERS_HIGH, matmul_high)
     weights = matmul_high(int_cols(own_ext, width), inverse_two)
     own_id = 2 * upper + right

time: 140 us -> 139 us (level)
  waiting for transfers between devices: 58.1 us -> 56.2 us
    ppermute x9, waiting for transfers between devices: 58.1 us -> 56.2 us  [swap(): return lax.ppermute(value, axis, pairs)]
  transfers between devices with their start and end apart: 9 -> 9, of which waited for: 4 -> 4; matrix products, arithmetic and copies ran while one was open for 36% -> 39% of each run, Pallas kernels for 0% -> 0%
where the time goes in v8:
time: 139 us; the launch traced here: 138 us
  waiting for transfers between devices  56.2 us (40%)
  local copies, waits for them, and re-layouts  43.1 us (31%)
  matrix products  25.4 us (18%)
  starting transfers between devices  10.7 us (8%)
  other arithmetic  2.26 us (2%)
    ppermute x9, waiting for transfers between devices, swap(): return lax.ppermute(value, axis, pairs)  56.2 us
    gather x6, local copies, waits for them, and re-layouts, pick(): picked = jnp.take(matrix, rows, axis=0, mode='clip')  15.9 us
    gather x6, local copies, waits for them, and re-layouts, pick(): return jnp.take(picked, cols, axis=1, mode='clip')  15.6 us
    dot_general x9, matrix products, matmul_high(): jnp.dot(left, right, precision=lax.Precision.HIGH, preferred_element_type...  15.4 us
    ppermute x9, starting transfers between devices, swap(): return lax.ppermute(value, axis, pairs)  10.7 us
    dot_general x8, matrix products, matmul(): jnp.dot(left, right, precision=lax.Precision.HIGHEST, preferred_element_t...  10 us
    slice x3, local copies, waits for them, and re-layouts, first_rows(): rows[:, width:]  3.41 us
    slice x2, local copies, waits for them, and re-layouts, body(): solved_own = pair_solve(inverse_own, own_i1[:, width:], side_i1[:, width:])  3.3 us
  transfers between devices with their start and end apart: 9, of which 4 were waited for; matrix products, arithmetic and copies ran while one was open for 39% of the time, Pallas kernels for 0%

profile of v8, /device:TPU:0, one launch (start us, length us, event | category | flops | bytes accessed | tf_op | source)
XLA Modules:
  0.0 138.2 jit_solution(9295616486774632753)
XLA Ops:
  0.0 0.1 pad_add_fusion.1
  0.1 0.6 copy-done
  0.7 0.6 gather_fusion
  1.3 3.8 %gather_fusion.1 = f32[256,1024]{1,0:T(8,128)S(1)} fusion(f32[1024,1024]{1,0:T(8,128)} %bitcast.41, s32[1024]{0:T(1024)S(1)} %pad_clamp_fusion.2), kind=kCustom, calls=%fused_computation.1 | custom fusion | bytes 2098176 | tf_op jit(solution)/shard_map/jit(_take)/gather | solution.py:62
  5.0 0.3 copy.3
  5.4 3.5 %gather_fusion.2 = f32[1024,256]{1,0:T(8,128)S(1)} fusion(f32[256,1024]{0,1:T(8,128)S(1)} %copy.3, s32[1024]{0:T(1024)S(1)} %broadcast_clamp_fusion), kind=kCustom, calls=%fused_computation.2 | custom fusion | bytes 2101248 | tf_op jit(solution)/shard_map/jit(_take)/gather | solution.py:63
  8.9 1.3 copy.4
  10.2 4.0 %collective-permute-start = (f32[256,1024]{1,0:T(8,128)}, f32[256,1024]{1,0:T(8,128)}, u32[]{:S(2)}, u32[]{:S(2)}) collective-permute-start(f32[256,1024]{1,0:T(8,128)} %bitcast.7), channel_id=1, source_target_pairs={{0,4},{1,5},{2,6},{3,7},{4,0},{5,1},{6,2},{7,3},{8,12},{9,13},{10,... | collective-permute-start | bytes 3145736 | tf_op jit(solution)/shard_map/ppermute | solution.py:32
  14.3 2.1 %slice.119 = f32[256,768]{1,0:T(8,128)} slice(f32[256,1024]{1,0:T(8,128)} %bitcast.7), slice={[0:256], [256:1024]} | slice | bytes 1572864 | tf_op jit(solution)/shard_map/slice | solution.py:94
  16.4 1.5 %collective-permute-start.5 = (f32[256,768]{1,0:T(8,128)}, f32[256,768]{1,0:T(8,128)}, u32[]{:S(2)}, u32[]{:S(2)}) collective-permute-start(f32[256,768]{1,0:T(8,128)} %slice.119), channel_id=1, source_target_pairs={{0,16},{8,24},{16,0},{24,8},{1,17},{9,25},{17,1},{25,9},{2,18},{10... | collective-permute-start | bytes 2359304 | tf_op jit(solution)/shard_map/ppermute | solution.py:32
  17.9 3.8 %gather_fusion.5 = f32[256,1024]{1,0:T(8,128)S(1)} fusion(f32[1024,1024]{1,0:T(8,128)} %bitcast.42, s32[1024]{0:T(1024)S(1)} %pad_clamp_fusion), kind=kCustom, calls=%fused_computation.5 | custom fusion | bytes 2098176 | tf_op jit(solution)/shard_map/jit(_take)/gather | solution.py:62
  21.7 0.3 copy.7
  22.0 3.5 %gather_fusion.6 = f32[1024,256]{1,0:T(8,128)S(1)} fusion(f32[256,1024]{0,1:T(8,128)S(1)} %copy.7, s32[1024]{0:T(1024)S(1)} %broadcast_clamp_fusion), kind=kCustom, calls=%fused_computation.6 | custom fusion | bytes 2101248 | tf_op jit(solution)/shard_map/jit(_take)/gather | solution.py:63
  25.5 0.3 copy.8
  25.8 0.6 collective-permute-start.3
  26.4 0.8 slice.176
  27.2 1.0 slice.175
  28.2 5.8 %gather_fusion.3 = f32[512,1024]{1,0:T(8,128)} fusion(f32[1024,1024]{1,0:T(8,128)} %bitcast.43, s32[1024]{0:T(1024)S(1)} %pad_clamp_fusion.1), kind=kCustom, calls=%fused_computation.3 | custom fusion | bytes 4196352 | tf_op jit(solution)/shard_map/jit(_take)/gather | solution.py:62
  34.0 1.9 %copy.5 = f32[512,1024]{0,1:T(8,128)S(1)} copy(f32[512,1024]{1,0:T(8,128)} %gather_fusion.3) | data formatting | bytes 4194304 | tf_op jit(solution)/shard_map/jit(_take)/gather | solution.py:62
  35.9 4.9 %gather_fusion.4 = f32[1024,512]{1,0:T(8,128)} fusion(f32[512,1024]{0,1:T(8,128)S(1)} %copy.5, s32[1024]{0:T(1024)S(1)} %broadcast_clamp_fusion), kind=kCustom, calls=%fused_computation.4 | custom fusion | bytes 4198400 | tf_op jit(solution)/shard_map/jit(_take)/gather | solution.py:63
  40.8 2.1 %copy.6 = f32[1024,512]{0,1:T(8,128)S(1)} copy(f32[1024,512]{1,0:T(8,128)} %gather_fusion.4) | data formatting | bytes 4194304 | tf_op jit(solution)/shard_map/jit(_take)/gather | solution.py:63
  42.9 1.3 slice.165
  44.3 15.9 %collective-permute-done = f32[256,1024]{1,0:T(8,128)} collective-permute-done((f32[256,1024]{1,0:T(8,128)}, f32[256,1024]{1,0:T(8,128)}, u32[]{:S(2)}, u32[]{:S(2)}) %collective-permute-start) | collective-permute-done | bytes 1048608 | tf_op jit(solution)/shard_map/ppermute | solution.py:32
  60.2 1.1 select_reduce_fusion.1
  61.4 0.4 fusion.33
  61.8 0.5 convolution_subtract_fusion.3
  62.3 0.4 fusion.60
  62.7 0.4 convolution_subtract_fusion.2
  63.0 1.6 %collective-permute-start.4 = (f32[256,256]{1,0:T(8,128)S(1)}, f32[256,256]{1,0:T(8,128)S(1)}, u32[]{:S(2)}, u32[]{:S(2)}) collective-permute-start(f32[256,256]{1,0:T(8,128)S(1)} %convolution_subtract_fusion.2), channel_id=1, source_target_pairs={{0,16},{8,24},{16,0},{24,8},{1,17},{9,25},{17,1},{25,9},{2,18},{10... | collective-permute-start | bytes 786440 | tf_op jit(solution)/shard_map/ppermute | solution.py:32
  64.7 1.2 slice.179
  65.9 0.5 collective-permute-start.6
  66.4 1.2 slice.123
  67.6 2.7 %convolution_negate_fusion.1 = f32[256,1536]{1,0:T(8,128)S(1)} fusion(f32[256,256]{1,0:T(8,128)S(1)} %convolution_subtract_fusion.2, f32[256,768]{1,0:T(8,128)S(1)} %slice.123, f32[256,768]{1,0:T(8,128)} %slice.119), kind=kOutput, calls=%fused_computation.11 | convolution fusion | flops 1208745984 | bytes 3407872 | tf_op jit(solution)/shard_map/dot_general | solution.py:11
  70.3 1.5 %convolution_add_fusion.1 = f32[256,1536]{1,0:T(8,128)S(1)} fusion(f32[256,1536]{1,0:T(8,128)S(1)} %convolution_negate_fusion.1, f32[256,768]{1,0:T(8,128)S(1)} %copy-done.3, f32[256,1024]{1,0:T(8,128)S(1)} %bitcast.48), kind=kOutput, calls=%fused_computation.9 | convolution fusion | flops 1208352768 | bytes 4194304 | tf_op jit(solution)/shard_map/dot_general | solution.py:11
  71.7 2.8 %convolution_add_fusion = f32[512,1536]{1,0:T(8,128)S(1)} fusion(f32[256,1536]{1,0:T(8,128)S(1)} %convolution_negate_fusion.1, f32[512,768]{1,0:T(8,128)S(1)} %copy-done.2, f32[512,1024]{1,0:T(8,128)S(1)} %bitcast.50), kind=kOutput, calls=%fused_computation.8 | convolution fusion | flops 2416705536 | bytes 6815744 | tf_op jit(solution)/shard_map/dot_general | solution.py:11
  74.5 1.2 slice.177
  75.7 0.5 broadcast.42.clone
  76.2 0.1 slice_dynamic-update-slice_fusion.1
  76.3 0.1 slice_dynamic-update-slice_fusion
  76.4 0.1 fusion.54
  76.5 14.6 %collective-permute-done.1 = f32[256,512]{1,0:T(8,128)S(1)} collective-permute-done((f32[256,512]{1,0:T(8,128)S(1)}, f32[256,512]{1,0:T(8,128)S(1)}, u32[]{:S(2)}, u32[]{:S(2)}) %collective-permute-start.1) | collective-permute-done | bytes 524320 | tf_op jit(solution)/shard_map/ppermute | solution.py:32
  91.1 1.3 collective-permute-start.7
  92.5 2.0 %convolution_negate_fusion = f32[256,1536]{1,0:T(8,128)S(1)} fusion(f32[256,256]{1,0:T(8,128)S(1)} %collective-permute-done.4, f32[256,768]{1,0:T(8,128)S(1)} %collective-permute-done.6, f32[256,768]{1,0:T(8,128)} %collective-permute-done.5), kind=kOutput, calls=%fused_computation.10 | convolution fusion | flops 604766208 | bytes 3407872 | tf_op jit(solution)/shard_map/dot_general | solution.py:15
  94.5 1.8 %pad_add_fusion = f32[256,1536]{1,0:T(8,128)S(1)} fusion(f32[256,768]{1,0:T(8,128)S(1)} %slice.177, f32[256,1536]{1,0:T(8,128)S(1)} %convolution_negate_fusion, f32[256,1024]{1,0:T(8,128)} %collective-permute-done.3), kind=kOutput, calls=%fused_computation.19 | convolution fusion | flops 604372992 | bytes 4194304 | tf_op jit(solution)/shard_map/dot_general | solution.py:15
  96.3 0.2 fusion.55
  96.5 18.9 %collective-permute-done.2 = f32[256,512]{1,0:T(8,128)S(1)} collective-permute-done((f32[256,512]{1,0:T(8,128)S(1)}, f32[256,512]{1,0:T(8,128)S(1)}, u32[]{:S(2)}, u32[]{:S(2)}) %collective-permute-start.2) | collective-permute-done | bytes 524320 | tf_op jit(solution)/shard_map/ppermute | solution.py:32
  115.4 1.5 %maximum_add_fusion = f32[256,1536]{1,0:T(8,128)S(1)} fusion(f32[256,256]{1,0:T(8,128)S(1)} %slice.130, f32[256,512]{1,0:T(8,128)S(1)} %collective-permute-done.2, f32[1536]{0:T(1024)S(1)} %pad.17.clone, f32[256,1536]{1,0:T(8,128)S(1)} %convolution_negate_fusion.1, f32[256,512]{1,0:T(8,128)S(1)} %collective-permute-done.1), kind=kOutput, calls=%fused_computation.15 | convolution fusion | flops 1209139200 | bytes 4202496 | tf_op jit(solution)/shard_map/dot_general | solution.py:11
  116.8 0.7 broadcast.42.clone.1
  117.6 0.1 maximum_dynamic-update-slice_fusion
  117.7 0.8 fusion.23
  118.5 0.1 fusion.57
  118.6 0.3 fusion.6
  118.9 1.1 collective-permute-start.8
  120.0 0.1 select_reduce_fusion
  120.1 1.1 fusion.13
  121.3 1.3 convolution_subtract_fusion.1
  122.6 1.0 fusion.61
  123.6 1.1 convolution_subtract_fusion
  124.7 1.0 fusion.9
  125.7 6.8 %collective-permute-done.8 = f32[256,512]{1,0:T(8,128)S(1)} collective-permute-done((f32[256,512]{1,0:T(8,128)S(1)}, f32[256,512]{1,0:T(8,128)S(1)}, u32[]{:S(2)}, u32[]{:S(2)}) %collective-permute-start.8) | collective-permute-done | bytes 524320 | tf_op jit(solution)/shard_map/ppermute | solution.py:32
  132.6 0.1 slice_add_fusion
  132.7 0.1 maximum_dynamic-update-slice_fusion.1
  132.8 0.1 maximum_dynamic-update-slice_fusion.2
  132.9 5.3 %subtract_bitcast_fusion = f32[1,1,512,2048]{3,2,1,0:T(8,128)} fusion(f32[512,2048]{1,0:T(8,128)S(1)} %slice_dynamic-update-slice_fusion, f32[512,512]{1,0:T(8,128)S(1)} %fusion.9, f32[512,2048]{1,0:T(8,128)S(1)} %maximum_dynamic-update-slice_fusion.2), kind=kOutput, calls=%fused_computation.7 | convolution fusion | flops 3222274048 | bytes 13631488 | tf_op jit(solution)/shard_map/dot_general | solution.py:15
  (33 shorter events, 0.3 us)
Async XLA Ops:
  0.0 0.7 copy-start
  10.2 50.0 %collective-permute-start = (f32[256,1024]{1,0:T(8,128)}, f32[256,1024]{1,0:T(8,128)}, u32[]{:S(2)}, u32[]{:S(2)}) collective-permute-start(f32[256,1024]{1,0:T(8,128)} %bitcast.7), channel_id=1, source_target_pairs={{0,4},{1,5},{2,6},{3,7},{4,0},{5,1},{6,2},{7,3},{8,12},{9,13},{10,... | collective-permute-start | bytes 3145736 | tf_op jit(solution)/shard_map/ppermute | solution.py:32
  16.4 76.1 %collective-permute-start.5 = (f32[256,768]{1,0:T(8,128)}, f32[256,768]{1,0:T(8,128)}, u32[]{:S(2)}, u32[]{:S(2)}) collective-permute-start(f32[256,768]{1,0:T(8,128)} %slice.119), channel_id=1, source_target_pairs={{0,16},{8,24},{16,0},{24,8},{1,17},{9,25},{17,1},{25,9},{2,18},{10... | collective-permute-start | bytes 2359304 | tf_op jit(solution)/shard_map/ppermute | solution.py:32
  25.8 48.7 %collective-permute-start.3 = (f32[256,1024]{1,0:T(8,128)S(1)}, f32[256,1024]{1,0:T(8,128)}, u32[]{:S(2)}, u32[]{:S(2)}) collective-permute-start(f32[256,1024]{1,0:T(8,128)S(1)} %bitcast.44), channel_id=1, source_target_pairs={{0,16},{8,24},{16,0},{24,8},{1,17},{9,25},{17,1},{25,9},{2,18},{10... | collective-permute-start | bytes 3145736 | tf_op jit(solution)/shard_map/ppermute | solution.py:32
  63.0 29.4 %collective-permute-start.4 = (f32[256,256]{1,0:T(8,128)S(1)}, f32[256,256]{1,0:T(8,128)S(1)}, u32[]{:S(2)}, u32[]{:S(2)}) collective-permute-start(f32[256,256]{1,0:T(8,128)S(1)} %convolution_subtract_fusion.2), channel_id=1, source_target_pairs={{0,16},{8,24},{16,0},{24,8},{1,17},{9,25},{17,1},{25,9},{2,18},{10... | collective-permute-start | bytes 786440 | tf_op jit(solution)/shard_map/ppermute | solution.py:32
  65.9 26.6 %collective-permute-start.6 = (f32[256,768]{1,0:T(8,128)S(1)}, f32[256,768]{1,0:T(8,128)S(1)}, u32[]{:S(2)}, u32[]{:S(2)}) collective-permute-start(f32[256,768]{1,0:T(8,128)S(1)} %slice.179), channel_id=1, source_target_pairs={{0,16},{8,24},{16,0},{24,8},{1,17},{9,25},{17,1},{25,9},{2,18},{10... | collective-permute-start | bytes 2359304 | tf_op jit(solution)/shard_map/ppermute | solution.py:32
  66.4 24.7 %collective-permute-start.1 = (f32[256,512]{1,0:T(8,128)S(1)}, f32[256,512]{1,0:T(8,128)S(1)}, u32[]{:S(2)}, u32[]{:S(2)}) collective-permute-start(f32[256,512]{1,0:T(8,128)S(1)} %pad_maximum_fusion.1), channel_id=1, source_target_pairs={{0,4},{1,5},{2,6},{3,7},{4,0},{5,1},{6,2},{7,3},{8,12},{9,13},{10,... | collective-permute-start | bytes 1572872 | tf_op jit(solution)/shard_map/ppermute | solution.py:32
  67.6 2.7 %copy-start.3 = (f32[256,768]{1,0:T(8,128)S(1)}, f32[256,768]{1,0:T(8,128)}, u32[]{:S(2)}) copy-start(f32[256,768]{1,0:T(8,128)} %slice.175) | copy-start | bytes 2359300
  70.3 1.5 %copy-start.2 = (f32[512,768]{1,0:T(8,128)S(1)}, f32[512,768]{1,0:T(8,128)}, u32[]{:S(2)}) copy-start(f32[512,768]{1,0:T(8,128)} %slice.165) | copy-start | bytes 4718596
  76.4 14.6 %copy-start.4 = (f32[256,512]{1,0:T(8,128)S(1)}, f32[256,512]{1,0:T(8,128)}, u32[]{:S(2)}) copy-start(f32[256,512]{1,0:T(8,128)} %slice.176) | copy-start | bytes 1572868
  91.1 24.3 %collective-permute-start.2 = (f32[256,512]{1,0:T(8,128)S(1)}, f32[256,512]{1,0:T(8,128)S(1)}, u32[]{:S(2)}, u32[]{:S(2)}) collective-permute-start(f32[256,512]{1,0:T(8,128)S(1)} %copy-done.4), channel_id=1, source_target_pairs={{0,4},{1,5},{2,6},{3,7},{4,0},{5,1},{6,2},{7,3},{8,12},{9,13},{10,... | collective-permute-start | bytes 1572872 | tf_op jit(solution)/shard_map/ppermute | solution.py:32
  91.1 26.6 %collective-permute-start.7 = (f32[256,512]{1,0:T(8,128)S(1)}, f32[256,512]{1,0:T(8,128)S(1)}, u32[]{:S(2)}, u32[]{:S(2)}) collective-permute-start(f32[256,512]{1,0:T(8,128)S(1)} %collective-permute-done.1), channel_id=1, source_target_pairs={{0,16},{8,24},{16,0},{24,8},{1,17},{9,25},{17,1},{25,9},{2,18},{10... | collective-permute-start | bytes 1572872 | tf_op jit(solution)/shard_map/ppermute | solution.py:32
  118.9 13.7 %collective-permute-start.8 = (f32[256,512]{1,0:T(8,128)S(1)}, f32[256,512]{1,0:T(8,128)S(1)}, u32[]{:S(2)}, u32[]{:S(2)}) collective-permute-start(f32[256,512]{1,0:T(8,128)S(1)} %collective-permute-done.2), channel_id=1, source_target_pairs={{0,16},{8,24},{16,0},{24,8},{1,17},{9,25},{17,1},{25,9},{2,18},{10... | collective-permute-start | bytes 1572872 | tf_op jit(solution)/shard_map/ppermute | solution.py:32
  132.9 5.3 %copy-start.1 = (s32[1,1,4,256]{3,2,1,0:T(4,128)S(1)}, s32[1,1,4,256]{3,2,1,0:T(4,128)}, u32[]{:S(2)}) copy-start(s32[1,1,4,256]{3,2,1,0:T(4,128)} %param.3) | copy-start | bytes 12292

commit v9 on v5

--- a/solution.py
+++ b/solution.py
@@ -92,10 +92,10 @@
     side_i2 = jnp.concatenate([side_first, side_second], 0)
     diag_i2 = jnp.concatenate([diag_first, diag_second], 0)
 
-    solved_own = pair_solve(inverse_own, own_i1[:, width:], side_i1[:, width:])
-    own_ext = first_rows(own_ov, solved_own, width)
-    own_int = first_rows(own_i2, solved_own, width)
-    side_int = second_rows(side_i2, solved_own, width)
+    solved_own = pair_solve(inverse_own, own_i1[:, width:], side_i1[:, width:], matmul_high)
+    own_ext = first_rows(own_ov, solved_own, width, matmul_high)
+    own_int = first_rows(own_i2, solved_own, width, matmul_high)
+    side_int = second_rows(side_i2, solved_own, width, matmul_high)
 
     solved_other = pair_solve(inverse_other, vert_ie, diag_ie, matmul_high)
     vert_int = first_rows(vert_i2, solved_other, width, matmul_high)

time: 136 us -> 136 us (level)
  waiting for transfers between devices: 55.3 us -> 58.5 us
  matrix products: 24.8 us -> 22 us
    dot_general x8 -> x4, matrix products: 9.83 us -> 1.65 us  [matmul(): jnp.dot(left, right, precision=lax.Precision.HIGHEST, preferred_element_t...]
    dot_general x9 -> x13, matrix products: 15 us -> 20.3 us  [matmul_high(): jnp.dot(left, right, precision=lax.Precision.HIGH, preferred_element_type...]
    ppermute x9, waiting for transfers between devices: 55.3 us -> 58.5 us  [swap(): return lax.ppermute(value, axis, pairs)]
  transfers between devices with their start and end apart: 9 -> 9, of which waited for: 5 -> 5; matrix products, arithmetic and copies ran while one was open for 35% -> 32% of each run, Pallas kernels for 0% -> 0%
where the time goes in v9:
time: 136 us
  waiting for transfers between devices  58.5 us (43%)
  local copies, waits for them, and re-layouts  42.3 us (31%)
  matrix products  22 us (16%)
  starting transfers between devices  10.6 us (8%)
  other arithmetic  1.88 us (1%)
    ppermute x9, waiting for transfers between devices, swap(): return lax.ppermute(value, axis, pairs)  58.5 us
    dot_general x13, matrix products, matmul_high(): jnp.dot(left, right, precision=lax.Precision.HIGH, preferred_element_type...  20.3 us
    gather x6, local copies, waits for them, and re-layouts, pick(): picked = jnp.take(matrix, rows, axis=0, mode='clip')  15.9 us
    gather x6, local copies, waits for them, and re-layouts, pick(): return jnp.take(picked, cols, axis=1, mode='clip')  15.6 us
    ppermute x9, starting transfers between devices, swap(): return lax.ppermute(value, axis, pairs)  10.6 us
    slice x3, local copies, waits for them, and re-layouts, first_rows(): rows[:, width:]  3.41 us
  transfers between devices with their start and end apart: 9, of which 5 were waited for; matrix products, arithmetic and copies ran while one was open for 32% of the time, Pallas kernels for 0%

profile of v9, /device:TPU:0, one launch (start us, length us, event | category | flops | bytes accessed | tf_op | source)
XLA Modules:
  0.0 135.7 jit_solution(14078028168953484512)
XLA Ops:
  0.0 0.1 pad_add_fusion.3
  0.1 0.6 copy-done
  0.7 0.6 gather_fusion
  1.3 3.8 %gather_fusion.1 = f32[256,1024]{1,0:T(8,128)S(1)} fusion(f32[1024,1024]{1,0:T(8,128)} %bitcast.41, s32[1024]{0:T(1024)S(1)} %get-tuple-element.30), kind=kCustom, calls=%fused_computation.1 | custom fusion | bytes 2098176 | tf_op jit(solution)/shard_map/jit(_take)/gather | solution.py:62
  5.1 0.3 copy.3
  5.4 3.5 %gather_fusion.2 = f32[1024,256]{1,0:T(8,128)S(1)} fusion(f32[256,1024]{0,1:T(8,128)S(1)} %copy.3, s32[1024]{0:T(1024)S(1)} %get-tuple-element.31), kind=kCustom, calls=%fused_computation.2 | custom fusion | bytes 2101248 | tf_op jit(solution)/shard_map/jit(_take)/gather | solution.py:63
  8.9 1.3 copy.4
  10.2 4.0 %collective-permute-start = (f32[256,1024]{1,0:T(8,128)}, f32[256,1024]{1,0:T(8,128)}, u32[]{:S(2)}, u32[]{:S(2)}) collective-permute-start(f32[256,1024]{1,0:T(8,128)} %bitcast.7), channel_id=1, source_target_pairs={{0,4},{1,5},{2,6},{3,7},{4,0},{5,1},{6,2},{7,3},{8,12},{9,13},{10,... | collective-permute-start | bytes 3145736 | tf_op jit(solution)/shard_map/ppermute | solution.py:32
  14.2 2.1 %slice.106 = f32[256,768]{1,0:T(8,128)} slice(f32[256,1024]{1,0:T(8,128)} %bitcast.7), slice={[0:256], [256:1024]} | slice | bytes 1572864 | tf_op jit(solution)/shard_map/slice | solution.py:95
  16.3 1.5 %collective-permute-start.5 = (f32[256,768]{1,0:T(8,128)}, f32[256,768]{1,0:T(8,128)}, u32[]{:S(2)}, u32[]{:S(2)}) collective-permute-start(f32[256,768]{1,0:T(8,128)} %slice.106), channel_id=1, source_target_pairs={{0,16},{8,24},{16,0},{24,8},{1,17},{9,25},{17,1},{25,9},{2,18},{10... | collective-permute-start | bytes 2359304 | tf_op jit(solution)/shard_map/ppermute | solution.py:32
  17.9 3.8 %gather_fusion.5 = f32[256,1024]{1,0:T(8,128)S(1)} fusion(f32[1024,1024]{1,0:T(8,128)} %bitcast.42, s32[1024]{0:T(1024)S(1)} %get-tuple-element.28), kind=kCustom, calls=%fused_computation.5 | custom fusion | bytes 2098176 | tf_op jit(solution)/shard_map/jit(_take)/gather | solution.py:62
  21.6 0.3 copy.7
  22.0 3.5 %gather_fusion.6 = f32[1024,256]{1,0:T(8,128)S(1)} fusion(f32[256,1024]{0,1:T(8,128)S(1)} %copy.7, s32[1024]{0:T(1024)S(1)} %get-tuple-element.31), kind=kCustom, calls=%fused_computation.6 | custom fusion | bytes 2101248 | tf_op jit(solution)/shard_map/jit(_take)/gather | solution.py:63
  25.5 0.3 copy.8
  25.8 0.6 collective-permute-start.3
  26.4 1.0 slice.157
  27.3 5.8 %gather_fusion.3 = f32[512,1024]{1,0:T(8,128)} fusion(f32[1024,1024]{1,0:T(8,128)} %bitcast.43, s32[1024]{0:T(1024)S(1)} %get-tuple-element.29), kind=kCustom, calls=%fused_computation.3 | custom fusion | bytes 4196352 | tf_op jit(solution)/shard_map/jit(_take)/gather | solution.py:62
  33.1 1.9 %copy.5 = f32[512,1024]{0,1:T(8,128)S(1)} copy(f32[512,1024]{1,0:T(8,128)} %gather_fusion.3) | data formatting | bytes 4194304 | tf_op jit(solution)/shard_map/jit(_take)/gather | solution.py:62
  35.0 4.9 %gather_fusion.4 = f32[1024,512]{1,0:T(8,128)} fusion(f32[512,1024]{0,1:T(8,128)S(1)} %copy.5, s32[1024]{0:T(1024)S(1)} %get-tuple-element.31), kind=kCustom, calls=%fused_computation.4 | custom fusion | bytes 4198400 | tf_op jit(solution)/shard_map/jit(_take)/gather | solution.py:63
  39.9 2.1 %copy.6 = f32[1024,512]{0,1:T(8,128)S(1)} copy(f32[1024,512]{1,0:T(8,128)} %gather_fusion.4) | data formatting | bytes 4194304 | tf_op jit(solution)/shard_map/jit(_take)/gather | solution.py:63
  42.0 1.3 slice.148
  43.3 0.1 fusion.60
  43.4 16.8 %collective-permute-done = f32[256,1024]{1,0:T(8,128)} collective-permute-done((f32[256,1024]{1,0:T(8,128)}, f32[256,1024]{1,0:T(8,128)}, u32[]{:S(2)}, u32[]{:S(2)}) %collective-permute-start) | collective-permute-done | bytes 1048608 | tf_op jit(solution)/shard_map/ppermute | solution.py:32
  60.2 1.2 slice.109
  61.4 1.1 select_reduce_fusion.1
  62.5 0.4 fusion.38
  63.0 0.5 convolution_subtract_fusion.3
  63.4 0.4 fusion.62
  63.8 0.4 convolution_subtract_fusion.2
  64.2 1.6 %collective-permute-start.4 = (f32[256,256]{1,0:T(8,128)S(1)}, f32[256,256]{1,0:T(8,128)S(1)}, u32[]{:S(2)}, u32[]{:S(2)}) collective-permute-start(f32[256,256]{1,0:T(8,128)S(1)} %convolution_subtract_fusion.2), channel_id=1, source_target_pairs={{0,16},{8,24},{16,0},{24,8},{1,17},{9,25},{17,1},{25,9},{2,18},{10... | collective-permute-start | bytes 786440 | tf_op jit(solution)/shard_map/ppermute | solution.py:32
  65.9 2.0 %convolution_negate_fusion.1 = f32[256,1536]{1,0:T(8,128)S(1)} fusion(f32[256,256]{1,0:T(8,128)S(1)} %convolution_subtract_fusion.2, f32[256,768]{1,0:T(8,128)S(1)} %slice.109, f32[256,768]{1,0:T(8,128)} %slice.106), kind=kOutput, calls=%fused_computation.11 | convolution fusion | flops 604766208 | bytes 3407872 | tf_op jit(solution)/shard_map/dot_general | solution.py:15
  67.9 1.3 slice.164
  69.1 0.5 collective-permute-start.6
  69.7 0.8 convolution_add_fusion.1
  70.5 0.1 copy-done.2
  70.6 1.4 %convolution_add_fusion = f32[512,1536]{1,0:T(8,128)S(1)} fusion(f32[256,1536]{1,0:T(8,128)S(1)} %convolution_negate_fusion.1, f32[512,768]{1,0:T(8,128)S(1)} %copy-done.2, f32[512,1024]{1,0:T(8,128)S(1)} %bitcast.49), kind=kOutput, calls=%fused_computation.8 | convolution fusion | flops 1208745984 | bytes 6815744 | tf_op jit(solution)/shard_map/dot_general | solution.py:15
  72.0 0.5 broadcast.44.clone
  72.5 0.1 slice_dynamic-update-slice_fusion.1
  72.6 1.2 slice.162
  73.8 0.1 slice_dynamic-update-slice_fusion
  73.9 0.1 fusion.59
  74.0 11.4 %collective-permute-done.1 = f32[128,1024]{1,0:T(8,128)S(1)} collective-permute-done((f32[128,1024]{1,0:T(8,128)S(1)}, f32[128,1024]{1,0:T(8,128)S(1)}, u32[]{:S(2)}, u32[]{:S(2)}) %collective-permute-start.1) | collective-permute-done | bytes 524320 | tf_op jit(solution)/shard_map/ppermute | solution.py:32
  85.4 1.3 collective-permute-start.7
  86.8 3.1 %collective-permute-done.6 = f32[256,768]{1,0:T(8,128)S(1)} collective-permute-done((f32[256,768]{1,0:T(8,128)S(1)}, f32[256,768]{1,0:T(8,128)S(1)}, u32[]{:S(2)}, u32[]{:S(2)}) %collective-permute-start.6) | collective-permute-done | bytes 786464 | tf_op jit(solution)/shard_map/ppermute | solution.py:32
  89.8 2.0 %convolution_negate_fusion = f32[256,1536]{1,0:T(8,128)S(1)} fusion(f32[256,256]{1,0:T(8,128)S(1)} %collective-permute-done.4, f32[256,768]{1,0:T(8,128)S(1)} %collective-permute-done.6, f32[256,768]{1,0:T(8,128)} %collective-permute-done.5), kind=kOutput, calls=%fused_computation.10 | convolution fusion | flops 604766208 | bytes 3407872 | tf_op jit(solution)/shard_map/dot_general | solution.py:15
  91.8 1.8 %pad_add_fusion.1 = f32[256,1536]{1,0:T(8,128)S(1)} fusion(f32[256,768]{1,0:T(8,128)S(1)} %slice.162, f32[256,1536]{1,0:T(8,128)S(1)} %convolution_negate_fusion, f32[256,1024]{1,0:T(8,128)} %collective-permute-done.3), kind=kOutput, calls=%fused_computation.19 | convolution fusion | flops 604372992 | bytes 4194304 | tf_op jit(solution)/shard_map/dot_general | solution.py:15
  93.6 16.2 %collective-permute-done.2 = f32[128,1024]{1,0:T(8,128)S(1)} collective-permute-done((f32[128,1024]{1,0:T(8,128)S(1)}, f32[128,1024]{1,0:T(8,128)S(1)}, u32[]{:S(2)}, u32[]{:S(2)}) %collective-permute-start.2) | collective-permute-done | bytes 524320 | tf_op jit(solution)/shard_map/ppermute | solution.py:32
  109.8 0.1 slice.160
  109.9 1.0 collective-permute-start.8
  111.0 0.8 pad_add_fusion.2
  111.8 0.5 broadcast.44.clone.1
  112.3 0.1 maximum_dynamic-update-slice_fusion.1
  112.4 0.1 fusion.7
  112.5 11.1 %collective-permute-done.8 = f32[128,1024]{1,0:T(8,128)S(1)} collective-permute-done((f32[128,1024]{1,0:T(8,128)S(1)}, f32[128,1024]{1,0:T(8,128)S(1)}, u32[]{:S(2)}, u32[]{:S(2)}) %collective-permute-start.8) | collective-permute-done | bytes 524320 | tf_op jit(solution)/shard_map/ppermute | solution.py:32
  123.6 0.1 slice.165
  123.7 0.8 pad_add_fusion
  124.5 0.1 maximum_dynamic-update-slice_fusion
  124.6 0.3 select_reduce_fusion
  125.0 1.1 fusion.15
  126.1 1.5 %convolution_subtract_fusion.1 = f32[512,512]{1,0:T(8,128)S(1)} fusion(f32[512,512]{1,0:T(8,128)S(1)} %fusion.15, f32[512,512]{1,0:T(8,128)S(1)} %get-tuple-element.18, f32[512]{0:T(512)S(1)} %broadcast_divide_fusion), kind=kOutput, calls=%fused_computation.22 | convolution fusion | flops 808976384 | bytes 3147776 | tf_op jit(solution)/shard_map/dot_general | solution.py:15
  127.6 1.0 fusion.63
  128.6 1.0 convolution_subtract_fusion
  129.6 1.0 fusion.11
  130.6 5.1 %subtract_bitcast_fusion = f32[1,1,512,2048]{3,2,1,0:T(8,128)} fusion(f32[512,2048]{1,0:T(8,128)S(1)} %slice_dynamic-update-slice_fusion, f32[512,512]{1,0:T(8,128)S(1)} %fusion.11, f32[512,2048]{1,0:T(8,128)S(1)} %get-tuple-element.21), kind=kOutput, calls=%fused_computation.7 | convolution fusion | flops 3222274048 | bytes 13631488 | tf_op jit(solution)/shard_map/dot_general | solution.py:15
  (25 shorter events, 0.2 us)
Async XLA Ops:
  0.0 0.7 copy-start
  10.2 50.0 %collective-permute-start = (f32[256,1024]{1,0:T(8,128)}, f32[256,1024]{1,0:T(8,128)}, u32[]{:S(2)}, u32[]{:S(2)}) collective-permute-start(f32[256,1024]{1,0:T(8,128)} %bitcast.7), channel_id=1, source_target_pairs={{0,4},{1,5},{2,6},{3,7},{4,0},{5,1},{6,2},{7,3},{8,12},{9,13},{10,... | collective-permute-start | bytes 3145736 | tf_op jit(solution)/shard_map/ppermute | solution.py:32
  16.3 70.4 %collective-permute-start.5 = (f32[256,768]{1,0:T(8,128)}, f32[256,768]{1,0:T(8,128)}, u32[]{:S(2)}, u32[]{:S(2)}) collective-permute-start(f32[256,768]{1,0:T(8,128)} %slice.106), channel_id=1, source_target_pairs={{0,16},{8,24},{16,0},{24,8},{1,17},{9,25},{17,1},{25,9},{2,18},{10... | collective-permute-start | bytes 2359304 | tf_op jit(solution)/shard_map/ppermute | solution.py:32
  25.8 46.8 %collective-permute-start.3 = (f32[256,1024]{1,0:T(8,128)S(1)}, f32[256,1024]{1,0:T(8,128)}, u32[]{:S(2)}, u32[]{:S(2)}) collective-permute-start(f32[256,1024]{1,0:T(8,128)S(1)} %bitcast.44), channel_id=1, source_target_pairs={{0,16},{8,24},{16,0},{24,8},{1,17},{9,25},{17,1},{25,9},{2,18},{10... | collective-permute-start | bytes 3145736 | tf_op jit(solution)/shard_map/ppermute | solution.py:32
  60.2 25.2 %collective-permute-start.1 = (f32[128,1024]{1,0:T(8,128)S(1)}, f32[128,1024]{1,0:T(8,128)S(1)}, u32[]{:S(2)}, u32[]{:S(2)}) collective-permute-start(f32[128,1024]{1,0:T(8,128)S(1)} %get-tuple-element.14), channel_id=1, source_target_pairs={{0,4},{1,5},{2,6},{3,7},{4,0},{5,1},{6,2},{7,3},{8,12},{9,13},{10,... | collective-permute-start | bytes 1572872 | tf_op jit(solution)/shard_map/ppermute | solution.py:32
  64.2 22.6 %collective-permute-start.4 = (f32[256,256]{1,0:T(8,128)S(1)}, f32[256,256]{1,0:T(8,128)S(1)}, u32[]{:S(2)}, u32[]{:S(2)}) collective-permute-start(f32[256,256]{1,0:T(8,128)S(1)} %convolution_subtract_fusion.2), channel_id=1, source_target_pairs={{0,16},{8,24},{16,0},{24,8},{1,17},{9,25},{17,1},{25,9},{2,18},{10... | collective-permute-start | bytes 786440 | tf_op jit(solution)/shard_map/ppermute | solution.py:32
  67.9 1.8 %copy-start.3 = (f32[256,768]{1,0:T(8,128)S(1)}, f32[256,768]{1,0:T(8,128)}, u32[]{:S(2)}) copy-start(f32[256,768]{1,0:T(8,128)} %slice.157) | copy-start | bytes 2359300
  69.1 1.4 %copy-start.2 = (f32[512,768]{1,0:T(8,128)S(1)}, f32[512,768]{1,0:T(8,128)}, u32[]{:S(2)}) copy-start(f32[512,768]{1,0:T(8,128)} %slice.148) | copy-start | bytes 4718596
  69.1 20.7 %collective-permute-start.6 = (f32[256,768]{1,0:T(8,128)S(1)}, f32[256,768]{1,0:T(8,128)S(1)}, u32[]{:S(2)}, u32[]{:S(2)}) collective-permute-start(f32[256,768]{1,0:T(8,128)S(1)} %slice.164), channel_id=1, source_target_pairs={{0,16},{8,24},{16,0},{24,8},{1,17},{9,25},{17,1},{25,9},{2,18},{10... | collective-permute-start | bytes 2359304 | tf_op jit(solution)/shard_map/ppermute | solution.py:32
  85.4 24.3 %collective-permute-start.2 = (f32[128,1024]{1,0:T(8,128)S(1)}, f32[128,1024]{1,0:T(8,128)S(1)}, u32[]{:S(2)}, u32[]{:S(2)}) collective-permute-start(f32[128,1024]{1,0:T(8,128)S(1)} %get-tuple-element.16), channel_id=1, source_target_pairs={{0,4},{1,5},{2,6},{3,7},{4,0},{5,1},{6,2},{7,3},{8,12},{9,13},{10,... | collective-permute-start | bytes 1572872 | tf_op jit(solution)/shard_map/ppermute | solution.py:32
  85.4 25.5 %collective-permute-start.7 = (f32[128,1024]{1,0:T(8,128)S(1)}, f32[128,1024]{1,0:T(8,128)S(1)}, u32[]{:S(2)}, u32[]{:S(2)}) collective-permute-start(f32[128,1024]{1,0:T(8,128)S(1)} %collective-permute-done.1), channel_id=1, source_target_pairs={{0,16},{8,24},{16,0},{24,8},{1,17},{9,25},{17,1},{25,9},{2,18},{10... | collective-permute-start | bytes 1572872 | tf_op jit(solution)/shard_map/ppermute | solution.py:32
  109.9 13.7 %collective-permute-start.8 = (f32[128,1024]{1,0:T(8,128)S(1)}, f32[128,1024]{1,0:T(8,128)S(1)}, u32[]{:S(2)}, u32[]{:S(2)}) collective-permute-start(f32[128,1024]{1,0:T(8,128)S(1)} %collective-permute-done.2), channel_id=1, source_target_pairs={{0,16},{8,24},{16,0},{24,8},{1,17},{9,25},{17,1},{25,9},{2,18},{10... | collective-permute-start | bytes 1572872 | tf_op jit(solution)/shard_map/ppermute | solution.py:32
  130.6 5.1 %copy-start.1 = (s32[1,1,4,256]{3,2,1,0:T(4,128)S(1)}, s32[1,1,4,256]{3,2,1,0:T(4,128)}, u32[]{:S(2)}) copy-start(s32[1,1,4,256]{3,2,1,0:T(4,128)} %param.3) | copy-start | bytes 12292

commit v10 on v8

--- a/solution.py
+++ b/solution.py
@@ -74,27 +74,29 @@
     own_i1 = pick(leaf, perm[:width], perm)
     leaf, own_i1 = lax.optimization_barrier((leaf, own_i1))
     own_i2 = pick(leaf, perm[3 * width :], perm)
+    own_a = pick(leaf, perm[3 * width :], jnp.concatenate([perm[:width], perm[3 * width :]]))
+    own_b = pick(leaf, perm[3 * width :], perm[width : 3 * width])
     own_ov = pick(leaf, perm[width : 3 * width], perm)
 
-    half = width // 2
     vert_ie = swap(own_i1[:, width:], "grp")
     vert_i2 = swap(own_i2, "grp")
     side_i1 = swap(own_i1, "box")
     diag_ie = swap(side_i1[:, width:], "grp")
     inverse_own = newton(own_i1[:, :width] + side_i1[:, :width], ITERS_LOW)
     inverse_other = swap(inverse_own, "grp")
-    own_a = jnp.concatenate([own_i2[:, :width], own_i2[:, 3 * width :]], 1)
     part_a, side_i1 = lax.optimization_barrier((own_a, side_i1))
     side_a = swap(part_a, "box")
     diag_a = swap(side_a, "grp")
-    part_b, side_a = lax.optimization_barrier((own_i2[:, width : 3 * width], side_a))
+    part_b, side_a = lax.optimization_barrier((own_b, side_a))
     side_b = swap(part_b, "box")
-    side_i2 = jnp.concatenate([side_a[:, :width], side_b, side_a[:, width:]], 1)
 
     solved_own = pair_solve(inverse_own, own_i1[:, width:], side_i1[:, width:])
     own_ext = first_rows(own_ov, solved_own, width)
     own_int = first_rows(own_i2, solved_own, width)
-    side_int = second_rows(side_i2, solved_own, width)
+    side_prod = matmul(side_a[:, :width], solved_own)
+    side_inner = jnp.concatenate(
+        [side_prod[:, 2 * width : 3 * width], side_prod[:, 5 * width :] + side_a[:, width:]], 1
+    )
 
     solved_other = pair_solve(inverse_other, vert_ie, diag_ie, matmul_high)
     vert_int = first_rows(vert_i2, solved_other, width, matmul_high)
@@ -103,17 +105,19 @@
         [diag_prod[:, 2 * width : 3 * width], diag_prod[:, 5 * width :] + diag_a[:, width:]], 1
     )
 
-    near = jnp.concatenate([own_int, side_int], 0)
+    near_int = jnp.concatenate([int_cols(own_int, width), side_inner], 0)
     far_int = jnp.concatenate([int_cols(vert_int, width), diag_inner], 0)
-    system_two = int_cols(near, width) + far_int
-    system_two, side_b = lax.optimization_barrier((system_two, side_b))
+    near_int, side_b = lax.optimization_barrier((near_int, side_b))
     diag_b = swap(side_b, "grp")
+    system_two = near_int + far_int
     inverse_two = newton(system_two, ITERS_HIGH, matmul_high)
     weights = matmul_high(int_cols(own_ext, width), inverse_two)
     own_id = 2 * upper + right
     blocks = [
-        near[:, 0 : 2 * width],
-        near[:, 3 * width : 5 * width],
+        jnp.concatenate([own_int[:, 0 : 2 * width], side_prod[:, 0 : 2 * width]], 0),
+        jnp.concatenate(
+            [own_int[:, 3 * width : 5 * width], side_prod[:, 3 * width : 5 * width] + side_b], 0
+        ),
         jnp.concatenate([vert_int[:, 0 : 2 * width], diag_prod[:, 0 : 2 * width]], 0),
         jnp.concatenate(
             [vert_int[:, 3 * width : 5 * width], diag_prod[:, 3 * width : 5 * width] + diag_b], 0

time: 139 us -> 133 us (0.957)
  waiting for transfers between devices: 56.2 us -> 46.4 us
  local copies, waits for them, and re-layouts: 43.1 us -> 47.6 us
    ppermute x9, waiting for transfers between devices: 56.2 us -> 46.4 us  [swap(): return lax.ppermute(value, axis, pairs)]
    gather x6 -> x10, local copies, waits for them, and re-layouts: 15.6 us -> 20.7 us  [pick(): return jnp.take(picked, cols, axis=1, mode='clip')]
  transfers between devices with their start and end apart: 9 -> 9, of which waited for: 4 -> 4; matrix products, arithmetic and copies ran while one was open for 39% -> 45% of each run, Pallas kernels for 0% -> 0%
where the time goes in v10:
time: 133 us; the launch traced here: 132 us
  local copies, waits for them, and re-layouts  47.6 us (36%)
  waiting for transfers between devices  46.4 us (35%)
  matrix products  25.3 us (19%)
  starting transfers between devices  10.1 us (8%)
  other arithmetic  2.34 us (2%)
    ppermute x9, waiting for transfers between devices, swap(): return lax.ppermute(value, axis, pairs)  46.4 us
    gather x10, local copies, waits for them, and re-layouts, pick(): return jnp.take(picked, cols, axis=1, mode='clip')  20.7 us
    gather x6, local copies, waits for them, and re-layouts, pick(): picked = jnp.take(matrix, rows, axis=0, mode='clip')  15.9 us
    dot_general x9, matrix products, matmul_high(): jnp.dot(left, right, precision=lax.Precision.HIGH, preferred_element_type...  15.4 us
    ppermute x9, starting transfers between devices, swap(): return lax.ppermute(value, axis, pairs)  10.1 us
    dot_general x8, matrix products, matmul(): jnp.dot(left, right, precision=lax.Precision.HIGHEST, preferred_element_t...  9.92 us
    slice x3, local copies, waits for them, and re-layouts, first_rows(): rows[:, width:]  3.4 us
    slice x2, local copies, waits for them, and re-layouts, body(): solved_own = pair_solve(inverse_own, own_i1[:, width:], side_i1[:, width:])  3.29 us
  transfers between devices with their start and end apart: 9, of which 4 were waited for; matrix products, arithmetic and copies ran while one was open for 45% of the time, Pallas kernels for 0%

profile of v10, /device:TPU:0, one launch (start us, length us, event | category | flops | bytes accessed | tf_op | source)
XLA Modules:
  0.0 132.3 jit_solution(7279961286193436013)
XLA Ops:
  0.1 0.6 copy-done
  0.7 0.6 gather_fusion
  1.3 3.8 %gather_fusion.1 = f32[256,1024]{1,0:T(8,128)S(1)} fusion(f32[1024,1024]{1,0:T(8,128)} %bitcast.43, s32[1024]{0:T(1024)S(1)} %pad_clamp_fusion.3), kind=kCustom, calls=%fused_computation.1 | custom fusion | bytes 2098176 | tf_op jit(solution)/shard_map/jit(_take)/gather | solution.py:62
  5.1 0.3 copy.3
  5.4 3.5 %gather_fusion.2 = f32[1024,256]{1,0:T(8,128)S(1)} fusion(f32[256,1024]{0,1:T(8,128)S(1)} %copy.3, s32[1024]{0:T(1024)S(1)} %broadcast_clamp_fusion), kind=kCustom, calls=%fused_computation.2 | custom fusion | bytes 2101248 | tf_op jit(solution)/shard_map/jit(_take)/gather | solution.py:63
  8.9 1.3 copy.4
  10.2 4.0 %collective-permute-start = (f32[256,1024]{1,0:T(8,128)}, f32[256,1024]{1,0:T(8,128)}, u32[]{:S(2)}, u32[]{:S(2)}) collective-permute-start(f32[256,1024]{1,0:T(8,128)} %bitcast.7), channel_id=1, source_target_pairs={{0,4},{1,5},{2,6},{3,7},{4,0},{5,1},{6,2},{7,3},{8,12},{9,13},{10,... | collective-permute-start | bytes 3145736 | tf_op jit(solution)/shard_map/ppermute | solution.py:32
  14.2 2.1 %slice.133 = f32[256,768]{1,0:T(8,128)} slice(f32[256,1024]{1,0:T(8,128)} %bitcast.7), slice={[0:256], [256:1024]} | slice | bytes 1572864 | tf_op jit(solution)/shard_map/slice | solution.py:93
  16.3 1.5 %collective-permute-start.5 = (f32[256,768]{1,0:T(8,128)}, f32[256,768]{1,0:T(8,128)}, u32[]{:S(2)}, u32[]{:S(2)}) collective-permute-start(f32[256,768]{1,0:T(8,128)} %slice.133), channel_id=1, source_target_pairs={{0,16},{8,24},{16,0},{24,8},{1,17},{9,25},{17,1},{25,9},{2,18},{10... | collective-permute-start | bytes 2359304 | tf_op jit(solution)/shard_map/ppermute | solution.py:32
  17.9 3.8 %gather_fusion.5 = f32[256,1024]{1,0:T(8,128)S(1)} fusion(f32[1024,1024]{1,0:T(8,128)} %bitcast.44, s32[1024]{0:T(1024)S(1)} %pad_clamp_fusion.1), kind=kCustom, calls=%fused_computation.5 | custom fusion | bytes 2098176 | tf_op jit(solution)/shard_map/jit(_take)/gather | solution.py:62
  21.6 0.3 copy.7
  22.0 3.5 %gather_fusion.7 = f32[1024,256]{1,0:T(8,128)S(1)} fusion(f32[256,1024]{0,1:T(8,128)S(1)} %copy.7, s32[1024]{0:T(1024)S(1)} %broadcast_clamp_fusion), kind=kCustom, calls=%fused_computation.7 | custom fusion | bytes 2101248 | tf_op jit(solution)/shard_map/jit(_take)/gather | solution.py:63
  25.4 0.3 copy.10
  25.8 0.6 collective-permute-start.3
  26.3 1.0 slice.195
  27.3 1.6 %gather_fusion.8 = f32[512,256]{1,0:T(8,128)S(1)} fusion(f32[256,1024]{0,1:T(8,128)S(1)} %copy.7, s32[1024]{0:T(1024)S(1)} %pad_clamp_fusion.2), kind=kCustom, calls=%fused_computation.8 | custom fusion | bytes 1050624 | tf_op jit(solution)/shard_map/jit(_take)/gather | solution.py:63
  28.9 5.8 %gather_fusion.3 = f32[512,1024]{1,0:T(8,128)} fusion(f32[1024,1024]{1,0:T(8,128)} %bitcast.45, s32[1024]{0:T(1024)S(1)} %pad_clamp_fusion.2), kind=kCustom, calls=%fused_computation.3 | custom fusion | bytes 4196352 | tf_op jit(solution)/shard_map/jit(_take)/gather | solution.py:62
  34.7 1.6 %gather_fusion.6 = f32[512,256]{1,0:T(8,128)S(1)} fusion(f32[256,1024]{0,1:T(8,128)S(1)} %copy.7, s32[1024]{0:T(1024)S(1)} %pad_clamp_fusion), kind=kCustom, calls=%fused_computation.6 | custom fusion | bytes 1050624 | tf_op jit(solution)/shard_map/jit(_take)/gather | solution.py:63
  36.3 1.0 copy.8
  37.3 1.0 copy.12
  38.3 1.9 %copy.5 = f32[512,1024]{0,1:T(8,128)S(1)} copy(f32[512,1024]{1,0:T(8,128)} %gather_fusion.3) | data formatting | bytes 4194304 | tf_op jit(solution)/shard_map/jit(_take)/gather | solution.py:62
  40.2 4.9 %gather_fusion.4 = f32[1024,512]{1,0:T(8,128)} fusion(f32[512,1024]{0,1:T(8,128)S(1)} %copy.5, s32[1024]{0:T(1024)S(1)} %broadcast_clamp_fusion), kind=kCustom, calls=%fused_computation.4 | custom fusion | bytes 4198400 | tf_op jit(solution)/shard_map/jit(_take)/gather | solution.py:63
  45.1 2.1 %copy.6 = f32[1024,512]{0,1:T(8,128)S(1)} copy(f32[1024,512]{1,0:T(8,128)} %gather_fusion.4) | data formatting | bytes 4194304 | tf_op jit(solution)/shard_map/jit(_take)/gather | solution.py:63
  47.2 1.3 slice.187
  48.4 11.7 %collective-permute-done = f32[256,1024]{1,0:T(8,128)} collective-permute-done((f32[256,1024]{1,0:T(8,128)}, f32[256,1024]{1,0:T(8,128)}, u32[]{:S(2)}, u32[]{:S(2)}) %collective-permute-start) | collective-permute-done | bytes 1048608 | tf_op jit(solution)/shard_map/ppermute | solution.py:32
  60.2 1.1 select_reduce_fusion.1
  61.3 0.4 fusion.29
  61.8 0.5 convolution_subtract_fusion.3
  62.2 0.4 fusion.57
  62.6 0.4 convolution_subtract_fusion.2
  63.0 1.6 %collective-permute-start.4 = (f32[256,256]{1,0:T(8,128)S(1)}, f32[256,256]{1,0:T(8,128)S(1)}, u32[]{:S(2)}, u32[]{:S(2)}) collective-permute-start(f32[256,256]{1,0:T(8,128)S(1)} %convolution_subtract_fusion.2), channel_id=1, source_target_pairs={{0,16},{8,24},{16,0},{24,8},{1,17},{9,25},{17,1},{25,9},{2,18},{10... | collective-permute-start | bytes 786440 | tf_op jit(solution)/shard_map/ppermute | solution.py:32
  64.7 1.2 slice.137
  65.9 2.7 %convolution_negate_fusion.1 = f32[256,1536]{1,0:T(8,128)S(1)} fusion(f32[256,256]{1,0:T(8,128)S(1)} %convolution_subtract_fusion.2, f32[256,768]{1,0:T(8,128)S(1)} %slice.137, f32[256,768]{1,0:T(8,128)} %slice.133), kind=kOutput, calls=%fused_computation.13 | convolution fusion | flops 1208745984 | bytes 3407872 | tf_op jit(solution)/shard_map/dot_general | solution.py:11
  68.5 1.5 %convolution_add_fusion.1 = f32[256,1536]{1,0:T(8,128)S(1)} fusion(f32[256,1536]{1,0:T(8,128)S(1)} %convolution_negate_fusion.1, f32[256,768]{1,0:T(8,128)S(1)} %copy-done.3, f32[256,1024]{1,0:T(8,128)S(1)} %bitcast.50), kind=kOutput, calls=%fused_computation.11 | convolution fusion | flops 1208352768 | bytes 4194304 | tf_op jit(solution)/shard_map/dot_general | solution.py:11
  70.0 0.2 fusion.51
  70.2 1.3 slice.203
  71.5 0.5 collective-permute-start.6
  72.0 2.7 %convolution_add_fusion = f32[512,1536]{1,0:T(8,128)S(1)} fusion(f32[256,1536]{1,0:T(8,128)S(1)} %convolution_negate_fusion.1, f32[512,768]{1,0:T(8,128)S(1)} %copy-done.2, f32[512,1024]{1,0:T(8,128)S(1)} %bitcast.47), kind=kOutput, calls=%fused_computation.10 | convolution fusion | flops 2416705536 | bytes 6815744 | tf_op jit(solution)/shard_map/dot_general | solution.py:11
  74.8 0.5 broadcast.40.clone
  75.6 1.2 slice.201
  76.8 12.6 %collective-permute-done.1 = f32[256,512]{1,0:T(8,128)S(1)} collective-permute-done((f32[256,512]{1,0:T(8,128)S(1)}, f32[256,512]{1,0:T(8,128)S(1)}, u32[]{:S(2)}, u32[]{:S(2)}) %collective-permute-start.1) | collective-permute-done | bytes 524320 | tf_op jit(solution)/shard_map/ppermute | solution.py:32
  89.3 1.4 %fusion.27 = f32[256,1536]{1,0:T(8,128)S(1)} fusion(f32[256,1536]{1,0:T(8,128)S(1)} %convolution_negate_fusion.1, f32[256,512]{1,0:T(8,128)S(1)} %collective-permute-done.1), kind=kOutput, calls=%fused_computation.61 | convolution fusion | flops 1207959552 | bytes 3407872 | tf_op jit(solution)/shard_map/dot_general | solution.py:11
  90.8 0.8 collective-permute-start.7
  91.7 0.1 maximum_maximum_fusion
  91.8 2.0 %convolution_negate_fusion = f32[256,1536]{1,0:T(8,128)S(1)} fusion(f32[256,256]{1,0:T(8,128)S(1)} %collective-permute-done.4, f32[256,768]{1,0:T(8,128)S(1)} %collective-permute-done.6, f32[256,768]{1,0:T(8,128)} %collective-permute-done.5), kind=kOutput, calls=%fused_computation.12 | convolution fusion | flops 604766208 | bytes 3407872 | tf_op jit(solution)/shard_map/dot_general | solution.py:15
  93.9 1.8 %pad_add_fusion = f32[256,1536]{1,0:T(8,128)S(1)} fusion(f32[256,768]{1,0:T(8,128)S(1)} %slice.201, f32[256,1536]{1,0:T(8,128)S(1)} %convolution_negate_fusion, f32[256,1024]{1,0:T(8,128)} %collective-permute-done.3), kind=kOutput, calls=%fused_computation.20 | convolution fusion | flops 604372992 | bytes 4194304 | tf_op jit(solution)/shard_map/dot_general | solution.py:15
  95.7 0.1 fusion.50
  95.8 0.3 fusion.52
  96.1 17.3 %collective-permute-done.2 = f32[256,512]{1,0:T(8,128)S(1)} collective-permute-done((f32[256,512]{1,0:T(8,128)S(1)}, f32[256,512]{1,0:T(8,128)S(1)}, u32[]{:S(2)}, u32[]{:S(2)}) %collective-permute-start.2) | collective-permute-done | bytes 524320 | tf_op jit(solution)/shard_map/ppermute | solution.py:32
  113.4 1.0 collective-permute-start.8
  114.4 0.1 slice_add_fusion.1
  114.5 0.9 fusion.20
  115.4 0.2 select_reduce_fusion
  115.6 1.1 fusion.10
  116.7 1.3 convolution_subtract_fusion.1
  118.0 1.0 fusion.58
  119.0 0.5 broadcast.40.clone.1
  119.7 1.0 convolution_subtract_fusion
  120.7 1.1 fusion.6
  121.8 4.9 %collective-permute-done.8 = f32[256,512]{1,0:T(8,128)S(1)} collective-permute-done((f32[256,512]{1,0:T(8,128)S(1)}, f32[256,512]{1,0:T(8,128)S(1)}, u32[]{:S(2)}, u32[]{:S(2)}) %collective-permute-start.8) | collective-permute-done | bytes 524320 | tf_op jit(solution)/shard_map/ppermute | solution.py:32
  126.7 0.1 slice_add_fusion
  126.8 0.1 maximum_dynamic-update-slice_fusion.2
  126.9 0.1 maximum_dynamic-update-slice_fusion.3
  127.0 5.3 %subtract_bitcast_fusion = f32[1,1,512,2048]{3,2,1,0:T(8,128)} fusion(f32[512,2048]{1,0:T(8,128)S(1)} %slice_dynamic-update-slice_fusion, f32[512,512]{1,0:T(8,128)S(1)} %fusion.6, f32[512,2048]{1,0:T(8,128)S(1)} %maximum_dynamic-update-slice_fusion.3), kind=kOutput, calls=%fused_computation.9 | convolution fusion | flops 3222274048 | bytes 13631488 | tf_op jit(solution)/shard_map/dot_general | solution.py:15
  (40 shorter events, 0.8 us)
Async XLA Ops:
  0.0 0.7 copy-start
  10.2 50.0 %collective-permute-start = (f32[256,1024]{1,0:T(8,128)}, f32[256,1024]{1,0:T(8,128)}, u32[]{:S(2)}, u32[]{:S(2)}) collective-permute-start(f32[256,1024]{1,0:T(8,128)} %bitcast.7), channel_id=1, source_target_pairs={{0,4},{1,5},{2,6},{3,7},{4,0},{5,1},{6,2},{7,3},{8,12},{9,13},{10,... | collective-permute-start | bytes 3145736 | tf_op jit(solution)/shard_map/ppermute | solution.py:32
  16.3 75.5 %collective-permute-start.5 = (f32[256,768]{1,0:T(8,128)}, f32[256,768]{1,0:T(8,128)}, u32[]{:S(2)}, u32[]{:S(2)}) collective-permute-start(f32[256,768]{1,0:T(8,128)} %slice.133), channel_id=1, source_target_pairs={{0,16},{8,24},{16,0},{24,8},{1,17},{9,25},{17,1},{25,9},{2,18},{10... | collective-permute-start | bytes 2359304 | tf_op jit(solution)/shard_map/ppermute | solution.py:32
  25.8 49.8 %collective-permute-start.3 = (f32[256,1024]{1,0:T(8,128)S(1)}, f32[256,1024]{1,0:T(8,128)}, u32[]{:S(2)}, u32[]{:S(2)}) collective-permute-start(f32[256,1024]{1,0:T(8,128)S(1)} %bitcast.48), channel_id=1, source_target_pairs={{0,16},{8,24},{16,0},{24,8},{1,17},{9,25},{17,1},{25,9},{2,18},{10... | collective-permute-start | bytes 3145736 | tf_op jit(solution)/shard_map/ppermute | solution.py:32
  48.4 16.2 %copy-start.5 = (f32[512,256]{0,1:T(8,128)S(1)}, f32[512,256]{0,1:T(8,128)}, u32[]{:S(2)}) copy-start(f32[512,256]{0,1:T(8,128)} %copy.8) | copy-start | bytes 1572868
  63.0 28.8 %collective-permute-start.4 = (f32[256,256]{1,0:T(8,128)S(1)}, f32[256,256]{1,0:T(8,128)S(1)}, u32[]{:S(2)}, u32[]{:S(2)}) collective-permute-start(f32[256,256]{1,0:T(8,128)S(1)} %convolution_subtract_fusion.2), channel_id=1, source_target_pairs={{0,16},{8,24},{16,0},{24,8},{1,17},{9,25},{17,1},{25,9},{2,18},{10... | collective-permute-start | bytes 786440 | tf_op jit(solution)/shard_map/ppermute | solution.py:32
  64.7 24.7 %collective-permute-start.1 = (f32[256,512]{1,0:T(8,128)S(1)}, f32[256,512]{1,0:T(8,128)S(1)}, u32[]{:S(2)}, u32[]{:S(2)}) collective-permute-start(f32[256,512]{1,0:T(8,128)S(1)} %bitcast.52), channel_id=1, source_target_pairs={{0,4},{1,5},{2,6},{3,7},{4,0},{5,1},{6,2},{7,3},{8,12},{9,13},{10,... | collective-permute-start | bytes 1572872 | tf_op jit(solution)/shard_map/ppermute | solution.py:32
  65.8 2.7 %copy-start.3 = (f32[256,768]{1,0:T(8,128)S(1)}, f32[256,768]{1,0:T(8,128)}, u32[]{:S(2)}) copy-start(f32[256,768]{1,0:T(8,128)} %slice.195) | copy-start | bytes 2359300
  70.0 2.0 %copy-start.2 = (f32[512,768]{1,0:T(8,128)S(1)}, f32[512,768]{1,0:T(8,128)}, u32[]{:S(2)}) copy-start(f32[512,768]{1,0:T(8,128)} %slice.187) | copy-start | bytes 4718596
  71.5 20.4 %collective-permute-start.6 = (f32[256,768]{1,0:T(8,128)S(1)}, f32[256,768]{1,0:T(8,128)S(1)}, u32[]{:S(2)}, u32[]{:S(2)}) collective-permute-start(f32[256,768]{1,0:T(8,128)S(1)} %slice.203), channel_id=1, source_target_pairs={{0,16},{8,24},{16,0},{24,8},{1,17},{9,25},{17,1},{25,9},{2,18},{10... | collective-permute-start | bytes 2359304 | tf_op jit(solution)/shard_map/ppermute | solution.py:32
  75.4 13.9 %copy-start.4 = (f32[512,256]{0,1:T(8,128)S(1)}, f32[512,256]{0,1:T(8,128)}, u32[]{:S(2)}) copy-start(f32[512,256]{0,1:T(8,128)} %copy.12) | copy-start | bytes 1572868
  89.3 24.0 %collective-permute-start.2 = (f32[256,512]{1,0:T(8,128)S(1)}, f32[256,512]{1,0:T(8,128)S(1)}, u32[]{:S(2)}, u32[]{:S(2)}) collective-permute-start(f32[256,512]{1,0:T(8,128)S(1)} %bitcast.51), channel_id=1, source_target_pairs={{0,4},{1,5},{2,6},{3,7},{4,0},{5,1},{6,2},{7,3},{8,12},{9,13},{10,... | collective-permute-start | bytes 1572872 | tf_op jit(solution)/shard_map/ppermute | solution.py:32
  90.8 23.6 %collective-permute-start.7 = (f32[256,512]{1,0:T(8,128)S(1)}, f32[256,512]{1,0:T(8,128)S(1)}, u32[]{:S(2)}, u32[]{:S(2)}) collective-permute-start(f32[256,512]{1,0:T(8,128)S(1)} %collective-permute-done.1), channel_id=1, source_target_pairs={{0,16},{8,24},{16,0},{24,8},{1,17},{9,25},{17,1},{25,9},{2,18},{10... | collective-permute-start | bytes 1572872 | tf_op jit(solution)/shard_map/ppermute | solution.py:32
  113.4 13.3 %collective-permute-start.8 = (f32[256,512]{1,0:T(8,128)S(1)}, f32[256,512]{1,0:T(8,128)S(1)}, u32[]{:S(2)}, u32[]{:S(2)}) collective-permute-start(f32[256,512]{1,0:T(8,128)S(1)} %collective-permute-done.2), channel_id=1, source_target_pairs={{0,16},{8,24},{16,0},{24,8},{1,17},{9,25},{17,1},{25,9},{2,18},{10... | collective-permute-start | bytes 1572872 | tf_op jit(solution)/shard_map/ppermute | solution.py:32
  127.0 5.3 %copy-start.1 = (s32[1,1,4,256]{3,2,1,0:T(4,128)S(1)}, s32[1,1,4,256]{3,2,1,0:T(4,128)}, u32[]{:S(2)}) copy-start(s32[1,1,4,256]{3,2,1,0:T(4,128)} %param.3) | copy-start | bytes 12292

commit v11 on v10

--- a/solution.py
+++ b/solution.py
@@ -124,7 +124,7 @@
         ),
     ]
     coupling_two = jnp.zeros((2 * width, 8 * width), jnp.float32)
-    for rel, block in enumerate(blocks):
+    for rel, block in enumerate(blocks[:3]):
         start = jnp.bitwise_xor(own_id, rel) * (2 * width)
         coupling_two = lax.dynamic_update_slice(coupling_two, block, (0, start))
     own_block = jnp.zeros((2 * width, 8 * width), jnp.float32)
@@ -132,6 +132,12 @@
     mate_start = jnp.bitwise_xor(own_id, 1) * (2 * width)
     own_block = lax.dynamic_update_slice(own_block, own_ext[:, 3 * width : 5 * width], (0, mate_start))
     merged = own_block - matmul_high(weights, coupling_two)
+    merged, diag_b = lax.optimization_barrier((merged, diag_b))
+    blocks[3] = jnp.concatenate(
+        [vert_int[:, 3 * width : 5 * width], diag_prod[:, 3 * width : 5 * width] + diag_b], 0
+    )
+    last_start = jnp.bitwise_xor(own_id, 3) * (2 * width)
+    merged = lax.dynamic_update_slice(merged, -matmul_high(weights, blocks[3]), (0, last_start))
     return merged[None, None]
 
 

time: 133 us -> 132 us (level)
  waiting for transfers between devices: 46.4 us -> 42 us
  matrix products: 25.3 us -> 27.4 us
    ppermute x9, waiting for transfers between devices: 46.4 us -> 42 us  [swap(): return lax.ppermute(value, axis, pairs)]
    dot_general x9 -> x10, matrix products: 15.4 us -> 17.4 us  [matmul_high(): jnp.dot(left, right, precision=lax.Precision.HIGH, preferred_element_type...]
  transfers between devices with their start and end apart: 9 -> 9, of which waited for: 4 -> 3; matrix products, arithmetic and copies ran while one was open for 45% -> 49% of each run, Pallas kernels for 0% -> 0%
where the time goes in v11:
time: 132 us; the launch traced here: 131 us
  local copies, waits for them, and re-layouts  48.9 us (37%)
  waiting for transfers between devices  42 us (32%)
  matrix products  27.4 us (21%)
  starting transfers between devices  10.1 us (8%)
  other arithmetic  2.38 us (2%)
    ppermute x9, waiting for transfers between devices, swap(): return lax.ppermute(value, axis, pairs)  42 us
    gather x10, local copies, waits for them, and re-layouts, pick(): return jnp.take(picked, cols, axis=1, mode='clip')  20.7 us
    dot_general x10, matrix products, matmul_high(): jnp.dot(left, right, precision=lax.Precision.HIGH, preferred_element_type...  17.4 us
    gather x6, local copies, waits for them, and re-layouts, pick(): picked = jnp.take(matrix, rows, axis=0, mode='clip')  15.9 us
    ppermute x9, starting transfers between devices, swap(): return lax.ppermute(value, axis, pairs)  10.1 us
    dot_general x8, matrix products, matmul(): jnp.dot(left, right, precision=lax.Precision.HIGHEST, preferred_element_t...  9.94 us
    slice x3, local copies, waits for them, and re-layouts, first_rows(): rows[:, width:]  3.41 us
    slice x2, local copies, waits for them, and re-layouts, body(): solved_own = pair_solve(inverse_own, own_i1[:, width:], side_i1[:, width:])  3.29 us
  transfers between devices with their start and end apart: 9, of which 3 were waited for; matrix products, arithmetic and copies ran while one was open for 49% of the time, Pallas kernels for 0%

profile of v11, /device:TPU:0, one launch (start us, length us, event | category | flops | bytes accessed | tf_op | source)
XLA Modules:
  0.0 131.2 jit_solution(2360575786327069473)
XLA Ops:
  0.1 0.6 copy-done
  0.7 0.6 gather_fusion
  1.3 3.8 %gather_fusion.1 = f32[256,1024]{1,0:T(8,128)S(1)} fusion(f32[1024,1024]{1,0:T(8,128)} %bitcast.47, s32[1024]{0:T(1024)S(1)} %pad_clamp_fusion.3), kind=kCustom, calls=%fused_computation.1 | custom fusion | bytes 2098176 | tf_op jit(solution)/shard_map/jit(_take)/gather | solution.py:62
  5.1 0.3 copy.3
  5.4 3.5 %gather_fusion.2 = f32[1024,256]{1,0:T(8,128)S(1)} fusion(f32[256,1024]{0,1:T(8,128)S(1)} %copy.3, s32[1024]{0:T(1024)S(1)} %broadcast_clamp_fusion), kind=kCustom, calls=%fused_computation.2 | custom fusion | bytes 2101248 | tf_op jit(solution)/shard_map/jit(_take)/gather | solution.py:63
  8.9 1.3 %copy.4 = f32[1024,256]{0,1:T(8,128)} copy(f32[1024,256]{1,0:T(8,128)S(1)} %gather_fusion.2) | data formatting | bytes 2097152 | tf_op jit(solution)/shard_map/jit(_take)/gather | solution.py:63
  10.2 4.0 %collective-permute-start = (f32[256,1024]{1,0:T(8,128)}, f32[256,1024]{1,0:T(8,128)}, u32[]{:S(2)}, u32[]{:S(2)}) collective-permute-start(f32[256,1024]{1,0:T(8,128)} %bitcast.7), channel_id=1, source_target_pairs={{0,4},{1,5},{2,6},{3,7},{4,0},{5,1},{6,2},{7,3},{8,12},{9,13},{10,... | collective-permute-start | bytes 3145736 | tf_op jit(solution)/shard_map/ppermute | solution.py:32
  14.2 2.1 %slice.133 = f32[256,768]{1,0:T(8,128)} slice(f32[256,1024]{1,0:T(8,128)} %bitcast.7), slice={[0:256], [256:1024]} | slice | bytes 1572864 | tf_op jit(solution)/shard_map/slice | solution.py:93
  16.3 1.5 %collective-permute-start.5 = (f32[256,768]{1,0:T(8,128)}, f32[256,768]{1,0:T(8,128)}, u32[]{:S(2)}, u32[]{:S(2)}) collective-permute-start(f32[256,768]{1,0:T(8,128)} %slice.133), channel_id=1, source_target_pairs={{0,16},{8,24},{16,0},{24,8},{1,17},{9,25},{17,1},{25,9},{2,18},{10... | collective-permute-start | bytes 2359304 | tf_op jit(solution)/shard_map/ppermute | solution.py:32
  17.9 3.8 %gather_fusion.5 = f32[256,1024]{1,0:T(8,128)S(1)} fusion(f32[1024,1024]{1,0:T(8,128)} %bitcast.48, s32[1024]{0:T(1024)S(1)} %pad_clamp_fusion.1), kind=kCustom, calls=%fused_computation.5 | custom fusion | bytes 2098176 | tf_op jit(solution)/shard_map/jit(_take)/gather | solution.py:62
  21.6 0.3 copy.7
  22.0 3.5 %gather_fusion.7 = f32[1024,256]{1,0:T(8,128)S(1)} fusion(f32[256,1024]{0,1:T(8,128)S(1)} %copy.7, s32[1024]{0:T(1024)S(1)} %broadcast_clamp_fusion), kind=kCustom, calls=%fused_computation.7 | custom fusion | bytes 2101248 | tf_op jit(solution)/shard_map/jit(_take)/gather | solution.py:63
  25.4 0.3 copy.10
  25.8 0.6 collective-permute-start.3
  26.4 1.0 slice.195
  27.3 1.6 %gather_fusion.8 = f32[512,256]{1,0:T(8,128)S(1)} fusion(f32[256,1024]{0,1:T(8,128)S(1)} %copy.7, s32[1024]{0:T(1024)S(1)} %pad_clamp_fusion.2), kind=kCustom, calls=%fused_computation.8 | custom fusion | bytes 1050624 | tf_op jit(solution)/shard_map/jit(_take)/gather | solution.py:63
  28.9 5.8 %gather_fusion.3 = f32[512,1024]{1,0:T(8,128)} fusion(f32[1024,1024]{1,0:T(8,128)} %bitcast.49, s32[1024]{0:T(1024)S(1)} %pad_clamp_fusion.2), kind=kCustom, calls=%fused_computation.3 | custom fusion | bytes 4196352 | tf_op jit(solution)/shard_map/jit(_take)/gather | solution.py:62
  34.7 1.6 %gather_fusion.6 = f32[512,256]{1,0:T(8,128)S(1)} fusion(f32[256,1024]{0,1:T(8,128)S(1)} %copy.7, s32[1024]{0:T(1024)S(1)} %pad_clamp_fusion), kind=kCustom, calls=%fused_computation.6 | custom fusion | bytes 1050624 | tf_op jit(solution)/shard_map/jit(_take)/gather | solution.py:63
  36.3 1.0 copy.8
  37.3 1.0 copy.12
  38.3 1.9 %copy.5 = f32[512,1024]{0,1:T(8,128)S(1)} copy(f32[512,1024]{1,0:T(8,128)} %gather_fusion.3) | data formatting | bytes 4194304 | tf_op jit(solution)/shard_map/jit(_take)/gather | solution.py:62
  40.2 4.9 %gather_fusion.4 = f32[1024,512]{1,0:T(8,128)} fusion(f32[512,1024]{0,1:T(8,128)S(1)} %copy.5, s32[1024]{0:T(1024)S(1)} %broadcast_clamp_fusion), kind=kCustom, calls=%fused_computation.4 | custom fusion | bytes 4198400 | tf_op jit(solution)/shard_map/jit(_take)/gather | solution.py:63
  45.1 2.1 %copy.6 = f32[1024,512]{0,1:T(8,128)S(1)} copy(f32[1024,512]{1,0:T(8,128)} %gather_fusion.4) | data formatting | bytes 4194304 | tf_op jit(solution)/shard_map/jit(_take)/gather | solution.py:63
  47.2 1.3 slice.187
  48.5 11.7 %collective-permute-done = f32[256,1024]{1,0:T(8,128)} collective-permute-done((f32[256,1024]{1,0:T(8,128)}, f32[256,1024]{1,0:T(8,128)}, u32[]{:S(2)}, u32[]{:S(2)}) %collective-permute-start) | collective-permute-done | bytes 1048608 | tf_op jit(solution)/shard_map/ppermute | solution.py:32
  60.2 1.1 select_reduce_fusion.1
  61.3 0.4 fusion.34
  61.8 0.5 convolution_subtract_fusion.4
  62.3 0.4 fusion.63
  62.6 0.4 convolution_subtract_fusion.3
  63.0 1.6 %collective-permute-start.4 = (f32[256,256]{1,0:T(8,128)S(1)}, f32[256,256]{1,0:T(8,128)S(1)}, u32[]{:S(2)}, u32[]{:S(2)}) collective-permute-start(f32[256,256]{1,0:T(8,128)S(1)} %convolution_subtract_fusion.3), channel_id=1, source_target_pairs={{0,16},{8,24},{16,0},{24,8},{1,17},{9,25},{17,1},{25,9},{2,18},{10... | collective-permute-start | bytes 786440 | tf_op jit(solution)/shard_map/ppermute | solution.py:32
  64.7 1.2 slice.137
  65.9 2.7 %convolution_negate_fusion.1 = f32[256,1536]{1,0:T(8,128)S(1)} fusion(f32[256,256]{1,0:T(8,128)S(1)} %convolution_subtract_fusion.3, f32[256,768]{1,0:T(8,128)S(1)} %slice.137, f32[256,768]{1,0:T(8,128)} %slice.133), kind=kOutput, calls=%fused_computation.13 | convolution fusion | flops 1208745984 | bytes 3407872 | tf_op jit(solution)/shard_map/dot_general | solution.py:11
  68.5 1.2 slice.203
  69.7 0.5 collective-permute-start.6
  70.3 1.5 %convolution_add_fusion.1 = f32[256,1536]{1,0:T(8,128)S(1)} fusion(f32[256,1536]{1,0:T(8,128)S(1)} %convolution_negate_fusion.1, f32[256,768]{1,0:T(8,128)S(1)} %copy-done.5, f32[256,1024]{1,0:T(8,128)S(1)} %bitcast.54), kind=kOutput, calls=%fused_computation.11 | convolution fusion | flops 1208352768 | bytes 4194304 | tf_op jit(solution)/shard_map/dot_general | solution.py:11
  71.8 2.7 %convolution_add_fusion = f32[512,1536]{1,0:T(8,128)S(1)} fusion(f32[256,1536]{1,0:T(8,128)S(1)} %convolution_negate_fusion.1, f32[512,768]{1,0:T(8,128)S(1)} %copy-done.4, f32[512,1024]{1,0:T(8,128)S(1)} %bitcast.51), kind=kOutput, calls=%fused_computation.9 | convolution fusion | flops 2416705536 | bytes 6815744 | tf_op jit(solution)/shard_map/dot_general | solution.py:11
  74.5 0.2 fusion.57
  74.7 0.5 broadcast.40.clone
  75.2 0.1 slice_dynamic-update-slice_fusion.1
  75.4 1.2 slice.201
  76.6 12.7 %collective-permute-done.1 = f32[256,512]{1,0:T(8,128)S(1)} collective-permute-done((f32[256,512]{1,0:T(8,128)S(1)}, f32[256,512]{1,0:T(8,128)S(1)}, u32[]{:S(2)}, u32[]{:S(2)}) %collective-permute-start.1) | collective-permute-done | bytes 524320 | tf_op jit(solution)/shard_map/ppermute | solution.py:32
  89.3 1.4 %fusion.32 = f32[256,1536]{1,0:T(8,128)S(1)} fusion(f32[256,1536]{1,0:T(8,128)S(1)} %convolution_negate_fusion.1, f32[256,512]{1,0:T(8,128)S(1)} %collective-permute-done.1), kind=kOutput, calls=%fused_computation.66 | convolution fusion | flops 1207959552 | bytes 3407872 | tf_op jit(solution)/shard_map/dot_general | solution.py:11
  90.9 0.8 collective-permute-start.7
  91.7 0.1 maximum_maximum_fusion
  91.8 2.0 %convolution_negate_fusion = f32[256,1536]{1,0:T(8,128)S(1)} fusion(f32[256,256]{1,0:T(8,128)S(1)} %collective-permute-done.4, f32[256,768]{1,0:T(8,128)S(1)} %collective-permute-done.6, f32[256,768]{1,0:T(8,128)} %collective-permute-done.5), kind=kOutput, calls=%fused_computation.12 | convolution fusion | flops 604766208 | bytes 3407872 | tf_op jit(solution)/shard_map/dot_general | solution.py:15
  93.9 1.8 %pad_add_fusion = f32[256,1536]{1,0:T(8,128)S(1)} fusion(f32[256,768]{1,0:T(8,128)S(1)} %slice.201, f32[256,1536]{1,0:T(8,128)S(1)} %convolution_negate_fusion, f32[256,1024]{1,0:T(8,128)} %collective-permute-done.3), kind=kOutput, calls=%fused_computation.20 | convolution fusion | flops 604372992 | bytes 4194304 | tf_op jit(solution)/shard_map/dot_general | solution.py:15
  95.8 17.6 %collective-permute-done.2 = f32[256,512]{1,0:T(8,128)S(1)} collective-permute-done((f32[256,512]{1,0:T(8,128)S(1)}, f32[256,512]{1,0:T(8,128)S(1)}, u32[]{:S(2)}, u32[]{:S(2)}) %collective-permute-start.2) | collective-permute-done | bytes 524320 | tf_op jit(solution)/shard_map/ppermute | solution.py:32
  113.4 1.0 collective-permute-start.8
  114.4 0.1 slice_add_fusion.1
  114.5 0.9 fusion.25
  115.5 0.2 select_reduce_fusion
  115.7 0.9 copy-done.2
  116.6 1.1 fusion.15
  117.6 1.3 convolution_subtract_fusion.2
  118.9 1.0 fusion.64
  119.9 1.0 convolution_subtract_fusion.1
  120.9 1.0 fusion.8
  122.0 0.5 broadcast.40.clone.1
  122.5 0.1 maximum_dynamic-update-slice_fusion
  122.7 0.8 slice-done
  123.5 0.3 slice_dynamic-update-slice_fusion
  123.9 5.3 %convolution_subtract_fusion = f32[512,2048]{1,0:T(8,128)} fusion(f32[512,2048]{1,0:T(8,128)S(1)} %get-tuple-element.47, f32[512,512]{1,0:T(8,128)S(1)} %fusion.8, f32[512,2048]{1,0:T(8,128)S(1)} %get-tuple-element.48), kind=kOutput, calls=%fused_computation.10 | convolution fusion | flops 3222274048 | bytes 13631488 | tf_op jit(solution)/shard_map/dot_general | solution.py:15
  129.2 2.0 %fusion.7 = f32[1,1,512,2048]{3,2,1,0:T(8,128)} fusion(f32[1,1,512,2048]{3,2,1,0:T(8,128)} %bitcast.55, s32[]{:T(128)S(6)} %select_n.37, f32[512,512]{1,0:T(8,128)S(1)} %fusion.8, f32[256,512]{1,0:T(8,128)S(1)} %slice_add_fusion, f32[256,512]{1,0:T(8,128)S(1)} %get-tuple-element.31), kind=kOutput, calls=%fused_computation.23 | convolution fusion | flops 805830656 | bytes 3145732 | tf_op jit(solution)/shard_map/dot_general | solution.py:15
  (45 shorter events, 0.7 us)
Async XLA Ops:
  0.0 0.7 copy-start
  10.2 50.0 %collective-permute-start = (f32[256,1024]{1,0:T(8,128)}, f32[256,1024]{1,0:T(8,128)}, u32[]{:S(2)}, u32[]{:S(2)}) collective-permute-start(f32[256,1024]{1,0:T(8,128)} %bitcast.7), channel_id=1, source_target_pairs={{0,4},{1,5},{2,6},{3,7},{4,0},{5,1},{6,2},{7,3},{8,12},{9,13},{10,... | collective-permute-start | bytes 3145736 | tf_op jit(solution)/shard_map/ppermute | solution.py:32
  16.3 75.5 %collective-permute-start.5 = (f32[256,768]{1,0:T(8,128)}, f32[256,768]{1,0:T(8,128)}, u32[]{:S(2)}, u32[]{:S(2)}) collective-permute-start(f32[256,768]{1,0:T(8,128)} %slice.133), channel_id=1, source_target_pairs={{0,16},{8,24},{16,0},{24,8},{1,17},{9,25},{17,1},{25,9},{2,18},{10... | collective-permute-start | bytes 2359304 | tf_op jit(solution)/shard_map/ppermute | solution.py:32
  25.8 49.6 %collective-permute-start.3 = (f32[256,1024]{1,0:T(8,128)S(1)}, f32[256,1024]{1,0:T(8,128)}, u32[]{:S(2)}, u32[]{:S(2)}) collective-permute-start(f32[256,1024]{1,0:T(8,128)S(1)} %bitcast.52), channel_id=1, source_target_pairs={{0,16},{8,24},{16,0},{24,8},{1,17},{9,25},{17,1},{25,9},{2,18},{10... | collective-permute-start | bytes 3145736 | tf_op jit(solution)/shard_map/ppermute | solution.py:32
  48.5 16.2 %copy-start.7 = (f32[512,256]{0,1:T(8,128)S(1)}, f32[512,256]{0,1:T(8,128)}, u32[]{:S(2)}) copy-start(f32[512,256]{0,1:T(8,128)} %copy.8) | copy-start | bytes 1572868
  63.0 28.8 %collective-permute-start.4 = (f32[256,256]{1,0:T(8,128)S(1)}, f32[256,256]{1,0:T(8,128)S(1)}, u32[]{:S(2)}, u32[]{:S(2)}) collective-permute-start(f32[256,256]{1,0:T(8,128)S(1)} %convolution_subtract_fusion.3), channel_id=1, source_target_pairs={{0,16},{8,24},{16,0},{24,8},{1,17},{9,25},{17,1},{25,9},{2,18},{10... | collective-permute-start | bytes 786440 | tf_op jit(solution)/shard_map/ppermute | solution.py:32
  64.7 24.7 %collective-permute-start.1 = (f32[256,512]{1,0:T(8,128)S(1)}, f32[256,512]{1,0:T(8,128)S(1)}, u32[]{:S(2)}, u32[]{:S(2)}) collective-permute-start(f32[256,512]{1,0:T(8,128)S(1)} %bitcast.57), channel_id=1, source_target_pairs={{0,4},{1,5},{2,6},{3,7},{4,0},{5,1},{6,2},{7,3},{8,12},{9,13},{10,... | collective-permute-start | bytes 1572872 | tf_op jit(solution)/shard_map/ppermute | solution.py:32
  65.9 4.4 %copy-start.5 = (f32[256,768]{1,0:T(8,128)S(1)}, f32[256,768]{1,0:T(8,128)}, u32[]{:S(2)}) copy-start(f32[256,768]{1,0:T(8,128)} %slice.195) | copy-start | bytes 2359300
  69.7 2.0 %copy-start.4 = (f32[512,768]{1,0:T(8,128)S(1)}, f32[512,768]{1,0:T(8,128)}, u32[]{:S(2)}) copy-start(f32[512,768]{1,0:T(8,128)} %slice.187) | copy-start | bytes 4718596
  69.7 22.1 %collective-permute-start.6 = (f32[256,768]{1,0:T(8,128)S(1)}, f32[256,768]{1,0:T(8,128)S(1)}, u32[]{:S(2)}, u32[]{:S(2)}) collective-permute-start(f32[256,768]{1,0:T(8,128)S(1)} %slice.203), channel_id=1, source_target_pairs={{0,16},{8,24},{16,0},{24,8},{1,17},{9,25},{17,1},{25,9},{2,18},{10... | collective-permute-start | bytes 2359304 | tf_op jit(solution)/shard_map/ppermute | solution.py:32
  75.2 14.1 %copy-start.6 = (f32[512,256]{0,1:T(8,128)S(1)}, f32[512,256]{0,1:T(8,128)}, u32[]{:S(2)}) copy-start(f32[512,256]{0,1:T(8,128)} %copy.12) | copy-start | bytes 1572868
  89.3 24.0 %collective-permute-start.2 = (f32[256,512]{1,0:T(8,128)S(1)}, f32[256,512]{1,0:T(8,128)S(1)}, u32[]{:S(2)}, u32[]{:S(2)}) collective-permute-start(f32[256,512]{1,0:T(8,128)S(1)} %bitcast.56), channel_id=1, source_target_pairs={{0,4},{1,5},{2,6},{3,7},{4,0},{5,1},{6,2},{7,3},{8,12},{9,13},{10,... | collective-permute-start | bytes 1572872 | tf_op jit(solution)/shard_map/ppermute | solution.py:32
  90.9 23.6 %collective-permute-start.7 = (f32[256,512]{1,0:T(8,128)S(1)}, f32[256,512]{1,0:T(8,128)S(1)}, u32[]{:S(2)}, u32[]{:S(2)}) collective-permute-start(f32[256,512]{1,0:T(8,128)S(1)} %collective-permute-done.1), channel_id=1, source_target_pairs={{0,16},{8,24},{16,0},{24,8},{1,17},{9,25},{17,1},{25,9},{2,18},{10... | collective-permute-start | bytes 1572872 | tf_op jit(solution)/shard_map/ppermute | solution.py:32
  113.4 15.8 %collective-permute-start.8 = (f32[256,512]{1,0:T(8,128)S(1)}, f32[256,512]{1,0:T(8,128)S(1)}, u32[]{:S(2)}, u32[]{:S(2)}) collective-permute-start(f32[256,512]{1,0:T(8,128)S(1)} %collective-permute-done.2), channel_id=1, source_target_pairs={{0,16},{8,24},{16,0},{24,8},{1,17},{9,25},{17,1},{25,9},{2,18},{10... | collective-permute-start | bytes 1572872 | tf_op jit(solution)/shard_map/ppermute | solution.py:32
  115.4 1.2 copy-start.2
  122.5 1.0 slice-start
  123.8 5.3 %copy-start.3 = (f32[256,1536]{1,0:T(8,128)S(1)}, f32[256,1536]{1,0:T(8,128)}, u32[]{:S(2)}) copy-start(f32[256,1536]{1,0:T(8,128)} %copy-done.2) | copy-start | bytes 4718596
  123.8 7.4 %copy-start.1 = (s32[1,1,4,256]{3,2,1,0:T(4,128)S(1)}, s32[1,1,4,256]{3,2,1,0:T(4,128)}, u32[]{:S(2)}) copy-start(s32[1,1,4,256]{3,2,1,0:T(4,128)} %param.3) | copy-start | bytes 12292

commit v12 on v11

--- a/solution.py
+++ b/solution.py
@@ -123,15 +123,15 @@
             [vert_int[:, 3 * width : 5 * width], diag_prod[:, 3 * width : 5 * width] + diag_b], 0
         ),
     ]
-    coupling_two = jnp.zeros((2 * width, 8 * width), jnp.float32)
-    for rel, block in enumerate(blocks[:3]):
+    first_three = matmul_high(weights, jnp.concatenate(blocks[:3], 1))
+    own_parts = [own_ext[:, 0 : 2 * width], own_ext[:, 3 * width : 5 * width], None]
+    merged = jnp.zeros((2 * width, 8 * width), jnp.float32)
+    for rel, own_part in enumerate(own_parts):
+        piece = -first_three[:, rel * 2 * width : (rel + 1) * 2 * width]
+        if own_part is not None:
+            piece = own_part + piece
         start = jnp.bitwise_xor(own_id, rel) * (2 * width)
-        coupling_two = lax.dynamic_update_slice(coupling_two, block, (0, start))
-    own_block = jnp.zeros((2 * width, 8 * width), jnp.float32)
-    own_block = lax.dynamic_update_slice(own_block, own_ext[:, 0 : 2 * width], (0, own_id * (2 * width)))
-    mate_start = jnp.bitwise_xor(own_id, 1) * (2 * width)
-    own_block = lax.dynamic_update_slice(own_block, own_ext[:, 3 * width : 5 * width], (0, mate_start))
-    merged = own_block - matmul_high(weights, coupling_two)
+        merged = lax.dynamic_update_slice(merged, piece, (0, start))
     merged, diag_b = lax.optimization_barrier((merged, diag_b))
     blocks[3] = jnp.concatenate(
         [vert_int[:, 3 * width : 5 * width], diag_prod[:, 3 * width : 5 * width] + diag_b], 0

time: 132 us -> 138 us (1.045)
  waiting for transfers between devices: 42 us -> 47.2 us
  local copies, waits for them, and re-layouts: 48.9 us -> 51.6 us
  matrix products: 27.4 us -> 25.2 us
    ppermute x9, waiting for transfers between devices: 42 us -> 47.2 us  [swap(): return lax.ppermute(value, axis, pairs)]
    unnamed x19 -> x21, local copies, waits for them, and re-layouts: 1.53 us -> 3.94 us
    dot_general x10, matrix products: 17.4 us -> 15.2 us  [matmul_high(): jnp.dot(left, right, precision=lax.Precision.HIGH, preferred_element_type...]
    gather x10, local copies, waits for them, and re-layouts: 20.7 us -> 22.4 us  [pick(): return jnp.take(picked, cols, axis=1, mode='clip')]
  transfers between devices with their start and end apart: 9 -> 9, of which waited for: 3 -> 4; matrix products, arithmetic and copies ran while one was open for 49% -> 46% of each run, Pallas kernels for 0% -> 0%
where the time goes in v12:
time: 138 us
  local copies, waits for them, and re-layouts  51.6 us (37%)
  waiting for transfers between devices  47.2 us (34%)
  matrix products  25.2 us (18%)
  starting transfers between devices  10.8 us (8%)
  other arithmetic  2.38 us (2%)
    ppermute x9, waiting for transfers between devices, swap(): return lax.ppermute(value, axis, pairs)  47.2 us
    gather x10, local copies, waits for them, and re-layouts, pick(): return jnp.take(picked, cols, axis=1, mode='clip')  22.4 us
    gather x6, local copies, waits for them, and re-layouts, pick(): picked = jnp.take(matrix, rows, axis=0, mode='clip')  15.9 us
    dot_general x10, matrix products, matmul_high(): jnp.dot(left, right, precision=lax.Precision.HIGH, preferred_element_type...  15.2 us
    ppermute x9, starting transfers between devices, swap(): return lax.ppermute(value, axis, pairs)  10.8 us
    dot_general x8, matrix products, matmul(): jnp.dot(left, right, precision=lax.Precision.HIGHEST, preferred_element_t...  10 us
    unnamed x21, local copies, waits for them, and re-layouts  3.94 us
    slice x3, local copies, waits for them, and re-layouts, first_rows(): rows[:, width:]  3.41 us
  transfers between devices with their start and end apart: 9, of which 4 were waited for; matrix products, arithmetic and copies ran while one was open for 46% of the time, Pallas kernels for 0%

profile of v12, /device:TPU:0, one launch (start us, length us, event | category | flops | bytes accessed | tf_op | source)
XLA Modules:
  0.0 137.6 jit_solution(4037188360154071399)
XLA Ops:
  0.1 0.6 copy-done
  0.7 0.6 gather_fusion
  1.3 3.8 %gather_fusion.1 = f32[256,1024]{1,0:T(8,128)S(1)} fusion(f32[1024,1024]{1,0:T(8,128)} %bitcast.46, s32[1024]{0:T(1024)S(1)} %pad_clamp_fusion.3), kind=kCustom, calls=%fused_computation.1 | custom fusion | bytes 2098176 | tf_op jit(solution)/shard_map/jit(_take)/gather | solution.py:62
  5.0 0.3 copy.3
  5.4 3.5 %gather_fusion.2 = f32[1024,256]{1,0:T(8,128)S(1)} fusion(f32[256,1024]{0,1:T(8,128)S(1)} %copy.3, s32[1024]{0:T(1024)S(1)} %broadcast_clamp_fusion), kind=kCustom, calls=%fused_computation.2 | custom fusion | bytes 2101248 | tf_op jit(solution)/shard_map/jit(_take)/gather | solution.py:63
  8.9 1.3 copy.4
  10.2 4.0 %collective-permute-start = (f32[256,1024]{1,0:T(8,128)}, f32[256,1024]{1,0:T(8,128)}, u32[]{:S(2)}, u32[]{:S(2)}) collective-permute-start(f32[256,1024]{1,0:T(8,128)} %bitcast.7), channel_id=1, source_target_pairs={{0,4},{1,5},{2,6},{3,7},{4,0},{5,1},{6,2},{7,3},{8,12},{9,13},{10,... | collective-permute-start | bytes 3145736 | tf_op jit(solution)/shard_map/ppermute | solution.py:32
  14.2 2.1 %slice.142 = f32[256,768]{1,0:T(8,128)} slice(f32[256,1024]{1,0:T(8,128)} %bitcast.7), slice={[0:256], [256:1024]} | slice | bytes 1572864 | tf_op jit(solution)/shard_map/slice | solution.py:93
  16.3 1.5 %collective-permute-start.5 = (f32[256,768]{1,0:T(8,128)}, f32[256,768]{1,0:T(8,128)}, u32[]{:S(2)}, u32[]{:S(2)}) collective-permute-start(f32[256,768]{1,0:T(8,128)} %slice.142), channel_id=1, source_target_pairs={{0,16},{8,24},{16,0},{24,8},{1,17},{9,25},{17,1},{25,9},{2,18},{10... | collective-permute-start | bytes 2359304 | tf_op jit(solution)/shard_map/ppermute | solution.py:32
  17.9 3.8 %gather_fusion.5 = f32[256,1024]{1,0:T(8,128)S(1)} fusion(f32[1024,1024]{1,0:T(8,128)} %bitcast.47, s32[1024]{0:T(1024)S(1)} %pad_clamp_fusion.1), kind=kCustom, calls=%fused_computation.5 | custom fusion | bytes 2098176 | tf_op jit(solution)/shard_map/jit(_take)/gather | solution.py:62
  21.6 0.3 copy.7
  22.0 3.5 %gather_fusion.7 = f32[1024,256]{1,0:T(8,128)S(1)} fusion(f32[256,1024]{0,1:T(8,128)S(1)} %copy.7, s32[1024]{0:T(1024)S(1)} %broadcast_clamp_fusion), kind=kCustom, calls=%fused_computation.7 | custom fusion | bytes 2101248 | tf_op jit(solution)/shard_map/jit(_take)/gather | solution.py:63
  25.4 0.3 copy.10
  25.8 0.6 collective-permute-start.3
  26.3 1.0 slice.206
  27.3 5.8 %gather_fusion.3 = f32[512,1024]{1,0:T(8,128)} fusion(f32[1024,1024]{1,0:T(8,128)} %bitcast.48, s32[1024]{0:T(1024)S(1)} %pad_clamp_fusion.2), kind=kCustom, calls=%fused_computation.3 | custom fusion | bytes 4196352 | tf_op jit(solution)/shard_map/jit(_take)/gather | solution.py:62
  33.1 2.2 %gather_fusion.8 = f32[512,256]{1,0:T(8,128)} fusion(f32[256,1024]{0,1:T(8,128)S(1)} %copy.7, s32[1024]{0:T(1024)S(1)} %pad_clamp_fusion.2), kind=kCustom, calls=%fused_computation.8 | custom fusion | bytes 1050624 | tf_op jit(solution)/shard_map/jit(_take)/gather | solution.py:63
  35.4 1.6 %gather_fusion.6 = f32[512,256]{1,0:T(8,128)S(1)} fusion(f32[256,1024]{0,1:T(8,128)S(1)} %copy.7, s32[1024]{0:T(1024)S(1)} %pad_clamp_fusion), kind=kCustom, calls=%fused_computation.6 | custom fusion | bytes 1050624 | tf_op jit(solution)/shard_map/jit(_take)/gather | solution.py:63
  36.9 1.0 copy.8
  38.0 1.9 %copy.5 = f32[512,1024]{0,1:T(8,128)S(1)} copy(f32[512,1024]{1,0:T(8,128)} %gather_fusion.3) | data formatting | bytes 4194304 | tf_op jit(solution)/shard_map/jit(_take)/gather | solution.py:62
  39.9 4.9 %gather_fusion.4 = f32[1024,512]{1,0:T(8,128)} fusion(f32[512,1024]{0,1:T(8,128)S(1)} %copy.5, s32[1024]{0:T(1024)S(1)} %broadcast_clamp_fusion), kind=kCustom, calls=%fused_computation.4 | custom fusion | bytes 4198400 | tf_op jit(solution)/shard_map/jit(_take)/gather | solution.py:63
  44.8 2.1 %copy.6 = f32[1024,512]{0,1:T(8,128)S(1)} copy(f32[1024,512]{1,0:T(8,128)} %gather_fusion.4) | data formatting | bytes 4194304 | tf_op jit(solution)/shard_map/jit(_take)/gather | solution.py:63
  46.9 1.3 slice.199
  48.1 2.0 %copy.12 = f32[512,256]{0,1:T(8,128)} copy(f32[512,256]{1,0:T(8,128)} %gather_fusion.8) | data formatting | bytes 1048576 | tf_op jit(solution)/shard_map/jit(_take)/gather | solution.py:63
  50.2 10.0 %collective-permute-done = f32[256,1024]{1,0:T(8,128)} collective-permute-done((f32[256,1024]{1,0:T(8,128)}, f32[256,1024]{1,0:T(8,128)}, u32[]{:S(2)}, u32[]{:S(2)}) %collective-permute-start) | collective-permute-done | bytes 1048608 | tf_op jit(solution)/shard_map/ppermute | solution.py:32
  60.2 1.2 slice.146
  61.3 1.1 select_reduce_fusion.1
  62.5 0.4 fusion.51
  62.9 0.5 convolution_subtract_fusion.3
  63.4 0.4 fusion.82
  63.8 0.4 convolution_subtract_fusion.2
  64.2 1.6 %collective-permute-start.4 = (f32[256,256]{1,0:T(8,128)S(1)}, f32[256,256]{1,0:T(8,128)S(1)}, u32[]{:S(2)}, u32[]{:S(2)}) collective-permute-start(f32[256,256]{1,0:T(8,128)S(1)} %convolution_subtract_fusion.2), channel_id=1, source_target_pairs={{0,16},{8,24},{16,0},{24,8},{1,17},{9,25},{17,1},{25,9},{2,18},{10... | collective-permute-start | bytes 786440 | tf_op jit(solution)/shard_map/ppermute | solution.py:32
  65.9 2.6 %convolution_negate_fusion.1 = f32[256,1536]{1,0:T(8,128)S(1)} fusion(f32[256,256]{1,0:T(8,128)S(1)} %convolution_subtract_fusion.2, f32[256,768]{1,0:T(8,128)S(1)} %slice.146, f32[256,768]{1,0:T(8,128)} %slice.142), kind=kOutput, calls=%fused_computation.24 | convolution fusion | flops 1208745984 | bytes 3407872 | tf_op jit(solution)/shard_map/dot_general | solution.py:11
  68.4 1.2 slice.214
  69.6 0.6 collective-permute-start.6
  70.3 2.9 %convolution_add_fusion = f32[512,1536]{1,0:T(8,128)S(1)} fusion(f32[256,1536]{1,0:T(8,128)S(1)} %convolution_negate_fusion.1, f32[512,768]{1,0:T(8,128)S(1)} %copy-done.4, f32[512,1024]{1,0:T(8,128)S(1)} %bitcast.50), kind=kOutput, calls=%fused_computation.9 | convolution fusion | flops 2416705536 | bytes 6815744 | tf_op jit(solution)/shard_map/dot_general | solution.py:11
  73.2 1.0 copy-done.6
  74.3 1.5 %convolution_add_fusion.1 = f32[256,1536]{1,0:T(8,128)S(1)} fusion(f32[256,1536]{1,0:T(8,128)S(1)} %convolution_negate_fusion.1, f32[256,768]{1,0:T(8,128)S(1)} %copy-done.6, f32[256,1024]{1,0:T(8,128)S(1)} %bitcast.53), kind=kOutput, calls=%fused_computation.22 | convolution fusion | flops 1208352768 | bytes 4194304 | tf_op jit(solution)/shard_map/dot_general | solution.py:11
  75.7 0.1 fusion.75
  75.9 1.2 slice.212
  77.1 17.8 %collective-permute-done.1 = f32[256,512]{1,0:T(8,128)S(1)} collective-permute-done((f32[256,512]{1,0:T(8,128)S(1)}, f32[256,512]{1,0:T(8,128)S(1)}, u32[]{:S(2)}, u32[]{:S(2)}) %collective-permute-start.1) | collective-permute-done | bytes 524320 | tf_op jit(solution)/shard_map/ppermute | solution.py:32
  94.9 1.4 %fusion.49 = f32[256,1536]{1,0:T(8,128)S(1)} fusion(f32[256,1536]{1,0:T(8,128)S(1)} %convolution_negate_fusion.1, f32[256,512]{1,0:T(8,128)S(1)} %collective-permute-done.1), kind=kOutput, calls=%fused_computation.80 | convolution fusion | flops 1207959552 | bytes 3407872 | tf_op jit(solution)/shard_map/dot_general | solution.py:11
  96.5 1.3 collective-permute-start.7
  97.8 0.1 maximum_maximum_fusion
  98.0 2.0 %convolution_negate_fusion = f32[256,1536]{1,0:T(8,128)S(1)} fusion(f32[256,256]{1,0:T(8,128)S(1)} %collective-permute-done.4, f32[256,768]{1,0:T(8,128)S(1)} %collective-permute-done.6, f32[256,768]{1,0:T(8,128)} %collective-permute-done.5), kind=kOutput, calls=%fused_computation.23 | convolution fusion | flops 604766208 | bytes 3407872 | tf_op jit(solution)/shard_map/dot_general | solution.py:15
  99.9 1.8 %pad_add_fusion = f32[256,1536]{1,0:T(8,128)S(1)} fusion(f32[256,768]{1,0:T(8,128)S(1)} %slice.212, f32[256,1536]{1,0:T(8,128)S(1)} %convolution_negate_fusion, f32[256,1024]{1,0:T(8,128)} %collective-permute-done.3), kind=kOutput, calls=%fused_computation.31 | convolution fusion | flops 604372992 | bytes 4194304 | tf_op jit(solution)/shard_map/dot_general | solution.py:15
  101.9 18.7 %collective-permute-done.2 = f32[256,512]{1,0:T(8,128)S(1)} collective-permute-done((f32[256,512]{1,0:T(8,128)S(1)}, f32[256,512]{1,0:T(8,128)S(1)}, u32[]{:S(2)}, u32[]{:S(2)}) %collective-permute-start.2) | collective-permute-done | bytes 524320 | tf_op jit(solution)/shard_map/ppermute | solution.py:32
  120.7 1.0 collective-permute-start.8
  121.9 1.1 fusion.42
  123.1 0.2 select_reduce_fusion
  123.2 0.9 copy-done.2
  124.2 1.1 fusion.32
  125.2 1.3 convolution_subtract_fusion.1
  126.5 1.0 fusion.83
  127.5 1.0 convolution_subtract_fusion
  128.5 1.1 fusion.25
  129.6 2.9 %fusion = f32[512,1536]{1,0:T(8,128)S(1)} fusion(f32[512,512]{1,0:T(8,128)S(1)} %fusion.25, f32[256,512]{1,0:T(8,128)S(1)} %slice-done, f32[256,512]{1,0:T(8,128)S(1)} %get-tuple-element.32, f32[256,512]{1,0:T(8,128)S(1)} %get-tuple-element.36, f32[256,512]{1,0:T(8,128)S(1)} %get-tuple-element.34, f32[256,512]{1,0:T(8,128)S(1)} %get-tuple-element.35, ...), kind=kOutput, calls=%fused_computation.10 | convolution fusion | flops 2419851264 | bytes 7340032 | tf_op jit(solution)/shard_map/dot_general | solution.py:15
  132.5 0.5 broadcast_in_dim.48
  133.0 0.2 fusion.24
  133.3 0.1 fusion.22
  133.5 0.6 collective-permute-done.8
  134.1 0.9 copy-done.3
  135.1 0.4 copy-done.5
  135.5 2.0 %fusion.19 = f32[1,1,512,2048]{3,2,1,0:T(8,128)} fusion(f32[1,1,512,2048]{3,2,1,0:T(8,128)} %bitcast.54, s32[]{:T(128)S(6)} %select_n.35, f32[512,512]{1,0:T(8,128)S(1)} %fusion.25, f32[256,512]{1,0:T(8,128)S(1)} %slice_add_fusion, f32[256,512]{1,0:T(8,128)S(1)} %get-tuple-element.31), kind=kOutput, calls=%fused_computation.34 | convolution fusion | flops 805830656 | bytes 3145732 | tf_op jit(solution)/shard_map/dot_general | solution.py:15
  (45 shorter events, 0.9 us)
Async XLA Ops:
  0.0 0.7 copy-start
  10.2 50.0 %collective-permute-start = (f32[256,1024]{1,0:T(8,128)}, f32[256,1024]{1,0:T(8,128)}, u32[]{:S(2)}, u32[]{:S(2)}) collective-permute-start(f32[256,1024]{1,0:T(8,128)} %bitcast.7), channel_id=1, source_target_pairs={{0,4},{1,5},{2,6},{3,7},{4,0},{5,1},{6,2},{7,3},{8,12},{9,13},{10,... | collective-permute-start | bytes 3145736 | tf_op jit(solution)/shard_map/ppermute | solution.py:32
  16.3 81.6 %collective-permute-start.5 = (f32[256,768]{1,0:T(8,128)}, f32[256,768]{1,0:T(8,128)}, u32[]{:S(2)}, u32[]{:S(2)}) collective-permute-start(f32[256,768]{1,0:T(8,128)} %slice.142), channel_id=1, source_target_pairs={{0,16},{8,24},{16,0},{24,8},{1,17},{9,25},{17,1},{25,9},{2,18},{10... | collective-permute-start | bytes 2359304 | tf_op jit(solution)/shard_map/ppermute | solution.py:32
  25.8 50.1 %collective-permute-start.3 = (f32[256,1024]{1,0:T(8,128)S(1)}, f32[256,1024]{1,0:T(8,128)}, u32[]{:S(2)}, u32[]{:S(2)}) collective-permute-start(f32[256,1024]{1,0:T(8,128)S(1)} %bitcast.51), channel_id=1, source_target_pairs={{0,16},{8,24},{16,0},{24,8},{1,17},{9,25},{17,1},{25,9},{2,18},{10... | collective-permute-start | bytes 3145736 | tf_op jit(solution)/shard_map/ppermute | solution.py:32
  64.2 6.1 %copy-start.8 = (f32[512,256]{0,1:T(8,128)S(1)}, f32[512,256]{0,1:T(8,128)}, u32[]{:S(2)}) copy-start(f32[512,256]{0,1:T(8,128)} %copy.8) | copy-start | bytes 1572868
  64.2 6.0 %copy-start.4 = (f32[512,768]{1,0:T(8,128)S(1)}, f32[512,768]{1,0:T(8,128)}, u32[]{:S(2)}) copy-start(f32[512,768]{1,0:T(8,128)} %slice.199) | copy-start | bytes 4718596
  64.2 33.7 %collective-permute-start.4 = (f32[256,256]{1,0:T(8,128)S(1)}, f32[256,256]{1,0:T(8,128)S(1)}, u32[]{:S(2)}, u32[]{:S(2)}) collective-permute-start(f32[256,256]{1,0:T(8,128)S(1)} %convolution_subtract_fusion.2), channel_id=1, source_target_pairs={{0,16},{8,24},{16,0},{24,8},{1,17},{9,25},{17,1},{25,9},{2,18},{10... | collective-permute-start | bytes 786440 | tf_op jit(solution)/shard_map/ppermute | solution.py:32
  69.6 28.3 %collective-permute-start.6 = (f32[256,768]{1,0:T(8,128)S(1)}, f32[256,768]{1,0:T(8,128)S(1)}, u32[]{:S(2)}, u32[]{:S(2)}) collective-permute-start(f32[256,768]{1,0:T(8,128)S(1)} %slice.214), channel_id=1, source_target_pairs={{0,16},{8,24},{16,0},{24,8},{1,17},{9,25},{17,1},{25,9},{2,18},{10... | collective-permute-start | bytes 2359304 | tf_op jit(solution)/shard_map/ppermute | solution.py:32
  70.2 24.7 %collective-permute-start.1 = (f32[256,512]{1,0:T(8,128)S(1)}, f32[256,512]{1,0:T(8,128)S(1)}, u32[]{:S(2)}, u32[]{:S(2)}) collective-permute-start(f32[256,512]{1,0:T(8,128)S(1)} %bitcast.56), channel_id=1, source_target_pairs={{0,4},{1,5},{2,6},{3,7},{4,0},{5,1},{6,2},{7,3},{8,12},{9,13},{10,... | collective-permute-start | bytes 1572872 | tf_op jit(solution)/shard_map/ppermute | solution.py:32
  73.1 1.1 copy-start.6
  94.9 1.5 %copy-start.7 = (f32[512,256]{0,1:T(8,128)S(1)}, f32[512,256]{0,1:T(8,128)}, u32[]{:S(2)}) copy-start(f32[512,256]{0,1:T(8,128)} %copy.12) | copy-start | bytes 1572868
  96.4 24.3 %collective-permute-start.2 = (f32[256,512]{1,0:T(8,128)S(1)}, f32[256,512]{1,0:T(8,128)S(1)}, u32[]{:S(2)}, u32[]{:S(2)}) collective-permute-start(f32[256,512]{1,0:T(8,128)S(1)} %bitcast.55), channel_id=1, source_target_pairs={{0,4},{1,5},{2,6},{3,7},{4,0},{5,1},{6,2},{7,3},{8,12},{9,13},{10,... | collective-permute-start | bytes 1572872 | tf_op jit(solution)/shard_map/ppermute | solution.py:32
  96.5 25.3 %collective-permute-start.7 = (f32[256,512]{1,0:T(8,128)S(1)}, f32[256,512]{1,0:T(8,128)S(1)}, u32[]{:S(2)}, u32[]{:S(2)}) collective-permute-start(f32[256,512]{1,0:T(8,128)S(1)} %collective-permute-done.1), channel_id=1, source_target_pairs={{0,16},{8,24},{16,0},{24,8},{1,17},{9,25},{17,1},{25,9},{2,18},{10... | collective-permute-start | bytes 1572872 | tf_op jit(solution)/shard_map/ppermute | solution.py:32
  120.7 13.4 %collective-permute-start.8 = (f32[256,512]{1,0:T(8,128)S(1)}, f32[256,512]{1,0:T(8,128)S(1)}, u32[]{:S(2)}, u32[]{:S(2)}) collective-permute-start(f32[256,512]{1,0:T(8,128)S(1)} %collective-permute-done.2), channel_id=1, source_target_pairs={{0,16},{8,24},{16,0},{24,8},{1,17},{9,25},{17,1},{25,9},{2,18},{10... | collective-permute-start | bytes 1572872 | tf_op jit(solution)/shard_map/ppermute | solution.py:32
  123.0 1.2 copy-start.2
  128.5 1.1 slice-start
  133.2 1.8 %copy-start.3 = (f32[256,1536]{1,0:T(8,128)S(1)}, f32[256,1536]{1,0:T(8,128)}, u32[]{:S(2)}) copy-start(f32[256,1536]{1,0:T(8,128)} %copy-done.2) | copy-start | bytes 4718596
  133.4 4.2 %copy-start.1 = (s32[1,1,4,256]{3,2,1,0:T(4,128)S(1)}, s32[1,1,4,256]{3,2,1,0:T(4,128)}, u32[]{:S(2)}) copy-start(s32[1,1,4,256]{3,2,1,0:T(4,128)} %param.3) | copy-start | bytes 12292
  133.5 2.0 %copy-start.5 = (f32[512,2048]{1,0:T(8,128)}, f32[512,2048]{1,0:T(8,128)S(1)}, u32[]{:S(2)}) copy-start(f32[512,2048]{1,0:T(8,128)S(1)} %fusion.20) | copy-start | bytes 12582916

commit v13 on v11

--- a/solution.py
+++ b/solution.py
@@ -74,16 +74,19 @@
     own_i1 = pick(leaf, perm[:width], perm)
     leaf, own_i1 = lax.optimization_barrier((leaf, own_i1))
     own_i2 = pick(leaf, perm[3 * width :], perm)
-    own_a = pick(leaf, perm[3 * width :], jnp.concatenate([perm[:width], perm[3 * width :]]))
-    own_b = pick(leaf, perm[3 * width :], perm[width : 3 * width])
+    split_order = jnp.concatenate([perm[:width], perm[3 * width :], perm[width : 3 * width]])
+    own_split = pick(leaf, perm[3 * width :], split_order)
+    own_a = own_split[:, : 2 * width]
+    own_b = own_split[:, 2 * width :]
     own_ov = pick(leaf, perm[width : 3 * width], perm)
 
     vert_ie = swap(own_i1[:, width:], "grp")
     vert_i2 = swap(own_i2, "grp")
     side_i1 = swap(own_i1, "box")
     diag_ie = swap(side_i1[:, width:], "grp")
-    inverse_own = newton(own_i1[:, :width] + side_i1[:, :width], ITERS_LOW)
-    inverse_other = swap(inverse_own, "grp")
+    system_own = own_i1[:, :width] + side_i1[:, :width]
+    inverse_other = newton(swap(system_own, "grp"), ITERS_LOW)
+    inverse_own = newton(system_own, ITERS_LOW)
     part_a, side_i1 = lax.optimization_barrier((own_a, side_i1))
     side_a = swap(part_a, "box")
     diag_a = swap(side_a, "grp")

time: 132 us -> 132 us (level)
  waiting for transfers between devices: 42 us -> 38.1 us
  local copies, waits for them, and re-layouts: 48.9 us -> 50.9 us
  matrix products: 27.4 us -> 29.2 us
    ppermute x9, waiting for transfers between devices: 42 us -> 38.1 us  [swap(): return lax.ppermute(value, axis, pairs)]
    dot_general x8 -> x12, matrix products: 9.94 us -> 11.5 us  [matmul(): jnp.dot(left, right, precision=lax.Precision.HIGHEST, preferred_element_t...]
    unnamed x19 -> x15, local copies, waits for them, and re-layouts: 1.53 us -> 2.75 us
    gather x10 -> x8, local copies, waits for them, and re-layouts: 20.7 us -> 20.3 us  [pick(): return jnp.take(picked, cols, axis=1, mode='clip')]
  transfers between devices with their start and end apart: 9 -> 9, of which waited for: 3 -> 3; matrix products, arithmetic and copies ran while one was open for 49% -> 51% of each run, Pallas kernels for 0% -> 0%
where the time goes in v13:
time: 132 us; the launch traced here: 131 us
  local copies, waits for them, and re-layouts  50.9 us (39%)
  waiting for transfers between devices  38.1 us (29%)
  matrix products  29.2 us (22%)
  starting transfers between devices  10.1 us (8%)
  other arithmetic  2.48 us (2%)
    ppermute x9, waiting for transfers between devices, swap(): return lax.ppermute(value, axis, pairs)  38.1 us
    gather x8, local copies, waits for them, and re-layouts, pick(): return jnp.take(picked, cols, axis=1, mode='clip')  20.3 us
    dot_general x10, matrix products, matmul_high(): jnp.dot(left, right, precision=lax.Precision.HIGH, preferred_element_type...  17.7 us
    gather x6, local copies, waits for them, and re-layouts, pick(): picked = jnp.take(matrix, rows, axis=0, mode='clip')  15.9 us
    dot_general x12, matrix products, matmul(): jnp.dot(left, right, precision=lax.Precision.HIGHEST, preferred_element_t...  11.5 us
    ppermute x9, starting transfers between devices, swap(): return lax.ppermute(value, axis, pairs)  10.1 us
    slice x3, local copies, waits for them, and re-layouts, first_rows(): rows[:, width:]  3.4 us
    slice x2, local copies, waits for them, and re-layouts, body(): solved_own = pair_solve(inverse_own, own_i1[:, width:], side_i1[:, width:])  3.28 us
  transfers between devices with their start and end apart: 9, of which 3 were waited for; matrix products, arithmetic and copies ran while one was open for 51% of the time, Pallas kernels for 0%

profile of v13, /device:TPU:0, one launch (start us, length us, event | category | flops | bytes accessed | tf_op | source)
XLA Modules:
  0.0 131.3 jit_solution(2645006690420581531)
XLA Ops:
  0.1 0.6 copy-done
  0.7 0.6 gather_fusion
  1.3 3.8 %gather_fusion.1 = f32[256,1024]{1,0:T(8,128)S(1)} fusion(f32[1024,1024]{1,0:T(8,128)} %bitcast.52, s32[1024]{0:T(1024)S(1)} %get-tuple-element.51), kind=kCustom, calls=%fused_computation.1 | custom fusion | bytes 2098176 | tf_op jit(solution)/shard_map/jit(_take)/gather | solution.py:62
  5.1 0.3 copy.3
  5.4 3.5 %gather_fusion.2 = f32[1024,256]{1,0:T(8,128)S(1)} fusion(f32[256,1024]{0,1:T(8,128)S(1)} %copy.3, s32[1024]{0:T(1024)S(1)} %broadcast_clamp_fusion), kind=kCustom, calls=%fused_computation.2 | custom fusion | bytes 2101248 | tf_op jit(solution)/shard_map/jit(_take)/gather | solution.py:63
  8.9 1.3 copy.4
  10.2 4.0 %collective-permute-start = (f32[256,1024]{1,0:T(8,128)}, f32[256,1024]{1,0:T(8,128)}, u32[]{:S(2)}, u32[]{:S(2)}) collective-permute-start(f32[256,1024]{1,0:T(8,128)} %bitcast.7), channel_id=1, source_target_pairs={{0,4},{1,5},{2,6},{3,7},{4,0},{5,1},{6,2},{7,3},{8,12},{9,13},{10,... | collective-permute-start | bytes 3145736 | tf_op jit(solution)/shard_map/ppermute | solution.py:32
  14.2 2.1 %slice.140 = f32[256,768]{1,0:T(8,128)} slice(f32[256,1024]{1,0:T(8,128)} %bitcast.7), slice={[0:256], [256:1024]} | slice | bytes 1572864 | tf_op jit(solution)/shard_map/slice | solution.py:96
  16.3 1.5 %collective-permute-start.5 = (f32[256,768]{1,0:T(8,128)}, f32[256,768]{1,0:T(8,128)}, u32[]{:S(2)}, u32[]{:S(2)}) collective-permute-start(f32[256,768]{1,0:T(8,128)} %slice.140), channel_id=1, source_target_pairs={{0,16},{8,24},{16,0},{24,8},{1,17},{9,25},{17,1},{25,9},{2,18},{10... | collective-permute-start | bytes 2359304 | tf_op jit(solution)/shard_map/ppermute | solution.py:32
  17.9 3.8 %gather_fusion.5 = f32[256,1024]{1,0:T(8,128)S(1)} fusion(f32[1024,1024]{1,0:T(8,128)} %bitcast.53, s32[1024]{0:T(1024)S(1)} %get-tuple-element.52), kind=kCustom, calls=%fused_computation.5 | custom fusion | bytes 2098176 | tf_op jit(solution)/shard_map/jit(_take)/gather | solution.py:62
  21.6 0.3 copy.7
  22.0 3.5 %gather_fusion.7 = f32[1024,256]{1,0:T(8,128)S(1)} fusion(f32[256,1024]{0,1:T(8,128)S(1)} %copy.7, s32[1024]{0:T(1024)S(1)} %broadcast_clamp_fusion), kind=kCustom, calls=%fused_computation.7 | custom fusion | bytes 2101248 | tf_op jit(solution)/shard_map/jit(_take)/gather | solution.py:63
  25.4 0.3 copy.10
  25.8 0.6 collective-permute-start.3
  26.4 1.0 slice.204
  27.3 3.5 %gather_fusion.6 = f32[1024,256]{1,0:T(8,128)S(1)} fusion(f32[256,1024]{0,1:T(8,128)S(1)} %copy.7, s32[1024]{0:T(1024)S(1)} %get-tuple-element.50), kind=kCustom, calls=%fused_computation.6 | custom fusion | bytes 2101248 | tf_op jit(solution)/shard_map/jit(_take)/gather | solution.py:63
  30.8 1.3 copy.8
  32.1 5.8 %gather_fusion.3 = f32[512,1024]{1,0:T(8,128)} fusion(f32[1024,1024]{1,0:T(8,128)} %bitcast.54, s32[1024]{0:T(1024)S(1)} %get-tuple-element.49), kind=kCustom, calls=%fused_computation.3 | custom fusion | bytes 4196352 | tf_op jit(solution)/shard_map/jit(_take)/gather | solution.py:62
  37.9 1.9 %copy.5 = f32[512,1024]{0,1:T(8,128)S(1)} copy(f32[512,1024]{1,0:T(8,128)} %gather_fusion.3) | data formatting | bytes 4194304 | tf_op jit(solution)/shard_map/jit(_take)/gather | solution.py:62
  39.8 4.9 %gather_fusion.4 = f32[1024,512]{1,0:T(8,128)} fusion(f32[512,1024]{0,1:T(8,128)S(1)} %copy.5, s32[1024]{0:T(1024)S(1)} %broadcast_clamp_fusion), kind=kCustom, calls=%fused_computation.4 | custom fusion | bytes 4198400 | tf_op jit(solution)/shard_map/jit(_take)/gather | solution.py:63
  44.7 2.1 %copy.6 = f32[1024,512]{0,1:T(8,128)S(1)} copy(f32[1024,512]{1,0:T(8,128)} %gather_fusion.4) | data formatting | bytes 4194304 | tf_op jit(solution)/shard_map/jit(_take)/gather | solution.py:63
  46.8 1.3 slice.195
  48.0 1.3 fusion.84
  49.3 10.9 %collective-permute-done = f32[256,1024]{1,0:T(8,128)} collective-permute-done((f32[256,1024]{1,0:T(8,128)}, f32[256,1024]{1,0:T(8,128)}, u32[]{:S(2)}, u32[]{:S(2)}) %collective-permute-start) | collective-permute-done | bytes 1048608 | tf_op jit(solution)/shard_map/ppermute | solution.py:32
  60.2 1.1 select_reduce_fusion.2
  61.4 1.6 %collective-permute-start.4 = (f32[256,256]{1,0:T(8,128)S(1)}, f32[256,256]{1,0:T(8,128)S(1)}, u32[]{:S(2)}, u32[]{:S(2)}) collective-permute-start(f32[256,256]{1,0:T(8,128)S(1)} %get-tuple-element.28), channel_id=1, source_target_pairs={{0,16},{8,24},{16,0},{24,8},{1,17},{9,25},{17,1},{25,9},{2,18},{10... | collective-permute-start | bytes 786440 | tf_op jit(solution)/shard_map/ppermute | solution.py:32
  63.0 0.4 fusion.36
  63.4 0.5 convolution_subtract_fusion.5
  63.9 0.4 fusion.86
  64.3 0.4 convolution_subtract_fusion.4
  64.7 1.2 slice.146
  65.9 1.2 slice.213
  67.1 0.5 collective-permute-start.6
  67.7 2.6 %convolution_negate_fusion.1 = f32[256,1536]{1,0:T(8,128)S(1)} fusion(f32[256,256]{1,0:T(8,128)S(1)} %convolution_subtract_fusion.4, f32[256,768]{1,0:T(8,128)S(1)} %slice.146, f32[256,768]{1,0:T(8,128)} %slice.140), kind=kOutput, calls=%fused_computation.12 | convolution fusion | flops 1208745984 | bytes 3407872 | tf_op jit(solution)/shard_map/dot_general | solution.py:11
  70.3 1.5 %convolution_add_fusion.1 = f32[256,1536]{1,0:T(8,128)S(1)} fusion(f32[256,1536]{1,0:T(8,128)S(1)} %convolution_negate_fusion.1, f32[256,768]{1,0:T(8,128)S(1)} %copy-done.5, f32[256,1024]{1,0:T(8,128)S(1)} %bitcast.59), kind=kOutput, calls=%fused_computation.10 | convolution fusion | flops 1208352768 | bytes 4194304 | tf_op jit(solution)/shard_map/dot_general | solution.py:11
  71.9 1.2 copy-done.4
  73.2 2.7 %convolution_add_fusion = f32[512,1536]{1,0:T(8,128)S(1)} fusion(f32[256,1536]{1,0:T(8,128)S(1)} %convolution_negate_fusion.1, f32[512,768]{1,0:T(8,128)S(1)} %copy-done.4, f32[512,1024]{1,0:T(8,128)S(1)} %bitcast.56), kind=kOutput, calls=%fused_computation.8 | convolution fusion | flops 2416705536 | bytes 6815744 | tf_op jit(solution)/shard_map/dot_general | solution.py:11
  75.9 0.5 broadcast.52.clone
  76.5 1.2 slice.211
  77.9 0.4 fusion.41
  78.3 0.5 multiply_subtract_fusion.3
  78.8 0.4 fusion.87
  79.2 0.4 convolution_subtract_fusion.3
  79.6 9.8 %collective-permute-done.1 = f32[256,512]{1,0:T(8,128)S(1)} collective-permute-done((f32[256,512]{1,0:T(8,128)S(1)}, f32[256,512]{1,0:T(8,128)S(1)}, u32[]{:S(2)}, u32[]{:S(2)}) %collective-permute-start.1) | collective-permute-done | bytes 524320 | tf_op jit(solution)/shard_map/ppermute | solution.py:32
  89.4 0.8 collective-permute-start.7
  90.2 1.4 %fusion.34 = f32[256,1536]{1,0:T(8,128)S(1)} fusion(f32[256,1536]{1,0:T(8,128)S(1)} %convolution_negate_fusion.1, f32[256,512]{1,0:T(8,128)S(1)} %collective-permute-done.1), kind=kOutput, calls=%fused_computation.72 | convolution fusion | flops 1207959552 | bytes 3407872 | tf_op jit(solution)/shard_map/dot_general | solution.py:11
  91.7 0.1 maximum_maximum_fusion
  91.8 2.2 %convolution_negate_fusion = f32[256,1536]{1,0:T(8,128)S(1)} fusion(f32[256,256]{1,0:T(8,128)S(1)} %convolution_subtract_fusion.3, f32[256,768]{1,0:T(8,128)S(1)} %collective-permute-done.6, f32[256,768]{1,0:T(8,128)} %collective-permute-done.5), kind=kOutput, calls=%fused_computation.11 | convolution fusion | flops 604766208 | bytes 3407872 | tf_op jit(solution)/shard_map/dot_general | solution.py:15
  94.1 1.8 %pad_add_fusion = f32[256,1536]{1,0:T(8,128)S(1)} fusion(f32[256,768]{1,0:T(8,128)S(1)} %slice.211, f32[256,1536]{1,0:T(8,128)S(1)} %convolution_negate_fusion, f32[256,1024]{1,0:T(8,128)} %collective-permute-done.3), kind=kOutput, calls=%fused_computation.19 | convolution fusion | flops 604372992 | bytes 4194304 | tf_op jit(solution)/shard_map/dot_general | solution.py:15
  96.1 17.4 %collective-permute-done.2 = f32[256,512]{1,0:T(8,128)S(1)} collective-permute-done((f32[256,512]{1,0:T(8,128)S(1)}, f32[256,512]{1,0:T(8,128)S(1)}, u32[]{:S(2)}, u32[]{:S(2)}) %collective-permute-start.2) | collective-permute-done | bytes 524320 | tf_op jit(solution)/shard_map/ppermute | solution.py:32
  113.4 1.0 collective-permute-start.8
  114.6 0.9 fusion.27
  115.5 0.2 select_reduce_fusion
  115.7 0.9 copy-done.2
  116.6 1.1 fusion.15
  117.7 1.3 convolution_subtract_fusion.2
  119.0 1.0 fusion.88
  120.0 1.0 convolution_subtract_fusion.1
  121.0 1.0 fusion.8
  122.1 0.5 broadcast.52.clone.1
  122.8 0.8 slice-done
  123.6 0.3 slice_dynamic-update-slice_fusion
  123.9 5.3 %convolution_subtract_fusion = f32[512,2048]{1,0:T(8,128)} fusion(f32[512,2048]{1,0:T(8,128)S(1)} %get-tuple-element.53, f32[512,512]{1,0:T(8,128)S(1)} %fusion.8, f32[512,2048]{1,0:T(8,128)S(1)} %get-tuple-element.54), kind=kOutput, calls=%fused_computation.9 | convolution fusion | flops 3222274048 | bytes 13631488 | tf_op jit(solution)/shard_map/dot_general | solution.py:15
  129.3 2.0 %fusion.7 = f32[1,1,512,2048]{3,2,1,0:T(8,128)} fusion(f32[1,1,512,2048]{3,2,1,0:T(8,128)} %bitcast.60, s32[]{:T(128)S(6)} %select_n.41, f32[512,512]{1,0:T(8,128)S(1)} %fusion.8, f32[256,512]{1,0:T(8,128)S(1)} %slice_add_fusion, f32[256,512]{1,0:T(8,128)S(1)} %get-tuple-element.31), kind=kOutput, calls=%fused_computation.22 | convolution fusion | flops 805830656 | bytes 3145732 | tf_op jit(solution)/shard_map/dot_general | solution.py:15
  (42 shorter events, 1.3 us)
Async XLA Ops:
  0.0 0.7 copy-start
  10.2 50.0 %collective-permute-start = (f32[256,1024]{1,0:T(8,128)}, f32[256,1024]{1,0:T(8,128)}, u32[]{:S(2)}, u32[]{:S(2)}) collective-permute-start(f32[256,1024]{1,0:T(8,128)} %bitcast.7), channel_id=1, source_target_pairs={{0,4},{1,5},{2,6},{3,7},{4,0},{5,1},{6,2},{7,3},{8,12},{9,13},{10,... | collective-permute-start | bytes 3145736 | tf_op jit(solution)/shard_map/ppermute | solution.py:32
  16.3 75.5 %collective-permute-start.5 = (f32[256,768]{1,0:T(8,128)}, f32[256,768]{1,0:T(8,128)}, u32[]{:S(2)}, u32[]{:S(2)}) collective-permute-start(f32[256,768]{1,0:T(8,128)} %slice.140), channel_id=1, source_target_pairs={{0,16},{8,24},{16,0},{24,8},{1,17},{9,25},{17,1},{25,9},{2,18},{10... | collective-permute-start | bytes 2359304 | tf_op jit(solution)/shard_map/ppermute | solution.py:32
  25.8 50.7 %collective-permute-start.3 = (f32[256,1024]{1,0:T(8,128)S(1)}, f32[256,1024]{1,0:T(8,128)}, u32[]{:S(2)}, u32[]{:S(2)}) collective-permute-start(f32[256,1024]{1,0:T(8,128)S(1)} %bitcast.57), channel_id=1, source_target_pairs={{0,16},{8,24},{16,0},{24,8},{1,17},{9,25},{17,1},{25,9},{2,18},{10... | collective-permute-start | bytes 3145736 | tf_op jit(solution)/shard_map/ppermute | solution.py:32
  61.4 16.4 %collective-permute-start.4 = (f32[256,256]{1,0:T(8,128)S(1)}, f32[256,256]{1,0:T(8,128)S(1)}, u32[]{:S(2)}, u32[]{:S(2)}) collective-permute-start(f32[256,256]{1,0:T(8,128)S(1)} %get-tuple-element.28), channel_id=1, source_target_pairs={{0,16},{8,24},{16,0},{24,8},{1,17},{9,25},{17,1},{25,9},{2,18},{10... | collective-permute-start | bytes 786440 | tf_op jit(solution)/shard_map/ppermute | solution.py:32
  64.7 24.7 %collective-permute-start.1 = (f32[256,512]{1,0:T(8,128)S(1)}, f32[256,512]{1,0:T(8,128)S(1)}, u32[]{:S(2)}, u32[]{:S(2)}) collective-permute-start(f32[256,512]{1,0:T(8,128)S(1)} %get-tuple-element.18), channel_id=1, source_target_pairs={{0,4},{1,5},{2,6},{3,7},{4,0},{5,1},{6,2},{7,3},{8,12},{9,13},{10,... | collective-permute-start | bytes 1572872 | tf_op jit(solution)/shard_map/ppermute | solution.py:32
  67.1 3.1 %copy-start.5 = (f32[256,768]{1,0:T(8,128)S(1)}, f32[256,768]{1,0:T(8,128)}, u32[]{:S(2)}) copy-start(f32[256,768]{1,0:T(8,128)} %slice.204) | copy-start | bytes 2359300
  67.1 24.7 %collective-permute-start.6 = (f32[256,768]{1,0:T(8,128)S(1)}, f32[256,768]{1,0:T(8,128)S(1)}, u32[]{:S(2)}, u32[]{:S(2)}) collective-permute-start(f32[256,768]{1,0:T(8,128)S(1)} %slice.213), channel_id=1, source_target_pairs={{0,16},{8,24},{16,0},{24,8},{1,17},{9,25},{17,1},{25,9},{2,18},{10... | collective-permute-start | bytes 2359304 | tf_op jit(solution)/shard_map/ppermute | solution.py:32
  71.8 1.4 %copy-start.4 = (f32[512,768]{1,0:T(8,128)S(1)}, f32[512,768]{1,0:T(8,128)}, u32[]{:S(2)}) copy-start(f32[512,768]{1,0:T(8,128)} %slice.195) | copy-start | bytes 4718596
  89.4 24.0 %collective-permute-start.2 = (f32[256,512]{1,0:T(8,128)S(1)}, f32[256,512]{1,0:T(8,128)S(1)}, u32[]{:S(2)}, u32[]{:S(2)}) collective-permute-start(f32[256,512]{1,0:T(8,128)S(1)} %get-tuple-element.20), channel_id=1, source_target_pairs={{0,4},{1,5},{2,6},{3,7},{4,0},{5,1},{6,2},{7,3},{8,12},{9,13},{10,... | collective-permute-start | bytes 1572872 | tf_op jit(solution)/shard_map/ppermute | solution.py:32
  89.4 25.1 %collective-permute-start.7 = (f32[256,512]{1,0:T(8,128)S(1)}, f32[256,512]{1,0:T(8,128)S(1)}, u32[]{:S(2)}, u32[]{:S(2)}) collective-permute-start(f32[256,512]{1,0:T(8,128)S(1)} %collective-permute-done.1), channel_id=1, source_target_pairs={{0,16},{8,24},{16,0},{24,8},{1,17},{9,25},{17,1},{25,9},{2,18},{10... | collective-permute-start | bytes 1572872 | tf_op jit(solution)/shard_map/ppermute | solution.py:32
  113.4 15.8 %collective-permute-start.8 = (f32[256,512]{1,0:T(8,128)S(1)}, f32[256,512]{1,0:T(8,128)S(1)}, u32[]{:S(2)}, u32[]{:S(2)}) collective-permute-start(f32[256,512]{1,0:T(8,128)S(1)} %collective-permute-done.2), channel_id=1, source_target_pairs={{0,16},{8,24},{16,0},{24,8},{1,17},{9,25},{17,1},{25,9},{2,18},{10... | collective-permute-start | bytes 1572872 | tf_op jit(solution)/shard_map/ppermute | solution.py:32
  115.5 1.2 copy-start.2
  122.6 1.0 slice-start
  123.9 5.3 %copy-start.3 = (f32[256,1536]{1,0:T(8,128)S(1)}, f32[256,1536]{1,0:T(8,128)}, u32[]{:S(2)}) copy-start(f32[256,1536]{1,0:T(8,128)} %copy-done.2) | copy-start | bytes 4718596
  123.9 7.4 %copy-start.1 = (s32[1,1,4,256]{3,2,1,0:T(4,128)S(1)}, s32[1,1,4,256]{3,2,1,0:T(4,128)}, u32[]{:S(2)}) copy-start(s32[1,1,4,256]{3,2,1,0:T(4,128)} %param.3) | copy-start | bytes 12292

commit v14 on v11

--- a/solution.py
+++ b/solution.py
@@ -82,7 +82,7 @@
     vert_i2 = swap(own_i2, "grp")
     side_i1 = swap(own_i1, "box")
     diag_ie = swap(side_i1[:, width:], "grp")
-    inverse_own = newton(own_i1[:, :width] + side_i1[:, :width], ITERS_LOW)
+    inverse_own = newton(own_i1[:, :width] + side_i1[:, :width], ITERS_LOW, matmul_high)
     inverse_other = swap(inverse_own, "grp")
     part_a, side_i1 = lax.optimization_barrier((own_a, side_i1))
     side_a = swap(part_a, "box")

time: 132 us -> 132 us (level)
    dot_general x8 -> x4, matrix products: 9.94 us -> 8.29 us  [matmul(): jnp.dot(left, right, precision=lax.Precision.HIGHEST, preferred_element_t...]
    dot_general x10 -> x14, matrix products: 17.4 us -> 18.9 us  [matmul_high(): jnp.dot(left, right, precision=lax.Precision.HIGH, preferred_element_type...]
where the time goes in v14:
time: 132 us; the launch traced here: 131 us
  local copies, waits for them, and re-layouts  48.9 us (37%)
  waiting for transfers between devices  42 us (32%)
  matrix products  27.2 us (21%)
  starting transfers between devices  10.1 us (8%)
  other arithmetic  2.38 us (2%)
    ppermute x9, waiting for transfers between devices, swap(): return lax.ppermute(value, axis, pairs)  42 us
    gather x10, local copies, waits for them, and re-layouts, pick(): return jnp.take(picked, cols, axis=1, mode='clip')  20.7 us
    dot_general x14, matrix products, matmul_high(): jnp.dot(left, right, precision=lax.Precision.HIGH, preferred_element_type...  18.9 us
    gather x6, local copies, waits for them, and re-layouts, pick(): picked = jnp.take(matrix, rows, axis=0, mode='clip')  15.9 us
    ppermute x9, starting transfers between devices, swap(): return lax.ppermute(value, axis, pairs)  10.1 us
    dot_general x4, matrix products, matmul(): jnp.dot(left, right, precision=lax.Precision.HIGHEST, preferred_element_t...  8.29 us
    slice x3, local copies, waits for them, and re-layouts, first_rows(): rows[:, width:]  3.41 us
    slice x2, local copies, waits for them, and re-layouts, body(): solved_own = pair_solve(inverse_own, own_i1[:, width:], side_i1[:, width:])  3.29 us
  transfers between devices with their start and end apart: 9, of which 3 were waited for; matrix products, arithmetic and copies ran while one was open for 49% of the time, Pallas kernels for 0%

profile of v14, /device:TPU:0, one launch (start us, length us, event | category | flops | bytes accessed | tf_op | source)
XLA Modules:
  0.0 131.1 jit_solution(3776141551530698283)
XLA Ops:
  0.1 0.6 copy-done
  0.7 0.6 gather_fusion
  1.3 3.8 %gather_fusion.1 = f32[256,1024]{1,0:T(8,128)S(1)} fusion(f32[1024,1024]{1,0:T(8,128)} %bitcast.47, s32[1024]{0:T(1024)S(1)} %pad_clamp_fusion.3), kind=kCustom, calls=%fused_computation.1 | custom fusion | bytes 2098176 | tf_op jit(solution)/shard_map/jit(_take)/gather | solution.py:62
  5.1 0.3 copy.3
  5.4 3.5 %gather_fusion.2 = f32[1024,256]{1,0:T(8,128)S(1)} fusion(f32[256,1024]{0,1:T(8,128)S(1)} %copy.3, s32[1024]{0:T(1024)S(1)} %broadcast_clamp_fusion), kind=kCustom, calls=%fused_computation.2 | custom fusion | bytes 2101248 | tf_op jit(solution)/shard_map/jit(_take)/gather | solution.py:63
  8.9 1.3 %copy.4 = f32[1024,256]{0,1:T(8,128)} copy(f32[1024,256]{1,0:T(8,128)S(1)} %gather_fusion.2) | data formatting | bytes 2097152 | tf_op jit(solution)/shard_map/jit(_take)/gather | solution.py:63
  10.2 4.0 %collective-permute-start = (f32[256,1024]{1,0:T(8,128)}, f32[256,1024]{1,0:T(8,128)}, u32[]{:S(2)}, u32[]{:S(2)}) collective-permute-start(f32[256,1024]{1,0:T(8,128)} %bitcast.7), channel_id=1, source_target_pairs={{0,4},{1,5},{2,6},{3,7},{4,0},{5,1},{6,2},{7,3},{8,12},{9,13},{10,... | collective-permute-start | bytes 3145736 | tf_op jit(solution)/shard_map/ppermute | solution.py:32
  14.2 2.1 %slice.133 = f32[256,768]{1,0:T(8,128)} slice(f32[256,1024]{1,0:T(8,128)} %bitcast.7), slice={[0:256], [256:1024]} | slice | bytes 1572864 | tf_op jit(solution)/shard_map/slice | solution.py:93
  16.3 1.5 %collective-permute-start.5 = (f32[256,768]{1,0:T(8,128)}, f32[256,768]{1,0:T(8,128)}, u32[]{:S(2)}, u32[]{:S(2)}) collective-permute-start(f32[256,768]{1,0:T(8,128)} %slice.133), channel_id=1, source_target_pairs={{0,16},{8,24},{16,0},{24,8},{1,17},{9,25},{17,1},{25,9},{2,18},{10... | collective-permute-start | bytes 2359304 | tf_op jit(solution)/shard_map/ppermute | solution.py:32
  17.9 3.8 %gather_fusion.5 = f32[256,1024]{1,0:T(8,128)S(1)} fusion(f32[1024,1024]{1,0:T(8,128)} %bitcast.48, s32[1024]{0:T(1024)S(1)} %pad_clamp_fusion.1), kind=kCustom, calls=%fused_computation.5 | custom fusion | bytes 2098176 | tf_op jit(solution)/shard_map/jit(_take)/gather | solution.py:62
  21.6 0.3 copy.7
  22.0 3.5 %gather_fusion.7 = f32[1024,256]{1,0:T(8,128)S(1)} fusion(f32[256,1024]{0,1:T(8,128)S(1)} %copy.7, s32[1024]{0:T(1024)S(1)} %broadcast_clamp_fusion), kind=kCustom, calls=%fused_computation.7 | custom fusion | bytes 2101248 | tf_op jit(solution)/shard_map/jit(_take)/gather | solution.py:63
  25.4 0.3 copy.10
  25.8 0.6 collective-permute-start.3
  26.4 1.0 slice.195
  27.3 1.6 %gather_fusion.8 = f32[512,256]{1,0:T(8,128)S(1)} fusion(f32[256,1024]{0,1:T(8,128)S(1)} %copy.7, s32[1024]{0:T(1024)S(1)} %pad_clamp_fusion.2), kind=kCustom, calls=%fused_computation.8 | custom fusion | bytes 1050624 | tf_op jit(solution)/shard_map/jit(_take)/gather | solution.py:63
  28.9 5.8 %gather_fusion.3 = f32[512,1024]{1,0:T(8,128)} fusion(f32[1024,1024]{1,0:T(8,128)} %bitcast.49, s32[1024]{0:T(1024)S(1)} %pad_clamp_fusion.2), kind=kCustom, calls=%fused_computation.3 | custom fusion | bytes 4196352 | tf_op jit(solution)/shard_map/jit(_take)/gather | solution.py:62
  34.7 1.6 %gather_fusion.6 = f32[512,256]{1,0:T(8,128)S(1)} fusion(f32[256,1024]{0,1:T(8,128)S(1)} %copy.7, s32[1024]{0:T(1024)S(1)} %pad_clamp_fusion), kind=kCustom, calls=%fused_computation.6 | custom fusion | bytes 1050624 | tf_op jit(solution)/shard_map/jit(_take)/gather | solution.py:63
  36.3 1.0 copy.8
  37.3 1.0 copy.12
  38.3 1.9 %copy.5 = f32[512,1024]{0,1:T(8,128)S(1)} copy(f32[512,1024]{1,0:T(8,128)} %gather_fusion.3) | data formatting | bytes 4194304 | tf_op jit(solution)/shard_map/jit(_take)/gather | solution.py:62
  40.2 4.9 %gather_fusion.4 = f32[1024,512]{1,0:T(8,128)} fusion(f32[512,1024]{0,1:T(8,128)S(1)} %copy.5, s32[1024]{0:T(1024)S(1)} %broadcast_clamp_fusion), kind=kCustom, calls=%fused_computation.4 | custom fusion | bytes 4198400 | tf_op jit(solution)/shard_map/jit(_take)/gather | solution.py:63
  45.1 2.1 %copy.6 = f32[1024,512]{0,1:T(8,128)S(1)} copy(f32[1024,512]{1,0:T(8,128)} %gather_fusion.4) | data formatting | bytes 4194304 | tf_op jit(solution)/shard_map/jit(_take)/gather | solution.py:63
  47.2 1.3 slice.187
  48.5 11.7 %collective-permute-done = f32[256,1024]{1,0:T(8,128)} collective-permute-done((f32[256,1024]{1,0:T(8,128)}, f32[256,1024]{1,0:T(8,128)}, u32[]{:S(2)}, u32[]{:S(2)}) %collective-permute-start) | collective-permute-done | bytes 1048608 | tf_op jit(solution)/shard_map/ppermute | solution.py:32
  60.2 1.1 select_reduce_fusion.1
  61.3 0.3 fusion.34
  61.7 0.4 convolution_subtract_fusion.4
  62.1 0.3 fusion.63
  62.3 0.3 convolution_subtract_fusion.3
  62.6 1.6 %collective-permute-start.4 = (f32[256,256]{1,0:T(8,128)S(1)}, f32[256,256]{1,0:T(8,128)S(1)}, u32[]{:S(2)}, u32[]{:S(2)}) collective-permute-start(f32[256,256]{1,0:T(8,128)S(1)} %convolution_subtract_fusion.3), channel_id=1, source_target_pairs={{0,16},{8,24},{16,0},{24,8},{1,17},{9,25},{17,1},{25,9},{2,18},{10... | collective-permute-start | bytes 786440 | tf_op jit(solution)/shard_map/ppermute | solution.py:32
  64.3 1.2 slice.137
  65.5 2.7 %convolution_negate_fusion.1 = f32[256,1536]{1,0:T(8,128)S(1)} fusion(f32[256,256]{1,0:T(8,128)S(1)} %convolution_subtract_fusion.3, f32[256,768]{1,0:T(8,128)S(1)} %slice.137, f32[256,768]{1,0:T(8,128)} %slice.133), kind=kOutput, calls=%fused_computation.13 | convolution fusion | flops 1208745984 | bytes 3407872 | tf_op jit(solution)/shard_map/dot_general | solution.py:11
  68.1 1.2 slice.203
  69.3 0.5 collective-permute-start.6
  69.8 1.5 %convolution_add_fusion.1 = f32[256,1536]{1,0:T(8,128)S(1)} fusion(f32[256,1536]{1,0:T(8,128)S(1)} %convolution_negate_fusion.1, f32[256,768]{1,0:T(8,128)S(1)} %copy-done.5, f32[256,1024]{1,0:T(8,128)S(1)} %bitcast.54), kind=kOutput, calls=%fused_computation.11 | convolution fusion | flops 1208352768 | bytes 4194304 | tf_op jit(solution)/shard_map/dot_general | solution.py:11
  71.3 2.7 %convolution_add_fusion = f32[512,1536]{1,0:T(8,128)S(1)} fusion(f32[256,1536]{1,0:T(8,128)S(1)} %convolution_negate_fusion.1, f32[512,768]{1,0:T(8,128)S(1)} %copy-done.4, f32[512,1024]{1,0:T(8,128)S(1)} %bitcast.51), kind=kOutput, calls=%fused_computation.9 | convolution fusion | flops 2416705536 | bytes 6815744 | tf_op jit(solution)/shard_map/dot_general | solution.py:11
  74.1 0.2 fusion.57
  74.3 0.5 broadcast.40.clone
  74.8 0.1 slice_dynamic-update-slice_fusion.1
  75.0 1.2 slice.201
  76.2 12.7 %collective-permute-done.1 = f32[256,512]{1,0:T(8,128)S(1)} collective-permute-done((f32[256,512]{1,0:T(8,128)S(1)}, f32[256,512]{1,0:T(8,128)S(1)}, u32[]{:S(2)}, u32[]{:S(2)}) %collective-permute-start.1) | collective-permute-done | bytes 524320 | tf_op jit(solution)/shard_map/ppermute | solution.py:32
  88.9 1.4 %fusion.32 = f32[256,1536]{1,0:T(8,128)S(1)} fusion(f32[256,1536]{1,0:T(8,128)S(1)} %convolution_negate_fusion.1, f32[256,512]{1,0:T(8,128)S(1)} %collective-permute-done.1), kind=kOutput, calls=%fused_computation.66 | convolution fusion | flops 1207959552 | bytes 3407872 | tf_op jit(solution)/shard_map/dot_general | solution.py:11
  90.5 0.8 collective-permute-start.7
  91.3 0.1 maximum_maximum_fusion
  91.4 2.0 %convolution_negate_fusion = f32[256,1536]{1,0:T(8,128)S(1)} fusion(f32[256,256]{1,0:T(8,128)S(1)} %collective-permute-done.4, f32[256,768]{1,0:T(8,128)S(1)} %collective-permute-done.6, f32[256,768]{1,0:T(8,128)} %collective-permute-done.5), kind=kOutput, calls=%fused_computation.12 | convolution fusion | flops 604766208 | bytes 3407872 | tf_op jit(solution)/shard_map/dot_general | solution.py:15
  93.4 1.8 %pad_add_fusion = f32[256,1536]{1,0:T(8,128)S(1)} fusion(f32[256,768]{1,0:T(8,128)S(1)} %slice.201, f32[256,1536]{1,0:T(8,128)S(1)} %convolution_negate_fusion, f32[256,1024]{1,0:T(8,128)} %collective-permute-done.3), kind=kOutput, calls=%fused_computation.20 | convolution fusion | flops 604372992 | bytes 4194304 | tf_op jit(solution)/shard_map/dot_general | solution.py:15
  95.4 17.6 %collective-permute-done.2 = f32[256,512]{1,0:T(8,128)S(1)} collective-permute-done((f32[256,512]{1,0:T(8,128)S(1)}, f32[256,512]{1,0:T(8,128)S(1)}, u32[]{:S(2)}, u32[]{:S(2)}) %collective-permute-start.2) | collective-permute-done | bytes 524320 | tf_op jit(solution)/shard_map/ppermute | solution.py:32
  113.0 1.0 collective-permute-start.8
  114.0 0.1 slice_add_fusion.1
  114.1 1.1 fusion.25
  115.3 0.2 select_reduce_fusion
  115.5 0.9 copy-done.2
  116.4 1.1 fusion.15
  117.5 1.3 convolution_subtract_fusion.2
  118.7 1.0 fusion.64
  119.7 1.0 convolution_subtract_fusion.1
  120.8 1.1 fusion.8
  121.8 0.5 broadcast.40.clone.1
  122.3 0.1 maximum_dynamic-update-slice_fusion
  122.5 0.8 slice-done
  123.4 0.3 slice_dynamic-update-slice_fusion
  123.7 5.3 %convolution_subtract_fusion = f32[512,2048]{1,0:T(8,128)} fusion(f32[512,2048]{1,0:T(8,128)S(1)} %get-tuple-element.47, f32[512,512]{1,0:T(8,128)S(1)} %fusion.8, f32[512,2048]{1,0:T(8,128)S(1)} %get-tuple-element.48), kind=kOutput, calls=%fused_computation.10 | convolution fusion | flops 3222274048 | bytes 13631488 | tf_op jit(solution)/shard_map/dot_general | solution.py:15
  129.0 2.0 %fusion.7 = f32[1,1,512,2048]{3,2,1,0:T(8,128)} fusion(f32[1,1,512,2048]{3,2,1,0:T(8,128)} %bitcast.55, s32[]{:T(128)S(6)} %select_n.37, f32[512,512]{1,0:T(8,128)S(1)} %fusion.8, f32[256,512]{1,0:T(8,128)S(1)} %slice_add_fusion, f32[256,512]{1,0:T(8,128)S(1)} %get-tuple-element.31), kind=kOutput, calls=%fused_computation.23 | convolution fusion | flops 805830656 | bytes 3145732 | tf_op jit(solution)/shard_map/dot_general | solution.py:15
  (45 shorter events, 0.7 us)
Async XLA Ops:
  0.0 0.7 copy-start
  10.2 50.0 %collective-permute-start = (f32[256,1024]{1,0:T(8,128)}, f32[256,1024]{1,0:T(8,128)}, u32[]{:S(2)}, u32[]{:S(2)}) collective-permute-start(f32[256,1024]{1,0:T(8,128)} %bitcast.7), channel_id=1, source_target_pairs={{0,4},{1,5},{2,6},{3,7},{4,0},{5,1},{6,2},{7,3},{8,12},{9,13},{10,... | collective-permute-start | bytes 3145736 | tf_op jit(solution)/shard_map/ppermute | solution.py:32
  16.3 75.1 %collective-permute-start.5 = (f32[256,768]{1,0:T(8,128)}, f32[256,768]{1,0:T(8,128)}, u32[]{:S(2)}, u32[]{:S(2)}) collective-permute-start(f32[256,768]{1,0:T(8,128)} %slice.133), channel_id=1, source_target_pairs={{0,16},{8,24},{16,0},{24,8},{1,17},{9,25},{17,1},{25,9},{2,18},{10... | collective-permute-start | bytes 2359304 | tf_op jit(solution)/shard_map/ppermute | solution.py:32
  25.8 49.2 %collective-permute-start.3 = (f32[256,1024]{1,0:T(8,128)S(1)}, f32[256,1024]{1,0:T(8,128)}, u32[]{:S(2)}, u32[]{:S(2)}) collective-permute-start(f32[256,1024]{1,0:T(8,128)S(1)} %bitcast.52), channel_id=1, source_target_pairs={{0,16},{8,24},{16,0},{24,8},{1,17},{9,25},{17,1},{25,9},{2,18},{10... | collective-permute-start | bytes 3145736 | tf_op jit(solution)/shard_map/ppermute | solution.py:32
  48.5 15.8 %copy-start.7 = (f32[512,256]{0,1:T(8,128)S(1)}, f32[512,256]{0,1:T(8,128)}, u32[]{:S(2)}) copy-start(f32[512,256]{0,1:T(8,128)} %copy.8) | copy-start | bytes 1572868
  62.6 28.8 %collective-permute-start.4 = (f32[256,256]{1,0:T(8,128)S(1)}, f32[256,256]{1,0:T(8,128)S(1)}, u32[]{:S(2)}, u32[]{:S(2)}) collective-permute-start(f32[256,256]{1,0:T(8,128)S(1)} %convolution_subtract_fusion.3), channel_id=1, source_target_pairs={{0,16},{8,24},{16,0},{24,8},{1,17},{9,25},{17,1},{25,9},{2,18},{10... | collective-permute-start | bytes 786440 | tf_op jit(solution)/shard_map/ppermute | solution.py:32
  64.3 24.7 %collective-permute-start.1 = (f32[256,512]{1,0:T(8,128)S(1)}, f32[256,512]{1,0:T(8,128)S(1)}, u32[]{:S(2)}, u32[]{:S(2)}) collective-permute-start(f32[256,512]{1,0:T(8,128)S(1)} %bitcast.57), channel_id=1, source_target_pairs={{0,4},{1,5},{2,6},{3,7},{4,0},{5,1},{6,2},{7,3},{8,12},{9,13},{10,... | collective-permute-start | bytes 1572872 | tf_op jit(solution)/shard_map/ppermute | solution.py:32
  65.4 4.4 %copy-start.5 = (f32[256,768]{1,0:T(8,128)S(1)}, f32[256,768]{1,0:T(8,128)}, u32[]{:S(2)}) copy-start(f32[256,768]{1,0:T(8,128)} %slice.195) | copy-start | bytes 2359300
  69.3 2.0 %copy-start.4 = (f32[512,768]{1,0:T(8,128)S(1)}, f32[512,768]{1,0:T(8,128)}, u32[]{:S(2)}) copy-start(f32[512,768]{1,0:T(8,128)} %slice.187) | copy-start | bytes 4718596
  69.3 22.1 %collective-permute-start.6 = (f32[256,768]{1,0:T(8,128)S(1)}, f32[256,768]{1,0:T(8,128)S(1)}, u32[]{:S(2)}, u32[]{:S(2)}) collective-permute-start(f32[256,768]{1,0:T(8,128)S(1)} %slice.203), channel_id=1, source_target_pairs={{0,16},{8,24},{16,0},{24,8},{1,17},{9,25},{17,1},{25,9},{2,18},{10... | collective-permute-start | bytes 2359304 | tf_op jit(solution)/shard_map/ppermute | solution.py:32
  74.8 14.1 %copy-start.6 = (f32[512,256]{0,1:T(8,128)S(1)}, f32[512,256]{0,1:T(8,128)}, u32[]{:S(2)}) copy-start(f32[512,256]{0,1:T(8,128)} %copy.12) | copy-start | bytes 1572868
  88.9 24.0 %collective-permute-start.2 = (f32[256,512]{1,0:T(8,128)S(1)}, f32[256,512]{1,0:T(8,128)S(1)}, u32[]{:S(2)}, u32[]{:S(2)}) collective-permute-start(f32[256,512]{1,0:T(8,128)S(1)} %bitcast.56), channel_id=1, source_target_pairs={{0,4},{1,5},{2,6},{3,7},{4,0},{5,1},{6,2},{7,3},{8,12},{9,13},{10,... | collective-permute-start | bytes 1572872 | tf_op jit(solution)/shard_map/ppermute | solution.py:32
  90.5 23.6 %collective-permute-start.7 = (f32[256,512]{1,0:T(8,128)S(1)}, f32[256,512]{1,0:T(8,128)S(1)}, u32[]{:S(2)}, u32[]{:S(2)}) collective-permute-start(f32[256,512]{1,0:T(8,128)S(1)} %collective-permute-done.1), channel_id=1, source_target_pairs={{0,16},{8,24},{16,0},{24,8},{1,17},{9,25},{17,1},{25,9},{2,18},{10... | collective-permute-start | bytes 1572872 | tf_op jit(solution)/shard_map/ppermute | solution.py:32
  113.0 16.0 %collective-permute-start.8 = (f32[256,512]{1,0:T(8,128)S(1)}, f32[256,512]{1,0:T(8,128)S(1)}, u32[]{:S(2)}, u32[]{:S(2)}) collective-permute-start(f32[256,512]{1,0:T(8,128)S(1)} %collective-permute-done.2), channel_id=1, source_target_pairs={{0,16},{8,24},{16,0},{24,8},{1,17},{9,25},{17,1},{25,9},{2,18},{10... | collective-permute-start | bytes 1572872 | tf_op jit(solution)/shard_map/ppermute | solution.py:32
  115.2 1.2 copy-start.2
  122.3 1.0 slice-start
  123.7 5.3 %copy-start.3 = (f32[256,1536]{1,0:T(8,128)S(1)}, f32[256,1536]{1,0:T(8,128)}, u32[]{:S(2)}) copy-start(f32[256,1536]{1,0:T(8,128)} %copy-done.2) | copy-start | bytes 4718596
  123.7 7.4 %copy-start.1 = (s32[1,1,4,256]{3,2,1,0:T(4,128)S(1)}, s32[1,1,4,256]{3,2,1,0:T(4,128)}, u32[]{:S(2)}) copy-start(s32[1,1,4,256]{3,2,1,0:T(4,128)} %param.3) | copy-start | bytes 12292
